TPU v7x, 512 devices: a whole 4x8x8 slice. The times are simulated.
512 devices in a mesh: seg: 16 (over z, x_lo), tok: 32 (over x_hi, y, core).
Axes of the slice: x: 4 (x_hi: 2, x_lo: 2; x = x_hi * 2 + x_lo), y: 8, z: 8, core: 2. Of those that a mesh axis runs over, the one named last changes fastest.
Arguments:
- seg_queries: bfloat16 [16, 4096, 2048], P('seg', 'tok'), may hold values from -8 to 8
- seg_keys: bfloat16 [16, 4096, 512], P('seg', 'tok'), may hold values from -8 to 8
- seg_values: bfloat16 [16, 4096, 512], P('seg', 'tok'), may hold values from -8 to 8
- grad_out: bfloat16 [16, 4096, 2048], P('seg', 'tok'), may hold values from -6 to 6
- mem_init: float32 [256, 1024], P('tok'), may hold values from -6 to 6
- mem_query: bfloat16 [256, 512], P('tok'), may hold values from -8 to 8
- retention: float32 [16, 1024], P('seg'), may hold values from 0 to 1
- seg_len: int32 [16], replicated, may hold values from 1024 to 4096, as said below
- doc_start: int32 [16], replicated, may hold values from 0 to 1, as said below
Outputs:
- attended: bfloat16 [16, 4096, 2048], P('seg', 'tok')
- memory_in: float32 [16, 256, 1024], P('seg', 'tok')
- memory_grad: float32 [16, 256, 1024], P('seg', 'tok')
Inputs may be any that keep to these rules, and one draw needn't show every extreme that they name: `seg_len`: A segment is full unless it is the last one of its document; segment 0 is always full and the last segment is the last one of its document. `doc_start`: segment 0 begins a document and segment 1 never does; any later segment may.
All inputs are finite; a program needn't handle non-finite values.
Results may differ from a plain program's by a relative error of at most 0.009.
Values may be sent and summed in bfloat16 or wider, within the bound.
No kernel may reach another device: no remote copies, remote signals or barrier semaphores. Data moves between devices by JAX's collectives and lax.ppermute only.
A program may use at most 64 MiB of HBM per device.

v0:
```python
import math

import jax
import jax.numpy as jnp
from jax import lax
from jax.sharding import PartitionSpec as P

HD = 128
QH = 16
KVH = 4


loss_scale = 16.0
neg_fill = -1e30
norm_eps = 1e-06


def gathered(block, axis, groups):
    size = lax.axis_size(axis)
    index = lax.axis_index(axis)
    held = block[None]
    axis_bits = []
    for group in groups:
        group = sorted(group)
        mine = sum(((index >> bit) & 1) << k for k, bit in enumerate(group))
        arrived = [held]
        for mask in range(1, 1 << len(group)):
            flip = sum(((mask >> k) & 1) << bit for k, bit in enumerate(group))
            arrived.append(lax.ppermute(held, axis, [(i, i ^ flip) for i in range(size)]))
        placed = []
        for place in range(1 << len(group)):
            value = arrived[0]
            for mask in range(1, 1 << len(group)):
                value = jnp.where((mine ^ mask) == place, arrived[mask], value)
            placed.append(value)
        held = jnp.stack(placed).reshape((2,) * len(group) + held.shape)
        axis_bits = group[::-1] + axis_bits
    order = sorted(range(len(axis_bits)), key=lambda k: -axis_bits[k])
    held = jnp.transpose(held, order + list(range(len(axis_bits), held.ndim)))
    return held.reshape((size,) + block.shape)


def scattered_sum(rows, axis, groups):
    size = lax.axis_size(axis)
    index = lax.axis_index(axis)
    held = rows.reshape((size, rows.shape[0] // size) + rows.shape[1:])
    low = 0
    for width in groups:
        ways = 1 << width
        held = held.reshape((held.shape[0] // ways, ways) + held.shape[1:])
        mine = (index >> low) & (ways - 1)
        total = lax.dynamic_index_in_dim(held, mine, axis=1, keepdims=False)
        for mask in range(1, ways):
            send = lax.dynamic_index_in_dim(held, mine ^ mask, axis=1, keepdims=False)
            flip = mask << low
            total = total + lax.ppermute(send, axis, [(i, i ^ flip) for i in range(size)])
        held = total
        low += width
    return held[0]


def slot_norm(raw_rows):
    parts = raw_rows.reshape(raw_rows.shape[0], 2 * KVH, HD)
    multiplier = lax.rsqrt(jnp.mean(parts * parts, axis=-1, keepdims=True) + norm_eps)
    return (parts * multiplier).reshape(raw_rows.shape)


def softmax_step(row_top, row_total, scores, allowed):
    scores = jnp.where(allowed, scores, neg_fill)
    new_top = jnp.maximum(row_top, jnp.max(scores, axis=-1))
    weights = jnp.where(allowed, jnp.exp(scores - new_top[..., None]), 0.0)
    multiplier = jnp.exp(row_top - new_top)
    new_total = row_total * multiplier + jnp.sum(weights, axis=-1)
    return (new_top, new_total, weights.astype(jnp.bfloat16), multiplier)


def shards(
    seg_queries, seg_keys, seg_values, grad_out, mem_init, mem_query, retention, seg_len, doc_start
):
    tok_rows = seg_queries.shape[1]
    mem_rows = mem_query.shape[0]
    group_size = QH // KVH
    width_kv = KVH * HD
    seg_count = lax.axis_size("seg")
    seg_index = lax.axis_index("seg")
    tok_index = lax.axis_index("tok")
    length = seg_len[seg_index]
    score_scale = 1.0 / math.sqrt(HD)
    queries = seg_queries[0].reshape(tok_rows, KVH, group_size, HD)
    slot_queries = mem_query.reshape(mem_rows, KVH, HD)
    row_pos = tok_index * tok_rows + jnp.arange(tok_rows)

    kv_piece = lax.all_gather(
        jnp.concatenate([seg_keys[0], seg_values[0]], axis=1), "tok", axis=0, tiled=True
    )
    piece_rows = kv_piece.shape[0]
    key_piece = kv_piece[:, :width_kv].reshape(piece_rows, KVH, HD)
    value_piece = kv_piece[:, width_kv:].reshape(piece_rows, KVH, HD)

    live_keys = jnp.arange(piece_rows) < length
    slot_scores = (
        jnp.einsum("rgd,ugd->gru", slot_queries, key_piece, preferred_element_type=jnp.float32)
        * score_scale
    )
    slot_scores = jnp.where(live_keys, slot_scores, neg_fill)
    slot_top = jnp.max(slot_scores, axis=-1, keepdims=True)
    slot_exp = jnp.where(live_keys, jnp.exp(slot_scores - slot_top), 0.0)
    slot_denom = jnp.transpose(jnp.sum(slot_exp, axis=-1))[..., None]
    slot_weights = slot_exp.astype(jnp.bfloat16)
    slot_keys = jnp.einsum(
        "gru,ugd->rgd", slot_weights, key_piece, preferred_element_type=jnp.float32
    )
    slot_values = jnp.einsum(
        "gru,ugd->rgd", slot_weights, value_piece, preferred_element_type=jnp.float32
    )
    raw_slots = jnp.concatenate(
        [
            (slot_keys / slot_denom).reshape(mem_rows, width_kv),
            (slot_values / slot_denom).reshape(mem_rows, width_kv),
        ],
        axis=1,
    )
    written = slot_norm(raw_slots)
    ret_row = retention[0]
    following = doc_start[jnp.minimum(seg_index + 1, seg_count - 1)].astype(jnp.float32)
    keep_flag = jnp.where(seg_index == seg_count - 1, 1.0, 1.0 - following)
    decay_rate = keep_flag * ret_row
    carried = keep_flag * (1.0 - ret_row) * written + (1.0 - keep_flag) * mem_init

    chain_terms = gathered(
        jnp.concatenate([carried, decay_rate[None]], axis=0), "seg", ((2, 3), (0, 1))
    )
    all_carried = chain_terms[:, :mem_rows]
    all_decay = chain_terms[:, mem_rows]
    memory_in = mem_init
    for step in range(seg_count - 1):
        following_memory = all_decay[step] * memory_in + all_carried[step]
        memory_in = jnp.where(step < seg_index, following_memory, memory_in)

    block_rows = math.gcd(piece_rows, 1024)
    blocks = piece_rows // block_rows
    running = (
        jnp.full((KVH, group_size, tok_rows), neg_fill, jnp.float32),
        jnp.zeros((KVH, group_size, tok_rows), jnp.float32),
        jnp.zeros((tok_rows, KVH, group_size, HD), jnp.float32),
    )
    for block in range(blocks):
        block_start = block * block_rows
        key_block = key_piece[block_start : block_start + block_rows]
        value_block = value_piece[block_start : block_start + block_rows]
        columns = block_start + jnp.arange(block_rows)
        causal = (columns[None, :] <= row_pos[:, None]) & (columns < length)[None, :]
        seg_scores = (
            jnp.einsum("tgjd,ugd->gjtu", queries, key_block, preferred_element_type=jnp.float32)
            * score_scale
        )
        seg_top, seg_total, seg_weights, seg_factor = softmax_step(
            running[0], running[1], seg_scores, causal
        )
        seg_acc = running[2] * jnp.transpose(seg_factor, (2, 0, 1))[..., None] + jnp.einsum(
            "gjtu,ugd->tgjd", seg_weights, value_block, preferred_element_type=jnp.float32
        )
        running = (seg_top, seg_total, seg_acc)

    memory_all = gathered(memory_in.astype(jnp.bfloat16), "tok", ((3, 4), (1, 2), (0,))).reshape(
        -1, 2 * width_kv
    )
    mem_keys = memory_all[:, :width_kv].reshape(-1, KVH, HD)
    mem_vals = memory_all[:, width_kv:].reshape(-1, KVH, HD)
    mem_scores = (
        jnp.einsum("tgjd,mgd->gjtm", queries, mem_keys, preferred_element_type=jnp.float32)
        * score_scale
    )
    row_top = jnp.maximum(running[0], jnp.max(mem_scores, axis=-1))
    seg_factor = jnp.exp(running[0] - row_top)
    mem_weights = jnp.exp(mem_scores - row_top[..., None])
    row_total = running[1] * seg_factor + jnp.sum(mem_weights, axis=-1)
    weighted = running[2] * jnp.transpose(seg_factor, (2, 0, 1))[..., None] + jnp.einsum(
        "gjtm,mgd->tgjd",
        mem_weights.astype(jnp.bfloat16),
        mem_vals,
        preferred_element_type=jnp.float32,
    )
    att_rows = weighted / jnp.transpose(row_total, (2, 0, 1))[..., None]
    log_total = row_top + jnp.log(row_total)
    attended = att_rows.reshape(1, tok_rows, QH * HD).astype(jnp.bfloat16)
    valid_rows = (row_pos < length).astype(jnp.bfloat16)[:, None]
    cotangent = (grad_out[0] * valid_rows * loss_scale).reshape(tok_rows, KVH, group_size, HD)
    row_delta = jnp.einsum("tgjd,tgjd->gjt", cotangent.astype(jnp.float32), att_rows)
    mem_prob = jnp.exp(mem_scores - log_total[..., None])
    grad_prob = jnp.einsum(
        "tgjd,mgd->gjtm", cotangent, mem_vals, preferred_element_type=jnp.float32
    )
    grad_score = mem_prob * (grad_prob - row_delta[..., None])
    grad_vals = jnp.einsum(
        "gjtm,tgjd->mgd",
        mem_prob.astype(jnp.bfloat16),
        cotangent,
        preferred_element_type=jnp.float32,
    )
    grad_keys = (
        jnp.einsum(
            "gjtm,tgjd->mgd",
            grad_score.astype(jnp.bfloat16),
            queries,
            preferred_element_type=jnp.float32,
        )
        * score_scale
    )
    grad_slots = jnp.concatenate(
        [grad_keys.reshape(-1, width_kv), grad_vals.reshape(-1, width_kv)], axis=1
    )
    local_grad = scattered_sum(grad_slots, "tok", (1, 2, 2))

    all_local = gathered(local_grad, "seg", ((2, 3), (0, 1)))
    memory_grad = all_local[seg_count - 1]
    for step in range(seg_count - 2, -1, -1):
        earlier_grad = all_local[step] + all_decay[step] * memory_grad
        memory_grad = jnp.where(step >= seg_index, earlier_grad, memory_grad)
    return (attended, memory_in[None], memory_grad[None])


def solution(mesh):
    placed = (
        P("seg", "tok", None),
        P("seg", "tok", None),
        P("seg", "tok", None),
        P("seg", "tok", None),
        P("tok", None),
        P("tok", None),
        P("seg", None),
        P(),
        P(),
    )
    return jax.shard_map(
        shards,
        mesh=mesh,
        in_specs=placed,
        out_specs=(P("seg", "tok", None), P("seg", "tok", None), P("seg", "tok", None)),
        check_vma=False,
    )
```

profile of v0, /device:TPU:2, one launch (start us, length us, event | category | flops | bytes accessed | tf_op | source)
XLA Modules:
  0.0 347.7 jit_solution(11766808417356156304)
XLA Ops:
  10.2 1.2 dynamic_slice.32
  12.1 1.4 reshape_squeeze.3
  13.5 1.3 copy.152
  14.8 1.2 dynamic_slice.31
  16.1 1.2 compare_convert_fusion
  20.0 2.2 compare_and_fusion.1
  22.1 106.7 %all-gather.2.cloned.1.call-done = bf16[4096,1024]{0,1:T(8,128)(2,1)} async-done(((bf16[128,1024]{0,1:T(8,128)(2,1)}), bf16[4096,1024]{0,1:T(8,128)(2,1)}) %all-gather.2.cloned.1.call-update) | async-done | bytes 8388624 | tf_op jit(solution)/shard_map/all_gather | solution.py:93
  128.8 6.1 %fusion.185 = (bf16[4096,512]{0,1:T(8,128)(2,1)}, bf16[4096,512]{0,1:T(8,128)(2,1)}) fusion(bf16[4096,1024]{0,1:T(8,128)(2,1)} %all-gather.2.cloned.1.call-done), kind=kLoop, calls=%fused_computation.282 | loop fusion | bytes 16777216 | tf_op jit(solution)/shard_map/slice | solution.py:97
  134.9 3.1 fusion.188
  138.0 3.5 %fusion.80 = f32[8,4,128]{2,0,1:T(8,128)S(1)} fusion(bf16[4096,4,128]{0,2,1:T(8,128)(2,1)} %bitcast.616, bf16[4,8,4096]{2,1,0:T(8,128)(2,1)S(1)} %get-tuple-element.90, f32[8,4]{0,1:T(4,128)S(1)} %bitcast.687), kind=kOutput, calls=%fused_computation.70 | convolution fusion | flops 33558528 | bytes 4472960 | tf_op jit(solution)/shard_map/gru,ugd->rgd/dot_general | solution.py:110
  141.6 3.5 %fusion.79 = f32[8,4,128]{2,0,1:T(8,128)S(1)} fusion(bf16[4096,4,128]{0,2,1:T(8,128)(2,1)} %bitcast.614, bf16[4,8,4096]{2,1,0:T(8,128)(2,1)S(1)} %get-tuple-element.90, f32[8,4]{0,1:T(4,128)S(1)} %bitcast.688), kind=kOutput, calls=%fused_computation.68 | convolution fusion | flops 33558528 | bytes 4472960 | tf_op jit(solution)/shard_map/gru,ugd->rgd/dot_general | solution.py:113
  145.3 6.6 %collective-permute-start = (f32[1,9,1024]{2,1,0:T(8,128)S(1)}, f32[1,9,1024]{2,1,0:T(8,128)S(1)}, u32[]{:S(2)}, u32[]{:S(2)}) collective-permute-start(f32[1,9,1024]{2,1,0:T(8,128)S(1)} %maximum_bitcast_fusion.1), channel_id=1, source_target_pairs={{0,384},{32,416},{64,448},{96,480},{128,256},{160,288},{192,320},{... | collective-permute-start | bytes 110600 | tf_op jit(solution)/shard_map/ppermute | solution.py:29
  151.9 3.5 %collective-permute-start.1 = (f32[1,9,1024]{2,1,0:T(8,128)S(1)}, f32[1,9,1024]{2,1,0:T(8,128)S(1)}, u32[]{:S(2)}, u32[]{:S(2)}) collective-permute-start(f32[1,9,1024]{2,1,0:T(8,128)S(1)} %maximum_bitcast_fusion.1), channel_id=1, source_target_pairs={{0,256},{32,288},{64,320},{96,352},{128,384},{160,416},{192,448},{... | collective-permute-start | bytes 110600 | tf_op jit(solution)/shard_map/ppermute | solution.py:29
  155.4 2.7 collective-permute-start.2
  158.1 2.4 fusion.184
  160.5 2.4 collective-permute-done.1
  162.9 1.8 collective-permute-done.2
  164.7 2.3 collective-permute-start.3
  167.0 4.4 %collective-permute-start.4 = (f32[2,2,1,9,1024]{4,3,1,0,2:T(8,128)S(1)}, f32[2,2,1,9,1024]{4,3,1,0,2:T(8,128)S(1)}, u32[]{:S(2)}, u32[]{:S(2)}) collective-permute-start(f32[2,2,1,9,1024]{4,3,1,0,2:T(8,128)S(1)} %bitcast.636), channel_id=1, source_target_pairs={{0,64},{32,96},{64,0},{96,32},{128,192},{160,224},{192,128},{224,1... | collective-permute-start | bytes 442376 | tf_op jit(solution)/shard_map/ppermute | solution.py:29
  171.5 2.5 collective-permute-start.5
  174.0 4.9 %fusion.4 = (f32[4,4,128]{2,1,0:T(4,128)S(1)}, f32[4,1024,128,4]{2,1,3,0:T(8,128)}) fusion(pred[128,1024]{0,1:T(8,128)(4,1)S(1)} %get-tuple-element.86, bf16[1024,4,128,1]{0,2,3,1:T(8,128)(2,1)S(1)} %bitcast.620, bf16[128,4,4,128]{3,2,1,0:T(4,128)(2,1)S(1)} %reshape_squeeze.3), kind=kOutput, calls=%fused_computation.12 | convolution fusion | flops 543160320 | bytes 10100736 | tf_op jit(solution)/shard_map/tgjd,ugd->gjtu/dot_general | solution.py:154
  178.8 2.3 collective-permute-done.4
  182.9 4.9 %collective-permute-start.6 = (bf16[1,8,1024]{2,1,0:T(8,128)(2,1)S(1)}, bf16[1,8,1024]{2,1,0:T(8,128)(2,1)S(1)}, u32[]{:S(2)}, u32[]{:S(2)}) collective-permute-start(bf16[1,8,1024]{2,1,0:T(8,128)(2,1)S(1)} %get-tuple-element.20), channel_id=1, source_target_pairs={{0,24},{1,25},{2,26},{3,27},{4,28},{5,29},{6,30},{7,31},{8,16},{9,... | collective-permute-start | bytes 49160 | tf_op jit(solution)/shard_map/ppermute | solution.py:29
  187.9 4.4 %collective-permute-start.7 = (bf16[1,8,1024]{2,1,0:T(8,128)(2,1)S(1)}, bf16[1,8,1024]{2,1,0:T(8,128)(2,1)S(1)}, u32[]{:S(2)}, u32[]{:S(2)}) collective-permute-start(bf16[1,8,1024]{2,1,0:T(8,128)(2,1)S(1)} %get-tuple-element.20), channel_id=1, source_target_pairs={{0,16},{1,17},{2,18},{3,19},{4,20},{5,21},{6,22},{7,23},{8,24},{9,... | collective-permute-start | bytes 49160 | tf_op jit(solution)/shard_map/ppermute | solution.py:29
  192.3 5.3 %collective-permute-start.8 = (bf16[1,8,1024]{2,1,0:T(8,128)(2,1)S(1)}, bf16[1,8,1024]{2,1,0:T(8,128)(2,1)S(1)}, u32[]{:S(2)}, u32[]{:S(2)}) collective-permute-start(bf16[1,8,1024]{2,1,0:T(8,128)(2,1)S(1)} %get-tuple-element.20), channel_id=1, source_target_pairs={{0,8},{1,9},{2,10},{3,11},{4,12},{5,13},{6,14},{7,15},{8,0},{9,1},... | collective-permute-start | bytes 49160 | tf_op jit(solution)/shard_map/ppermute | solution.py:29
  197.7 5.5 %fusion.3 = (f32[4,4,128]{2,1,0:T(4,128)}, f32[4,1024,128,4]{2,1,3,0:T(8,128)}) fusion(pred[128,1024]{0,1:T(8,128)(4,1)S(1)} %get-tuple-element.85, bf16[1024,4,128,1]{0,2,3,1:T(8,128)(2,1)S(1)} %bitcast.619, bf16[128,4,4,128]{3,2,1,0:T(4,128)(2,1)S(1)} %reshape_squeeze.3), kind=kOutput, calls=%fused_computation.11 | convolution fusion | flops 543160320 | bytes 10100736 | tf_op jit(solution)/shard_map/tgjd,ugd->gjtu/dot_general | solution.py:154
  203.2 4.0 %collective-permute-start.9 = (bf16[2,2,1,8,1024]{4,3,1,0,2:T(8,128)(2,1)S(1)}, bf16[2,2,1,8,1024]{4,3,1,0,2:T(8,128)(2,1)S(1)}, u32[]{:S(2)}, u32[]{:S(2)}) collective-permute-start(bf16[2,2,1,8,1024]{4,3,1,0,2:T(8,128)(2,1)S(1)} %bitcast.651), channel_id=1, source_target_pairs={{0,6},{1,7},{2,4},{3,5},{4,2},{5,3},{6,0},{7,1},{8,14},{9,15},{10,... | collective-permute-start | bytes 196616 | tf_op jit(solution)/shard_map/ppermute | solution.py:29
  207.3 2.7 collective-permute-start.10
  210.0 3.3 collective-permute-start.11
  213.3 5.5 %fusion.2 = (f32[4,4,128]{2,1,0:T(4,128)}, f32[4,1024,128,4]{2,1,3,0:T(8,128)}) fusion(pred[128,1024]{0,1:T(8,128)(4,1)S(1)} %get-tuple-element.87, bf16[1024,4,128,1]{0,2,3,1:T(8,128)(2,1)S(1)} %bitcast.618, bf16[128,4,4,128]{3,2,1,0:T(4,128)(2,1)S(1)} %reshape_squeeze.3), kind=kOutput, calls=%fused_computation.10 | convolution fusion | flops 543160320 | bytes 10100736 | tf_op jit(solution)/shard_map/tgjd,ugd->gjtu/dot_general | solution.py:154
  218.9 2.1 collective-permute-start.12
  221.1 4.8 %fusion.1 = (f32[4,4,128]{2,1,0:T(4,128)S(1)}, f32[4,1024,128,4]{2,1,3,0:T(8,128)}) fusion(pred[128,1024]{0,1:T(8,128)(4,1)S(1)} %copy-done.3, bf16[1024,4,128,1]{0,2,3,1:T(8,128)(2,1)S(1)} %bitcast.617, bf16[128,4,4,128]{3,2,1,0:T(4,128)(2,1)S(1)} %reshape_squeeze.3), kind=kOutput, calls=%fused_computation.9 | convolution fusion | flops 543160320 | bytes 10100736 | tf_op jit(solution)/shard_map/tgjd,ugd->gjtu/dot_general | solution.py:154
  227.6 1.5 bitcast_reduce_fusion
  230.2 4.6 %fusion.11 = f32[4,4,128]{2,1,0:T(4,128)S(1)} fusion(f32[4,1024,128,4]{2,1,3,0:T(8,128)} %get-tuple-element.94, f32[4,4,128]{2,1,0:T(4,128)S(1)} %get-tuple-element.17, pred[128,1024]{0,1:T(8,128)(4,1)S(1)} %get-tuple-element.86), kind=kLoop, calls=%fused_computation.19 | loop fusion | flops 10483712 | bytes 8536064 | tf_op jit(solution)/shard_map/reduce_sum | solution.py:73
  234.8 4.8 %fusion.9 = f32[4,4,128]{2,1,0:T(4,128)S(1)} fusion(f32[4,1024,128,4]{2,1,3,0:T(8,128)} %get-tuple-element.96, f32[4,4,128]{2,1,0:T(4,128)S(1)} %get-tuple-element.18, pred[128,1024]{0,1:T(8,128)(4,1)S(1)} %get-tuple-element.85), kind=kLoop, calls=%fused_computation.17 | loop fusion | flops 10483712 | bytes 8536064 | tf_op jit(solution)/shard_map/reduce_sum | solution.py:73
  240.0 2.0 fusion.7
  242.0 2.0 fusion.5
  244.7 1.8 copy.100
  246.5 5.9 %fusion.64 = f32[128,4,4,128]{0,3,2,1:T(8,128)S(1)} fusion(bf16[1024,4,128,1]{0,2,3,1:T(8,128)(2,1)} %bitcast.634, f32[4,1024,128,4]{2,1,3,0:T(8,128)} %get-tuple-element.100, f32[4,4,128]{2,1,0:T(4,128)} %copy-done.52, pred[128,1024]{0,1:T(8,128)(4,1)} %get-tuple-element.88, f32[128,4,4]{0,2,1:T(4,128)} %get-tuple-element.80, ...), kind=kOutput, calls=%fused_computation.59 | convolution fusion | flops 547880960 | bytes 10641408 | tf_op jit(solution)/shard_map/gjtu,ugd->tgjd/dot_general | solution.py:160
  252.5 5.7 %fusion.67 = f32[128,4,4,128]{0,3,2,1:T(8,128)S(1)} fusion(f32[128,4,4,128]{0,3,2,1:T(8,128)S(1)} %fusion.64, bf16[1024,4,128,1]{0,2,3,1:T(8,128)(2,1)S(1)} %bitcast.633, f32[4,1024,128,4]{2,1,3,0:T(8,128)} %get-tuple-element.98, f32[4,4,128]{2,1,0:T(4,128)S(1)} %copy-done.21, pred[128,1024]{0,1:T(8,128)(4,1)S(1)} %get-tuple-element.87, ...), kind=kOutput, calls=%fused_computation.60 | convolution fusion | flops 547880960 | bytes 11681792 | tf_op jit(solution)/shard_map/gjtu,ugd->tgjd/dot_general | solution.py:160
  258.3 2.4 fusion.70
  260.8 2.6 fusion.73
  263.5 1.4 fusion.189
  265.0 1.3 convolution_bitcast_fusion.1
  266.3 1.8 fusion.78
  268.3 1.5 copy.106
  270.0 1.3 copy.108
  271.6 2.4 collective-permute-start.13
  274.0 1.5 collective-permute-done.13
  275.6 4.0 %collective-permute-start.16 = (f32[4,8,1024]{2,1,0:T(8,128)S(1)}, f32[4,8,1024]{2,1,0:T(8,128)S(1)}, u32[]{:S(2)}, u32[]{:S(2)}) collective-permute-start(f32[4,8,1024]{2,1,0:T(8,128)S(1)} %get-tuple-element.56), channel_id=1, source_target_pairs={{0,6},{1,7},{2,4},{3,5},{4,2},{5,3},{6,0},{7,1},{8,14},{9,15},{10,... | collective-permute-start | bytes 393224 | tf_op jit(solution)/shard_map/ppermute | solution.py:56
  279.7 1.9 collective-permute-start.15
  281.6 4.1 %collective-permute-start.14 = (f32[4,8,1024]{2,1,0:T(8,128)S(1)}, f32[4,8,1024]{2,1,0:T(8,128)S(1)}, u32[]{:S(2)}, u32[]{:S(2)}) collective-permute-start(f32[4,8,1024]{2,1,0:T(8,128)S(1)} %get-tuple-element.55), channel_id=1, source_target_pairs={{0,2},{1,3},{2,0},{3,1},{4,6},{5,7},{6,4},{7,5},{8,10},{9,11},{10,... | collective-permute-start | bytes 393224 | tf_op jit(solution)/shard_map/ppermute | solution.py:56
  285.8 6.1 %collective-permute-done.15 = f32[4,8,1024]{2,1,0:T(8,128)S(1)} collective-permute-done((f32[4,8,1024]{2,1,0:T(8,128)S(1)}, f32[4,8,1024]{2,1,0:T(8,128)S(1)}, u32[]{:S(2)}, u32[]{:S(2)}) %collective-permute-start.15) | collective-permute-done | bytes 131104 | tf_op jit(solution)/shard_map/ppermute | solution.py:56
  292.1 5.8 %collective-permute-start.19 = (f32[1,8,1024]{2,1,0:T(8,128)S(1)}, f32[1,8,1024]{2,1,0:T(8,128)S(1)}, u32[]{:S(2)}, u32[]{:S(2)}) collective-permute-start(f32[1,8,1024]{2,1,0:T(8,128)S(1)} %get-tuple-element.74), channel_id=1, source_target_pairs={{0,24},{1,25},{2,26},{3,27},{4,28},{5,29},{6,30},{7,31},{8,16},{9,... | collective-permute-start | bytes 98312 | tf_op jit(solution)/shard_map/ppermute | solution.py:56
  297.9 4.4 %collective-permute-start.18 = (f32[1,8,1024]{2,1,0:T(8,128)S(1)}, f32[1,8,1024]{2,1,0:T(8,128)S(1)}, u32[]{:S(2)}, u32[]{:S(2)}) collective-permute-start(f32[1,8,1024]{2,1,0:T(8,128)S(1)} %get-tuple-element.75), channel_id=1, source_target_pairs={{0,16},{1,17},{2,18},{3,19},{4,20},{5,21},{6,22},{7,23},{8,24},{9,... | collective-permute-start | bytes 98312 | tf_op jit(solution)/shard_map/ppermute | solution.py:56
  302.3 4.4 %collective-permute-start.17 = (f32[1,8,1024]{2,1,0:T(8,128)S(1)}, f32[1,8,1024]{2,1,0:T(8,128)S(1)}, u32[]{:S(2)}, u32[]{:S(2)}) collective-permute-start(f32[1,8,1024]{2,1,0:T(8,128)S(1)} %get-tuple-element.73), channel_id=1, source_target_pairs={{0,8},{1,9},{2,10},{3,11},{4,12},{5,13},{6,14},{7,15},{8,0},{9,1},... | collective-permute-start | bytes 98312 | tf_op jit(solution)/shard_map/ppermute | solution.py:56
  306.8 5.4 %collective-permute-done.17 = f32[1,8,1024]{2,1,0:T(8,128)S(1)} collective-permute-done((f32[1,8,1024]{2,1,0:T(8,128)S(1)}, f32[1,8,1024]{2,1,0:T(8,128)S(1)}, u32[]{:S(2)}, u32[]{:S(2)}) %collective-permute-start.17) | collective-permute-done | bytes 32800 | tf_op jit(solution)/shard_map/ppermute | solution.py:56
  312.2 3.3 collective-permute-start.20
  315.6 4.3 %collective-permute-start.21 = (f32[1,8,1024]{2,1,0:T(8,128)S(1)}, f32[1,8,1024]{2,1,0:T(8,128)S(1)}, u32[]{:S(2)}, u32[]{:S(2)}) collective-permute-start(f32[1,8,1024]{2,1,0:T(8,128)S(1)} %add_add_fusion), channel_id=1, source_target_pairs={{0,256},{32,288},{64,320},{96,352},{128,384},{160,416},{192,448},{... | collective-permute-start | bytes 98312 | tf_op jit(solution)/shard_map/ppermute | solution.py:29
  319.9 4.6 %collective-permute-start.22 = (f32[1,8,1024]{2,1,0:T(8,128)S(1)}, f32[1,8,1024]{2,1,0:T(8,128)S(1)}, u32[]{:S(2)}, u32[]{:S(2)}) collective-permute-start(f32[1,8,1024]{2,1,0:T(8,128)S(1)} %add_add_fusion), channel_id=1, source_target_pairs={{0,128},{32,160},{64,192},{96,224},{128,0},{160,32},{192,64},{224,... | collective-permute-start | bytes 98312 | tf_op jit(solution)/shard_map/ppermute | solution.py:29
  326.7 3.9 %collective-permute-start.23 = (f32[2,2,1,8,1024]{4,3,1,0,2:T(8,128)S(1)}, f32[2,2,1,8,1024]{4,3,1,0,2:T(8,128)S(1)}, u32[]{:S(2)}, u32[]{:S(2)}) collective-permute-start(f32[2,2,1,8,1024]{4,3,1,0,2:T(8,128)S(1)} %bitcast.645), channel_id=1, source_target_pairs={{0,96},{32,64},{64,32},{96,0},{128,224},{160,192},{192,160},{224,1... | collective-permute-start | bytes 393224 | tf_op jit(solution)/shard_map/ppermute | solution.py:29
  330.5 2.4 collective-permute-start.24
  332.9 3.0 collective-permute-start.25
  337.4 2.4 collective-permute-done.25
  (212 shorter events, 17.3 us)
Async XLA Ops:
  7.2 127.8 %copy-start = (bf16[8,512]{1,0:T(8,128)(2,1)S(1)}, bf16[8,512]{1,0:T(8,128)(2,1)}, u32[]{:S(2)}) copy-start(bf16[8,512]{1,0:T(8,128)(2,1)} %param.14) | copy-start | bytes 24580
  7.2 121.6 %all-gather.2.cloned.1.call-start = ((), (), s32[]{:S(2)}) async-start(), calls=%async_computation | async-start | bytes 8650752 | tf_op jit(solution)/shard_map/all_gather | solution.py:93
  138.0 20.0 %copy-start.2 = (bf16[4096,1024]{0,1:T(8,128)(2,1)S(1)}, bf16[4096,1024]{0,1:T(8,128)(2,1)}, u32[]{:S(2)}) copy-start(bf16[4096,1024]{0,1:T(8,128)(2,1)} %all-gather.2.cloned.1.call-done) | copy-start | bytes 25165828
  145.3 15.2 %collective-permute-start = (f32[1,9,1024]{2,1,0:T(8,128)S(1)}, f32[1,9,1024]{2,1,0:T(8,128)S(1)}, u32[]{:S(2)}, u32[]{:S(2)}) collective-permute-start(f32[1,9,1024]{2,1,0:T(8,128)S(1)} %maximum_bitcast_fusion.1), channel_id=1, source_target_pairs={{0,384},{32,416},{64,448},{96,480},{128,256},{160,288},{192,320},{... | collective-permute-start | bytes 110600 | tf_op jit(solution)/shard_map/ppermute | solution.py:29
  151.9 11.0 %collective-permute-start.1 = (f32[1,9,1024]{2,1,0:T(8,128)S(1)}, f32[1,9,1024]{2,1,0:T(8,128)S(1)}, u32[]{:S(2)}, u32[]{:S(2)}) collective-permute-start(f32[1,9,1024]{2,1,0:T(8,128)S(1)} %maximum_bitcast_fusion.1), channel_id=1, source_target_pairs={{0,256},{32,288},{64,320},{96,352},{128,384},{160,416},{192,448},{... | collective-permute-start | bytes 110600 | tf_op jit(solution)/shard_map/ppermute | solution.py:29
  155.4 9.2 %collective-permute-start.2 = (f32[1,9,1024]{2,1,0:T(8,128)S(1)}, f32[1,9,1024]{2,1,0:T(8,128)S(1)}, u32[]{:S(2)}, u32[]{:S(2)}) collective-permute-start(f32[1,9,1024]{2,1,0:T(8,128)S(1)} %maximum_bitcast_fusion.1), channel_id=1, source_target_pairs={{0,128},{32,160},{64,192},{96,224},{128,0},{160,32},{192,64},{224,... | collective-permute-start | bytes 110600 | tf_op jit(solution)/shard_map/ppermute | solution.py:29
  164.7 14.1 %collective-permute-start.3 = (f32[2,2,1,9,1024]{4,3,1,0,2:T(8,128)S(1)}, f32[2,2,1,9,1024]{4,3,1,0,2:T(8,128)S(1)}, u32[]{:S(2)}, u32[]{:S(2)}) collective-permute-start(f32[2,2,1,9,1024]{4,3,1,0,2:T(8,128)S(1)} %bitcast.635), channel_id=1, source_target_pairs={{0,96},{32,64},{64,32},{96,0},{128,224},{160,192},{192,160},{224,1... | collective-permute-start | bytes 442376 | tf_op jit(solution)/shard_map/ppermute | solution.py:29
  167.0 14.1 %collective-permute-start.4 = (f32[2,2,1,9,1024]{4,3,1,0,2:T(8,128)S(1)}, f32[2,2,1,9,1024]{4,3,1,0,2:T(8,128)S(1)}, u32[]{:S(2)}, u32[]{:S(2)}) collective-permute-start(f32[2,2,1,9,1024]{4,3,1,0,2:T(8,128)S(1)} %bitcast.636), channel_id=1, source_target_pairs={{0,64},{32,96},{64,0},{96,32},{128,192},{160,224},{192,128},{224,1... | collective-permute-start | bytes 442376 | tf_op jit(solution)/shard_map/ppermute | solution.py:29
  171.5 10.1 %collective-permute-start.5 = (f32[2,2,1,9,1024]{4,3,1,0,2:T(8,128)S(1)}, f32[2,2,1,9,1024]{4,3,1,0,2:T(8,128)S(1)}, u32[]{:S(2)}, u32[]{:S(2)}) collective-permute-start(f32[2,2,1,9,1024]{4,3,1,0,2:T(8,128)S(1)} %bitcast.637), channel_id=1, source_target_pairs={{0,32},{32,0},{64,96},{96,64},{128,160},{160,128},{192,224},{224,1... | collective-permute-start | bytes 442376 | tf_op jit(solution)/shard_map/ppermute | solution.py:29
  182.0 15.5 %copy-start.26 = (f32[1,1,1024]{2,1,0:T(1,128)}, f32[1,1,1024]{2,1,0:T(1,128)S(1)}, u32[]{:S(2)}) copy-start(f32[1,1,1024]{2,1,0:T(1,128)S(1)} %get-tuple-element.34) | copy-start | bytes 12292
  182.0 15.5 %copy-start.28 = (f32[1,1,1024]{2,1,0:T(1,128)}, f32[1,1,1024]{2,1,0:T(1,128)S(1)}, u32[]{:S(2)}) copy-start(f32[1,1,1024]{2,1,0:T(1,128)S(1)} %get-tuple-element.35) | copy-start | bytes 12292
  182.0 15.5 %copy-start.30 = (f32[1,1,1024]{2,1,0:T(1,128)}, f32[1,1,1024]{2,1,0:T(1,128)S(1)}, u32[]{:S(2)}) copy-start(f32[1,1,1024]{2,1,0:T(1,128)S(1)} %get-tuple-element.36) | copy-start | bytes 12292
  182.0 15.5 %copy-start.32 = (f32[1,1,1024]{2,1,0:T(1,128)}, f32[1,1,1024]{2,1,0:T(1,128)S(1)}, u32[]{:S(2)}) copy-start(f32[1,1,1024]{2,1,0:T(1,128)S(1)} %get-tuple-element.37) | copy-start | bytes 12292
  182.0 15.5 %copy-start.34 = (f32[1,1,1024]{2,1,0:T(1,128)}, f32[1,1,1024]{2,1,0:T(1,128)S(1)}, u32[]{:S(2)}) copy-start(f32[1,1,1024]{2,1,0:T(1,128)S(1)} %get-tuple-element.38) | copy-start | bytes 12292
  182.1 15.5 %copy-start.36 = (f32[1,1,1024]{2,1,0:T(1,128)}, f32[1,1,1024]{2,1,0:T(1,128)S(1)}, u32[]{:S(2)}) copy-start(f32[1,1,1024]{2,1,0:T(1,128)S(1)} %get-tuple-element.39) | copy-start | bytes 12292
  182.1 15.5 %copy-start.38 = (f32[1,1,1024]{2,1,0:T(1,128)}, f32[1,1,1024]{2,1,0:T(1,128)S(1)}, u32[]{:S(2)}) copy-start(f32[1,1,1024]{2,1,0:T(1,128)S(1)} %get-tuple-element.40) | copy-start | bytes 12292
  182.1 15.5 %copy-start.40 = (f32[1,1,1024]{2,1,0:T(1,128)}, f32[1,1,1024]{2,1,0:T(1,128)S(1)}, u32[]{:S(2)}) copy-start(f32[1,1,1024]{2,1,0:T(1,128)S(1)} %get-tuple-element.41) | copy-start | bytes 12292
  182.1 15.5 %copy-start.42 = (f32[1,1,1024]{2,1,0:T(1,128)}, f32[1,1,1024]{2,1,0:T(1,128)S(1)}, u32[]{:S(2)}) copy-start(f32[1,1,1024]{2,1,0:T(1,128)S(1)} %get-tuple-element.42) | copy-start | bytes 12292
  182.1 15.5 %copy-start.44 = (f32[1,1,1024]{2,1,0:T(1,128)}, f32[1,1,1024]{2,1,0:T(1,128)S(1)}, u32[]{:S(2)}) copy-start(f32[1,1,1024]{2,1,0:T(1,128)S(1)} %get-tuple-element.43) | copy-start | bytes 12292
  182.1 15.5 %copy-start.46 = (f32[1,1,1024]{2,1,0:T(1,128)}, f32[1,1,1024]{2,1,0:T(1,128)S(1)}, u32[]{:S(2)}) copy-start(f32[1,1,1024]{2,1,0:T(1,128)S(1)} %get-tuple-element.44) | copy-start | bytes 12292
  182.1 15.5 %copy-start.48 = (f32[1,1,1024]{2,1,0:T(1,128)}, f32[1,1,1024]{2,1,0:T(1,128)S(1)}, u32[]{:S(2)}) copy-start(f32[1,1,1024]{2,1,0:T(1,128)S(1)} %get-tuple-element.45) | copy-start | bytes 12292
  182.1 15.5 %copy-start.50 = (f32[1,1,1024]{2,1,0:T(1,128)}, f32[1,1,1024]{2,1,0:T(1,128)S(1)}, u32[]{:S(2)}) copy-start(f32[1,1,1024]{2,1,0:T(1,128)S(1)} %get-tuple-element.46) | copy-start | bytes 12292
  182.1 36.7 %copy-start.22 = (f32[1,1,1024]{2,1,0:T(1,128)}, f32[1,1,1024]{2,1,0:T(1,128)S(1)}, u32[]{:S(2)}) copy-start(f32[1,1,1024]{2,1,0:T(1,128)S(1)} %get-tuple-element.32) | copy-start | bytes 12292
  182.1 36.7 %copy-start.24 = (f32[1,1,1024]{2,1,0:T(1,128)}, f32[1,1,1024]{2,1,0:T(1,128)S(1)}, u32[]{:S(2)}) copy-start(f32[1,1,1024]{2,1,0:T(1,128)S(1)} %get-tuple-element.33) | copy-start | bytes 12292
  182.9 20.2 %collective-permute-start.6 = (bf16[1,8,1024]{2,1,0:T(8,128)(2,1)S(1)}, bf16[1,8,1024]{2,1,0:T(8,128)(2,1)S(1)}, u32[]{:S(2)}, u32[]{:S(2)}) collective-permute-start(bf16[1,8,1024]{2,1,0:T(8,128)(2,1)S(1)} %get-tuple-element.20), channel_id=1, source_target_pairs={{0,24},{1,25},{2,26},{3,27},{4,28},{5,29},{6,30},{7,31},{8,16},{9,... | collective-permute-start | bytes 49160 | tf_op jit(solution)/shard_map/ppermute | solution.py:29
  187.9 15.3 %collective-permute-start.7 = (bf16[1,8,1024]{2,1,0:T(8,128)(2,1)S(1)}, bf16[1,8,1024]{2,1,0:T(8,128)(2,1)S(1)}, u32[]{:S(2)}, u32[]{:S(2)}) collective-permute-start(bf16[1,8,1024]{2,1,0:T(8,128)(2,1)S(1)} %get-tuple-element.20), channel_id=1, source_target_pairs={{0,16},{1,17},{2,18},{3,19},{4,20},{5,21},{6,22},{7,23},{8,24},{9,... | collective-permute-start | bytes 49160 | tf_op jit(solution)/shard_map/ppermute | solution.py:29
  192.3 10.9 %collective-permute-start.8 = (bf16[1,8,1024]{2,1,0:T(8,128)(2,1)S(1)}, bf16[1,8,1024]{2,1,0:T(8,128)(2,1)S(1)}, u32[]{:S(2)}, u32[]{:S(2)}) collective-permute-start(bf16[1,8,1024]{2,1,0:T(8,128)(2,1)S(1)} %get-tuple-element.20), channel_id=1, source_target_pairs={{0,8},{1,9},{2,10},{3,11},{4,12},{5,13},{6,14},{7,15},{8,0},{9,1},... | collective-permute-start | bytes 49160 | tf_op jit(solution)/shard_map/ppermute | solution.py:29
  203.1 17.9 %copy-start.3 = (pred[128,1024]{0,1:T(8,128)(4,1)S(1)}, pred[128,1024]{0,1:T(8,128)(4,1)}, u32[]{:S(2)}) copy-start(pred[128,1024]{0,1:T(8,128)(4,1)} %get-tuple-element.88) | copy-start | bytes 393220
  203.2 15.6 %collective-permute-start.9 = (bf16[2,2,1,8,1024]{4,3,1,0,2:T(8,128)(2,1)S(1)}, bf16[2,2,1,8,1024]{4,3,1,0,2:T(8,128)(2,1)S(1)}, u32[]{:S(2)}, u32[]{:S(2)}) collective-permute-start(bf16[2,2,1,8,1024]{4,3,1,0,2:T(8,128)(2,1)S(1)} %bitcast.651), channel_id=1, source_target_pairs={{0,6},{1,7},{2,4},{3,5},{4,2},{5,3},{6,0},{7,1},{8,14},{9,15},{10,... | collective-permute-start | bytes 196616 | tf_op jit(solution)/shard_map/ppermute | solution.py:29
  207.3 11.6 %collective-permute-start.10 = (bf16[2,2,1,8,1024]{4,3,1,0,2:T(8,128)(2,1)S(1)}, bf16[2,2,1,8,1024]{4,3,1,0,2:T(8,128)(2,1)S(1)}, u32[]{:S(2)}, u32[]{:S(2)}) collective-permute-start(bf16[2,2,1,8,1024]{4,3,1,0,2:T(8,128)(2,1)S(1)} %bitcast.652), channel_id=1, source_target_pairs={{0,4},{1,5},{2,6},{3,7},{4,0},{5,1},{6,2},{7,3},{8,12},{9,13},{10,... | collective-permute-start | bytes 196616 | tf_op jit(solution)/shard_map/ppermute | solution.py:29
  210.0 8.9 %collective-permute-start.11 = (bf16[2,2,1,8,1024]{4,3,1,0,2:T(8,128)(2,1)S(1)}, bf16[2,2,1,8,1024]{4,3,1,0,2:T(8,128)(2,1)S(1)}, u32[]{:S(2)}, u32[]{:S(2)}) collective-permute-start(bf16[2,2,1,8,1024]{4,3,1,0,2:T(8,128)(2,1)S(1)} %bitcast.653), channel_id=1, source_target_pairs={{0,2},{1,3},{2,0},{3,1},{4,6},{5,7},{6,4},{7,5},{8,10},{9,11},{10,... | collective-permute-start | bytes 196616 | tf_op jit(solution)/shard_map/ppermute | solution.py:29
  218.9 6.9 %collective-permute-start.12 = (bf16[2,2,2,2,1,8,1024]{6,5,3,2,1,0,4:T(8,128)(2,1)S(1)}, bf16[2,2,2,2,1,8,1024]{6,5,3,2,1,0,4:T(8,128)(2,1)S(1)}, u32[]{:S(2)}, u32[]{:S(2)}) collective-permute-start(bf16[2,2,2,2,1,8,1024]{6,5,3,2,1,0,4:T(8,128)(2,1)S(1)} %bitcast.639), channel_id=1, source_target_pairs={{0,1},{1,0},{2,3},{3,2},{4,5},{5,4},{6,7},{7,6},{8,9},{9,8},{10,11... | collective-permute-start | bytes 786440 | tf_op jit(solution)/shard_map/ppermute | solution.py:29
  229.8 14.9 %copy-start.14 = (f32[4,4,128]{2,1,0:T(4,128)}, f32[4,4,128]{2,1,0:T(4,128)S(1)}, u32[]{:S(2)}) copy-start(f32[4,4,128]{2,1,0:T(4,128)S(1)} %get-tuple-element.16) | copy-start | bytes 24580
  229.8 14.9 %copy-start.16 = (f32[4,4,128]{2,1,0:T(4,128)}, f32[4,4,128]{2,1,0:T(4,128)S(1)}, u32[]{:S(2)}) copy-start(f32[4,4,128]{2,1,0:T(4,128)S(1)} %get-tuple-element.17) | copy-start | bytes 24580
  266.3 74.5 %copy-start.1 = (bf16[8,512]{1,0:T(8,128)(2,1)S(1)}, bf16[8,512]{1,0:T(8,128)(2,1)}, u32[]{:S(2)}) copy-start(bf16[8,512]{1,0:T(8,128)(2,1)} %param.14) | copy-start | bytes 24580
  268.1 67.8 %copy-start.8 = (bf16[128,4,4,128]{0,3,2,1:T(8,128)(2,1)S(1)}, bf16[128,4,4,128]{0,3,2,1:T(8,128)(2,1)}, u32[]{:S(2)}) copy-start(bf16[128,4,4,128]{0,3,2,1:T(8,128)(2,1)} %get-tuple-element.101) | copy-start | bytes 1572868
  268.1 71.9 %copy-start.23 = (f32[1,1,1024]{2,1,0:T(1,128)S(1)}, f32[1,1,1024]{2,1,0:T(1,128)}, u32[]{:S(2)}) copy-start(f32[1,1,1024]{2,1,0:T(1,128)} %copy-done.22) | copy-start | bytes 12292
  268.1 71.9 %copy-start.25 = (f32[1,1,1024]{2,1,0:T(1,128)S(1)}, f32[1,1,1024]{2,1,0:T(1,128)}, u32[]{:S(2)}) copy-start(f32[1,1,1024]{2,1,0:T(1,128)} %copy-done.24) | copy-start | bytes 12292
  268.1 71.9 %copy-start.27 = (f32[1,1,1024]{2,1,0:T(1,128)S(1)}, f32[1,1,1024]{2,1,0:T(1,128)}, u32[]{:S(2)}) copy-start(f32[1,1,1024]{2,1,0:T(1,128)} %copy-done.26) | copy-start | bytes 12292
  268.1 71.9 %copy-start.29 = (f32[1,1,1024]{2,1,0:T(1,128)S(1)}, f32[1,1,1024]{2,1,0:T(1,128)}, u32[]{:S(2)}) copy-start(f32[1,1,1024]{2,1,0:T(1,128)} %copy-done.28) | copy-start | bytes 12292
  268.1 71.9 %copy-start.31 = (f32[1,1,1024]{2,1,0:T(1,128)S(1)}, f32[1,1,1024]{2,1,0:T(1,128)}, u32[]{:S(2)}) copy-start(f32[1,1,1024]{2,1,0:T(1,128)} %copy-done.30) | copy-start | bytes 12292
  268.2 71.9 %copy-start.33 = (f32[1,1,1024]{2,1,0:T(1,128)S(1)}, f32[1,1,1024]{2,1,0:T(1,128)}, u32[]{:S(2)}) copy-start(f32[1,1,1024]{2,1,0:T(1,128)} %copy-done.32) | copy-start | bytes 12292
  268.2 71.9 %copy-start.35 = (f32[1,1,1024]{2,1,0:T(1,128)S(1)}, f32[1,1,1024]{2,1,0:T(1,128)}, u32[]{:S(2)}) copy-start(f32[1,1,1024]{2,1,0:T(1,128)} %copy-done.34) | copy-start | bytes 12292
  268.2 71.9 %copy-start.37 = (f32[1,1,1024]{2,1,0:T(1,128)S(1)}, f32[1,1,1024]{2,1,0:T(1,128)}, u32[]{:S(2)}) copy-start(f32[1,1,1024]{2,1,0:T(1,128)} %copy-done.36) | copy-start | bytes 12292
  268.2 71.9 %copy-start.39 = (f32[1,1,1024]{2,1,0:T(1,128)S(1)}, f32[1,1,1024]{2,1,0:T(1,128)}, u32[]{:S(2)}) copy-start(f32[1,1,1024]{2,1,0:T(1,128)} %copy-done.38) | copy-start | bytes 12292
  268.2 71.9 %copy-start.41 = (f32[1,1,1024]{2,1,0:T(1,128)S(1)}, f32[1,1,1024]{2,1,0:T(1,128)}, u32[]{:S(2)}) copy-start(f32[1,1,1024]{2,1,0:T(1,128)} %copy-done.40) | copy-start | bytes 12292
  268.2 71.9 %copy-start.43 = (f32[1,1,1024]{2,1,0:T(1,128)S(1)}, f32[1,1,1024]{2,1,0:T(1,128)}, u32[]{:S(2)}) copy-start(f32[1,1,1024]{2,1,0:T(1,128)} %copy-done.42) | copy-start | bytes 12292
  268.2 71.9 %copy-start.45 = (f32[1,1,1024]{2,1,0:T(1,128)S(1)}, f32[1,1,1024]{2,1,0:T(1,128)}, u32[]{:S(2)}) copy-start(f32[1,1,1024]{2,1,0:T(1,128)} %copy-done.44) | copy-start | bytes 12292
  268.2 71.9 %copy-start.47 = (f32[1,1,1024]{2,1,0:T(1,128)S(1)}, f32[1,1,1024]{2,1,0:T(1,128)}, u32[]{:S(2)}) copy-start(f32[1,1,1024]{2,1,0:T(1,128)} %copy-done.46) | copy-start | bytes 12292
  268.2 71.9 %copy-start.49 = (f32[1,1,1024]{2,1,0:T(1,128)S(1)}, f32[1,1,1024]{2,1,0:T(1,128)}, u32[]{:S(2)}) copy-start(f32[1,1,1024]{2,1,0:T(1,128)} %copy-done.48) | copy-start | bytes 12292
  268.2 71.9 %copy-start.51 = (f32[1,1,1024]{2,1,0:T(1,128)S(1)}, f32[1,1,1024]{2,1,0:T(1,128)}, u32[]{:S(2)}) copy-start(f32[1,1,1024]{2,1,0:T(1,128)} %copy-done.50) | copy-start | bytes 12292
  271.6 3.9 %collective-permute-start.13 = (f32[16,8,1024]{2,1,0:T(8,128)S(1)}, f32[16,8,1024]{2,1,0:T(8,128)S(1)}, u32[]{:S(2)}, u32[]{:S(2)}) collective-permute-start(f32[16,8,1024]{2,1,0:T(8,128)S(1)} %dynamic-slice_bitcast_fusion), channel_id=1, source_target_pairs={{0,1},{1,0},{2,3},{3,2},{4,5},{5,4},{6,7},{7,6},{8,9},{9,8},{10,11... | collective-permute-start | bytes 1572872 | tf_op jit(solution)/shard_map/ppermute | solution.py:56
  275.6 10.2 %collective-permute-start.16 = (f32[4,8,1024]{2,1,0:T(8,128)S(1)}, f32[4,8,1024]{2,1,0:T(8,128)S(1)}, u32[]{:S(2)}, u32[]{:S(2)}) collective-permute-start(f32[4,8,1024]{2,1,0:T(8,128)S(1)} %get-tuple-element.56), channel_id=1, source_target_pairs={{0,6},{1,7},{2,4},{3,5},{4,2},{5,3},{6,0},{7,1},{8,14},{9,15},{10,... | collective-permute-start | bytes 393224 | tf_op jit(solution)/shard_map/ppermute | solution.py:56
  279.7 12.2 %collective-permute-start.15 = (f32[4,8,1024]{2,1,0:T(8,128)S(1)}, f32[4,8,1024]{2,1,0:T(8,128)S(1)}, u32[]{:S(2)}, u32[]{:S(2)}) collective-permute-start(f32[4,8,1024]{2,1,0:T(8,128)S(1)} %get-tuple-element.57), channel_id=1, source_target_pairs={{0,4},{1,5},{2,6},{3,7},{4,0},{5,1},{6,2},{7,3},{8,12},{9,13},{10,... | collective-permute-start | bytes 393224 | tf_op jit(solution)/shard_map/ppermute | solution.py:56
  281.6 10.4 %collective-permute-start.14 = (f32[4,8,1024]{2,1,0:T(8,128)S(1)}, f32[4,8,1024]{2,1,0:T(8,128)S(1)}, u32[]{:S(2)}, u32[]{:S(2)}) collective-permute-start(f32[4,8,1024]{2,1,0:T(8,128)S(1)} %get-tuple-element.55), channel_id=1, source_target_pairs={{0,2},{1,3},{2,0},{3,1},{4,6},{5,7},{6,4},{7,5},{8,10},{9,11},{10,... | collective-permute-start | bytes 393224 | tf_op jit(solution)/shard_map/ppermute | solution.py:56
  292.1 14.7 %collective-permute-start.19 = (f32[1,8,1024]{2,1,0:T(8,128)S(1)}, f32[1,8,1024]{2,1,0:T(8,128)S(1)}, u32[]{:S(2)}, u32[]{:S(2)}) collective-permute-start(f32[1,8,1024]{2,1,0:T(8,128)S(1)} %get-tuple-element.74), channel_id=1, source_target_pairs={{0,24},{1,25},{2,26},{3,27},{4,28},{5,29},{6,30},{7,31},{8,16},{9,... | collective-permute-start | bytes 98312 | tf_op jit(solution)/shard_map/ppermute | solution.py:56
  297.9 8.8 %collective-permute-start.18 = (f32[1,8,1024]{2,1,0:T(8,128)S(1)}, f32[1,8,1024]{2,1,0:T(8,128)S(1)}, u32[]{:S(2)}, u32[]{:S(2)}) collective-permute-start(f32[1,8,1024]{2,1,0:T(8,128)S(1)} %get-tuple-element.75), channel_id=1, source_target_pairs={{0,16},{1,17},{2,18},{3,19},{4,20},{5,21},{6,22},{7,23},{8,24},{9,... | collective-permute-start | bytes 98312 | tf_op jit(solution)/shard_map/ppermute | solution.py:56
  302.3 9.9 %collective-permute-start.17 = (f32[1,8,1024]{2,1,0:T(8,128)S(1)}, f32[1,8,1024]{2,1,0:T(8,128)S(1)}, u32[]{:S(2)}, u32[]{:S(2)}) collective-permute-start(f32[1,8,1024]{2,1,0:T(8,128)S(1)} %get-tuple-element.73), channel_id=1, source_target_pairs={{0,8},{1,9},{2,10},{3,11},{4,12},{5,13},{6,14},{7,15},{8,0},{9,1},... | collective-permute-start | bytes 98312 | tf_op jit(solution)/shard_map/ppermute | solution.py:56
  312.2 12.2 %collective-permute-start.20 = (f32[1,8,1024]{2,1,0:T(8,128)S(1)}, f32[1,8,1024]{2,1,0:T(8,128)S(1)}, u32[]{:S(2)}, u32[]{:S(2)}) collective-permute-start(f32[1,8,1024]{2,1,0:T(8,128)S(1)} %add_add_fusion), channel_id=1, source_target_pairs={{0,384},{32,416},{64,448},{96,480},{128,256},{160,288},{192,320},{... | collective-permute-start | bytes 98312 | tf_op jit(solution)/shard_map/ppermute | solution.py:29
  315.6 10.0 %collective-permute-start.21 = (f32[1,8,1024]{2,1,0:T(8,128)S(1)}, f32[1,8,1024]{2,1,0:T(8,128)S(1)}, u32[]{:S(2)}, u32[]{:S(2)}) collective-permute-start(f32[1,8,1024]{2,1,0:T(8,128)S(1)} %add_add_fusion), channel_id=1, source_target_pairs={{0,256},{32,288},{64,320},{96,352},{128,384},{160,416},{192,448},{... | collective-permute-start | bytes 98312 | tf_op jit(solution)/shard_map/ppermute | solution.py:29
  319.9 6.7 %collective-permute-start.22 = (f32[1,8,1024]{2,1,0:T(8,128)S(1)}, f32[1,8,1024]{2,1,0:T(8,128)S(1)}, u32[]{:S(2)}, u32[]{:S(2)}) collective-permute-start(f32[1,8,1024]{2,1,0:T(8,128)S(1)} %add_add_fusion), channel_id=1, source_target_pairs={{0,128},{32,160},{64,192},{96,224},{128,0},{160,32},{192,64},{224,... | collective-permute-start | bytes 98312 | tf_op jit(solution)/shard_map/ppermute | solution.py:29
  326.7 10.3 %collective-permute-start.23 = (f32[2,2,1,8,1024]{4,3,1,0,2:T(8,128)S(1)}, f32[2,2,1,8,1024]{4,3,1,0,2:T(8,128)S(1)}, u32[]{:S(2)}, u32[]{:S(2)}) collective-permute-start(f32[2,2,1,8,1024]{4,3,1,0,2:T(8,128)S(1)} %bitcast.645), channel_id=1, source_target_pairs={{0,96},{32,64},{64,32},{96,0},{128,224},{160,192},{192,160},{224,1... | collective-permute-start | bytes 393224 | tf_op jit(solution)/shard_map/ppermute | solution.py:29
  330.5 6.9 %collective-permute-start.24 = (f32[2,2,1,8,1024]{4,3,1,0,2:T(8,128)S(1)}, f32[2,2,1,8,1024]{4,3,1,0,2:T(8,128)S(1)}, u32[]{:S(2)}, u32[]{:S(2)}) collective-permute-start(f32[2,2,1,8,1024]{4,3,1,0,2:T(8,128)S(1)} %bitcast.646), channel_id=1, source_target_pairs={{0,64},{32,96},{64,0},{96,32},{128,192},{160,224},{192,128},{224,1... | collective-permute-start | bytes 393224 | tf_op jit(solution)/shard_map/ppermute | solution.py:29
  332.9 6.9 %collective-permute-start.25 = (f32[2,2,1,8,1024]{4,3,1,0,2:T(8,128)S(1)}, f32[2,2,1,8,1024]{4,3,1,0,2:T(8,128)S(1)}, u32[]{:S(2)}, u32[]{:S(2)}) collective-permute-start(f32[2,2,1,8,1024]{4,3,1,0,2:T(8,128)S(1)} %bitcast.647), channel_id=1, source_target_pairs={{0,32},{32,0},{64,96},{96,64},{128,160},{160,128},{192,224},{224,1... | collective-permute-start | bytes 393224 | tf_op jit(solution)/shard_map/ppermute | solution.py:29
  (30 other events, 194.5 us)
Sparse Core Ops, SparseCore 0:
  11.7 117.0 all-gather.1
where the time goes:
time: 349 us; the launch traced here: 348 us
  waiting for transfers between devices  132 us (38%)
  starting transfers between devices  97.4 us (28%)
  matrix products  53.2 us (15%)
  other arithmetic  24.5 us (7%)
  local copies, waits for them, and re-layouts  24.4 us (7%)
  between operations  16.4 us (5%)
    all_gather x1, waiting for transfers between devices, shards(): lax.all_gather(jnp.concatenate([seg_keys[0], seg_values[0]], axis=1), 'to...  107 us
    ppermute x19, starting transfers between devices, gathered(): lax.ppermute(held, axis, [(i, i ^ flip) for i in range(size)])  70.2 us
    ppermute x7, starting transfers between devices, scattered_sum(): lax.ppermute(send, axis, [(i, i ^ flip) for i in range(size)])  27.1 us
    dot_general x4, matrix products, shards(): jnp.einsum('tgjd,ugd->gjtu', queries, key_block, preferred_element_type=j...  20.6 us
    dot_general x4, matrix products, shards(): jnp.einsum('gjtu,ugd->tgjd', seg_weights, value_block, preferred_element_...  16.5 us
    reduce_sum x4, other arithmetic, softmax_step(): new_total = row_total * multiplier + jnp.sum(weights, axis=-1)  13.4 us
    ppermute x7, waiting for transfers between devices, scattered_sum(): lax.ppermute(send, axis, [(i, i ^ flip) for i in range(size)])  13.2 us
    ppermute x19, waiting for transfers between devices, gathered(): lax.ppermute(held, axis, [(i, i ^ flip) for i in range(size)])  11.8 us
  transfers between devices with their start and end apart: 27, of which 13 were waited for; matrix products, arithmetic and copies ran while one was open for 10% of the time, Pallas kernels for 0%

commit v1 on v0

--- a/solution.py
+++ b/solution.py
@@ -137,7 +137,7 @@
         following_memory = all_decay[step] * memory_in + all_carried[step]
         memory_in = jnp.where(step < seg_index, following_memory, memory_in)
 
-    block_rows = math.gcd(piece_rows, 1024)
+    block_rows = math.gcd(piece_rows, 2048)
     blocks = piece_rows // block_rows
     running = (
         jnp.full((KVH, group_size, tok_rows), neg_fill, jnp.float32),

time: 349 us -> 351 us (level)
  waiting for transfers between devices: 132 us -> 142 us
  matrix products: 53.2 us -> 45.4 us
    all_gather x1, waiting for transfers between devices: 107 us -> 114 us  [shards(): lax.all_gather(jnp.concatenate([seg_keys[0], seg_values[0]], axis=1), 'to...]
    dot_general x4 -> x2, matrix products: 20.6 us -> 14.8 us  [shards(): jnp.einsum('tgjd,ugd->gjtu', queries, key_block, preferred_element_type=j...]
    reduce_sum x4 -> x2, other arithmetic: 13.4 us -> 12.8 us  [softmax_step(): new_total = row_total * multiplier + jnp.sum(weights, axis=-1)]
    dot_general x4 -> x2, matrix products: 16.5 us -> 16.9 us  [shards(): jnp.einsum('gjtu,ugd->tgjd', seg_weights, value_block, preferred_element_...]
  transfers between devices with their start and end apart: 27 -> 27, of which waited for: 13 -> 12; matrix products, arithmetic and copies ran while one was open for 10% -> 8% of each run, Pallas kernels for 0% -> 0%
where the time goes in v1:
time: 351 us; the launch traced here: 349 us
  waiting for transfers between devices  142 us (40%)
  starting transfers between devices  97.4 us (28%)
  matrix products  45.4 us (13%)
  local copies, waits for them, and re-layouts  26.8 us (8%)
  other arithmetic  22 us (6%)
  between operations  15.7 us (4%)
    all_gather x1, waiting for transfers between devices, shards(): lax.all_gather(jnp.concatenate([seg_keys[0], seg_values[0]], axis=1), 'to...  114 us
    ppermute x19, starting transfers between devices, gathered(): lax.ppermute(held, axis, [(i, i ^ flip) for i in range(size)])  70.2 us
    ppermute x7, starting transfers between devices, scattered_sum(): lax.ppermute(send, axis, [(i, i ^ flip) for i in range(size)])  27.1 us
    dot_general x2, matrix products, shards(): jnp.einsum('gjtu,ugd->tgjd', seg_weights, value_block, preferred_element_...  16.9 us
    ppermute x19, waiting for transfers between devices, gathered(): lax.ppermute(held, axis, [(i, i ^ flip) for i in range(size)])  15.3 us
    dot_general x2, matrix products, shards(): jnp.einsum('tgjd,ugd->gjtu', queries, key_block, preferred_element_type=j...  14.8 us
    ppermute x7, waiting for transfers between devices, scattered_sum(): lax.ppermute(send, axis, [(i, i ^ flip) for i in range(size)])  13.3 us
    reduce_sum x2, other arithmetic, softmax_step(): new_total = row_total * multiplier + jnp.sum(weights, axis=-1)  12.8 us
  transfers between devices with their start and end apart: 27, of which 12 were waited for; matrix products, arithmetic and copies ran while one was open for 8% of the time, Pallas kernels for 0%

profile of v1, /device:TPU:2, one launch (start us, length us, event | category | flops | bytes accessed | tf_op | source)
XLA Modules:
  0.0 349.5 jit_solution(870559153786943836)
XLA Ops:
  7.2 1.0 copy.64
  8.3 1.0 copy.63
  10.0 1.2 dynamic_slice.32
  12.0 1.2 dynamic_slice.31
  15.2 113.6 %all-gather.2.cloned.1.call-done = bf16[4096,1024]{0,1:T(8,128)(2,1)} async-done(((bf16[128,1024]{0,1:T(8,128)(2,1)}), bf16[4096,1024]{0,1:T(8,128)(2,1)}) %all-gather.2.cloned.1.call-update) | async-done | bytes 8388624 | tf_op jit(solution)/shard_map/all_gather | solution.py:93
  128.8 6.0 %fusion.142 = (bf16[4096,512]{0,1:T(8,128)(2,1)}, bf16[4096,512]{0,1:T(8,128)(2,1)}) fusion(bf16[4096,1024]{0,1:T(8,128)(2,1)} %all-gather.2.cloned.1.call-done), kind=kLoop, calls=%fused_computation.237 | loop fusion | bytes 16777216 | tf_op jit(solution)/shard_map/slice | solution.py:97
  134.8 3.1 fusion.146
  137.9 3.5 %fusion.50 = f32[8,4,128]{2,0,1:T(8,128)S(1)} fusion(bf16[4096,4,128]{0,2,1:T(8,128)(2,1)} %bitcast.487, bf16[4,8,4096]{2,1,0:T(8,128)(2,1)S(1)} %get-tuple-element.80, f32[8,4]{0,1:T(4,128)S(1)} %bitcast.554), kind=kOutput, calls=%fused_computation.50 | convolution fusion | flops 33558528 | bytes 4472960 | tf_op jit(solution)/shard_map/gru,ugd->rgd/dot_general | solution.py:110
  141.4 1.2 fusion.49
  142.8 6.6 %collective-permute-start = (f32[1,9,1024]{2,1,0:T(8,128)S(1)}, f32[1,9,1024]{2,1,0:T(8,128)S(1)}, u32[]{:S(2)}, u32[]{:S(2)}) collective-permute-start(f32[1,9,1024]{2,1,0:T(8,128)S(1)} %maximum_bitcast_fusion.1), channel_id=1, source_target_pairs={{0,384},{32,416},{64,448},{96,480},{128,256},{160,288},{192,320},{... | collective-permute-start | bytes 110600 | tf_op jit(solution)/shard_map/ppermute | solution.py:29
  149.4 3.5 %collective-permute-start.1 = (f32[1,9,1024]{2,1,0:T(8,128)S(1)}, f32[1,9,1024]{2,1,0:T(8,128)S(1)}, u32[]{:S(2)}, u32[]{:S(2)}) collective-permute-start(f32[1,9,1024]{2,1,0:T(8,128)S(1)} %maximum_bitcast_fusion.1), channel_id=1, source_target_pairs={{0,256},{32,288},{64,320},{96,352},{128,384},{160,416},{192,448},{... | collective-permute-start | bytes 110600 | tf_op jit(solution)/shard_map/ppermute | solution.py:29
  153.0 2.7 collective-permute-start.2
  155.7 4.7 %collective-permute-done.1 = f32[1,9,1024]{2,1,0:T(8,128)S(1)} collective-permute-done((f32[1,9,1024]{2,1,0:T(8,128)S(1)}, f32[1,9,1024]{2,1,0:T(8,128)S(1)}, u32[]{:S(2)}, u32[]{:S(2)}) %collective-permute-start.1) | collective-permute-done | bytes 36896 | tf_op jit(solution)/shard_map/ppermute | solution.py:29
  160.4 1.8 collective-permute-done.2
  162.3 2.3 collective-permute-start.3
  164.6 4.4 %collective-permute-start.4 = (f32[2,2,1,9,1024]{4,3,1,0,2:T(8,128)S(1)}, f32[2,2,1,9,1024]{4,3,1,0,2:T(8,128)S(1)}, u32[]{:S(2)}, u32[]{:S(2)}) collective-permute-start(f32[2,2,1,9,1024]{4,3,1,0,2:T(8,128)S(1)} %bitcast.503), channel_id=1, source_target_pairs={{0,64},{32,96},{64,0},{96,32},{128,192},{160,224},{192,128},{224,1... | collective-permute-start | bytes 442376 | tf_op jit(solution)/shard_map/ppermute | solution.py:29
  169.0 2.5 collective-permute-start.5
  171.5 1.7 compare_and_fusion
  174.7 4.0 %collective-permute-done.4 = f32[2,2,1,9,1024]{4,3,1,0,2:T(8,128)S(1)} collective-permute-done((f32[2,2,1,9,1024]{4,3,1,0,2:T(8,128)S(1)}, f32[2,2,1,9,1024]{4,3,1,0,2:T(8,128)S(1)}, u32[]{:S(2)}, u32[]{:S(2)}) %collective-permute-start.4) | collective-permute-done | bytes 147488 | tf_op jit(solution)/shard_map/ppermute | solution.py:29
  179.4 1.2 select_bitcast_fusion.5
  180.9 0.7 convert_bitcast_fusion
  181.6 4.8 %collective-permute-start.6 = (bf16[1,8,1024]{2,1,0:T(8,128)(2,1)S(1)}, bf16[1,8,1024]{2,1,0:T(8,128)(2,1)S(1)}, u32[]{:S(2)}, u32[]{:S(2)}) collective-permute-start(bf16[1,8,1024]{2,1,0:T(8,128)(2,1)S(1)} %get-tuple-element.16), channel_id=1, source_target_pairs={{0,24},{1,25},{2,26},{3,27},{4,28},{5,29},{6,30},{7,31},{8,16},{9,... | collective-permute-start | bytes 49160 | tf_op jit(solution)/shard_map/ppermute | solution.py:29
  186.4 4.6 %collective-permute-start.7 = (bf16[1,8,1024]{2,1,0:T(8,128)(2,1)S(1)}, bf16[1,8,1024]{2,1,0:T(8,128)(2,1)S(1)}, u32[]{:S(2)}, u32[]{:S(2)}) collective-permute-start(bf16[1,8,1024]{2,1,0:T(8,128)(2,1)S(1)} %get-tuple-element.16), channel_id=1, source_target_pairs={{0,16},{1,17},{2,18},{3,19},{4,20},{5,21},{6,22},{7,23},{8,24},{9,... | collective-permute-start | bytes 49160 | tf_op jit(solution)/shard_map/ppermute | solution.py:29
  191.0 5.3 %collective-permute-start.8 = (bf16[1,8,1024]{2,1,0:T(8,128)(2,1)S(1)}, bf16[1,8,1024]{2,1,0:T(8,128)(2,1)S(1)}, u32[]{:S(2)}, u32[]{:S(2)}) collective-permute-start(bf16[1,8,1024]{2,1,0:T(8,128)(2,1)S(1)} %get-tuple-element.16), channel_id=1, source_target_pairs={{0,8},{1,9},{2,10},{3,11},{4,12},{5,13},{6,14},{7,15},{8,0},{9,1},... | collective-permute-start | bytes 49160 | tf_op jit(solution)/shard_map/ppermute | solution.py:29
  196.2 5.2 %fusion.143 = (bf16[2048,512]{0,1:T(8,128)(2,1)}, bf16[2048,512]{0,1:T(8,128)(2,1)S(1)}, bf16[2048,512]{0,1:T(8,128)(2,1)}, bf16[2048,512]{0,1:T(8,128)(2,1)S(1)}) fusion(bf16[4096,1024]{0,1:T(8,128)(2,1)} %all-gather.2.cloned.1.call-done), kind=kLoop, calls=%fused_computation.238 | loop fusion | bytes 16777216 | tf_op jit(solution)/shard_map/slice | solution.py:150
  201.5 4.2 %collective-permute-start.9 = (bf16[2,2,1,8,1024]{4,3,1,0,2:T(8,128)(2,1)S(1)}, bf16[2,2,1,8,1024]{4,3,1,0,2:T(8,128)(2,1)S(1)}, u32[]{:S(2)}, u32[]{:S(2)}) collective-permute-start(bf16[2,2,1,8,1024]{4,3,1,0,2:T(8,128)(2,1)S(1)} %bitcast.518), channel_id=1, source_target_pairs={{0,6},{1,7},{2,4},{3,5},{4,2},{5,3},{6,0},{7,1},{8,14},{9,15},{10,... | collective-permute-start | bytes 196616 | tf_op jit(solution)/shard_map/ppermute | solution.py:29
  205.7 2.6 collective-permute-start.10
  208.2 3.3 collective-permute-start.11
  211.6 7.4 %fusion.2 = (f32[4,4,128]{2,1,0:T(4,128)S(1)}, f32[4,2048,128,4]{2,1,3,0:T(8,128)}) fusion(pred[128,2048]{0,1:T(8,128)(4,1)S(1)} %get-tuple-element.77, bf16[2048,4,128,1]{0,2,3,1:T(8,128)(2,1)S(1)} %bitcast.489, bf16[128,4,4,128]{3,2,1,0:T(4,128)(2,1)S(1)} %reshape_squeeze.3), kind=kOutput, calls=%fused_computation.6 | convolution fusion | flops 1086322688 | bytes 19668992 | tf_op jit(solution)/shard_map/tgjd,ugd->gjtu/dot_general | solution.py:154
  219.1 2.1 collective-permute-start.12
  221.2 7.4 %fusion.1 = (f32[4,4,128]{2,1,0:T(4,128)S(1)}, f32[4,2048,128,4]{2,1,3,0:T(8,128)}) fusion(pred[128,2048]{0,1:T(8,128)(4,1)S(1)} %get-tuple-element.78, bf16[2048,4,128,1]{0,2,3,1:T(8,128)(2,1)S(1)} %bitcast.488, bf16[128,4,4,128]{3,2,1,0:T(4,128)(2,1)S(1)} %reshape_squeeze.3), kind=kOutput, calls=%fused_computation.5 | convolution fusion | flops 1086322688 | bytes 19668992 | tf_op jit(solution)/shard_map/tgjd,ugd->gjtu/dot_general | solution.py:154
  229.5 0.8 copy.79
  230.4 1.5 bitcast_reduce_fusion
  232.2 8.8 %fusion.5 = f32[4,4,128]{2,1,0:T(4,128)S(1)} fusion(f32[4,2048,128,4]{2,1,3,0:T(8,128)} %get-tuple-element.84, f32[4,4,128]{2,1,0:T(4,128)S(1)} %get-tuple-element.15, pred[128,2048]{0,1:T(8,128)(4,1)S(1)} %get-tuple-element.77), kind=kLoop, calls=%fused_computation.9 | loop fusion | flops 20969472 | bytes 17055744 | tf_op jit(solution)/shard_map/reduce_sum | solution.py:73
  240.9 1.8 copy-done.2
  242.8 4.0 %fusion.3 = f32[4,4,128]{2,1,0:T(4,128)S(1)} fusion(f32[4,2048,128,4]{2,1,3,0:T(8,128)S(1)} %copy-done.2, f32[4,4,128]{2,1,0:T(4,128)S(1)} %get-tuple-element.74, pred[128,2048]{0,1:T(8,128)(4,1)S(1)} %copy-done.5), kind=kLoop, calls=%fused_computation.7 | loop fusion | flops 20969472 | bytes 17055744 | tf_op jit(solution)/shard_map/reduce_sum | solution.py:73
  246.8 1.8 copy.82
  248.6 8.7 %fusion.43 = f32[128,4,4,128]{0,3,2,1:T(8,128)S(1)} fusion(bf16[2048,4,128,1]{0,2,3,1:T(8,128)(2,1)} %bitcast.501, f32[4,2048,128,4]{2,1,3,0:T(8,128)} %get-tuple-element.86, f32[4,4,128]{2,1,0:T(4,128)S(1)} %get-tuple-element.74, pred[128,2048]{0,1:T(8,128)(4,1)} %copy-done.4, f32[128,4,4]{0,2,1:T(4,128)S(1)} %get-tuple-element.72, ...), kind=kOutput, calls=%fused_computation.42 | convolution fusion | flops 1095237632 | bytes 20209664 | tf_op jit(solution)/shard_map/gjtu,ugd->tgjd/dot_general | solution.py:160
  257.4 8.2 %fusion.37 = f32[128,4,4,128]{0,3,2,1:T(8,128)S(1)} fusion(f32[128,4,4,128]{0,3,2,1:T(8,128)S(1)} %fusion.43, bf16[2048,4,128,1]{0,2,3,1:T(8,128)(2,1)S(1)} %bitcast.500, f32[4,2048,128,4]{2,1,3,0:T(8,128)} %get-tuple-element.84, f32[4,4,128]{2,1,0:T(4,128)S(1)} %get-tuple-element.15, pred[128,2048]{0,1:T(8,128)(4,1)S(1)} %get-tuple-element.77, ...), kind=kOutput, calls=%fused_computation.40 | convolution fusion | flops 1095237632 | bytes 21250048 | tf_op jit(solution)/shard_map/gjtu,ugd->tgjd/dot_general | solution.py:160
  265.6 1.4 fusion.147
  267.2 1.3 convolution_bitcast_fusion.1
  268.5 1.8 fusion.48
  270.2 1.4 copy.88
  271.9 1.3 copy.90
  273.6 2.4 collective-permute-start.13
  276.0 1.5 collective-permute-done.13
  277.6 4.2 %collective-permute-start.16 = (f32[4,8,1024]{2,1,0:T(8,128)S(1)}, f32[4,8,1024]{2,1,0:T(8,128)S(1)}, u32[]{:S(2)}, u32[]{:S(2)}) collective-permute-start(f32[4,8,1024]{2,1,0:T(8,128)S(1)} %get-tuple-element.48), channel_id=1, source_target_pairs={{0,6},{1,7},{2,4},{3,5},{4,2},{5,3},{6,0},{7,1},{8,14},{9,15},{10,... | collective-permute-start | bytes 393224 | tf_op jit(solution)/shard_map/ppermute | solution.py:56
  281.8 1.9 collective-permute-start.15
  283.7 4.0 %collective-permute-start.14 = (f32[4,8,1024]{2,1,0:T(8,128)S(1)}, f32[4,8,1024]{2,1,0:T(8,128)S(1)}, u32[]{:S(2)}, u32[]{:S(2)}) collective-permute-start(f32[4,8,1024]{2,1,0:T(8,128)S(1)} %get-tuple-element.47), channel_id=1, source_target_pairs={{0,2},{1,3},{2,0},{3,1},{4,6},{5,7},{6,4},{7,5},{8,10},{9,11},{10,... | collective-permute-start | bytes 393224 | tf_op jit(solution)/shard_map/ppermute | solution.py:56
  287.8 6.1 %collective-permute-done.15 = f32[4,8,1024]{2,1,0:T(8,128)S(1)} collective-permute-done((f32[4,8,1024]{2,1,0:T(8,128)S(1)}, f32[4,8,1024]{2,1,0:T(8,128)S(1)}, u32[]{:S(2)}, u32[]{:S(2)}) %collective-permute-start.15) | collective-permute-done | bytes 131104 | tf_op jit(solution)/shard_map/ppermute | solution.py:56
  294.1 5.6 %collective-permute-start.19 = (f32[1,8,1024]{2,1,0:T(8,128)S(1)}, f32[1,8,1024]{2,1,0:T(8,128)S(1)}, u32[]{:S(2)}, u32[]{:S(2)}) collective-permute-start(f32[1,8,1024]{2,1,0:T(8,128)S(1)} %get-tuple-element.66), channel_id=1, source_target_pairs={{0,24},{1,25},{2,26},{3,27},{4,28},{5,29},{6,30},{7,31},{8,16},{9,... | collective-permute-start | bytes 98312 | tf_op jit(solution)/shard_map/ppermute | solution.py:56
  299.7 4.6 %collective-permute-start.18 = (f32[1,8,1024]{2,1,0:T(8,128)S(1)}, f32[1,8,1024]{2,1,0:T(8,128)S(1)}, u32[]{:S(2)}, u32[]{:S(2)}) collective-permute-start(f32[1,8,1024]{2,1,0:T(8,128)S(1)} %get-tuple-element.67), channel_id=1, source_target_pairs={{0,16},{1,17},{2,18},{3,19},{4,20},{5,21},{6,22},{7,23},{8,24},{9,... | collective-permute-start | bytes 98312 | tf_op jit(solution)/shard_map/ppermute | solution.py:56
  304.3 4.4 %collective-permute-start.17 = (f32[1,8,1024]{2,1,0:T(8,128)S(1)}, f32[1,8,1024]{2,1,0:T(8,128)S(1)}, u32[]{:S(2)}, u32[]{:S(2)}) collective-permute-start(f32[1,8,1024]{2,1,0:T(8,128)S(1)} %get-tuple-element.65), channel_id=1, source_target_pairs={{0,8},{1,9},{2,10},{3,11},{4,12},{5,13},{6,14},{7,15},{8,0},{9,1},... | collective-permute-start | bytes 98312 | tf_op jit(solution)/shard_map/ppermute | solution.py:56
  308.7 5.6 %collective-permute-done.17 = f32[1,8,1024]{2,1,0:T(8,128)S(1)} collective-permute-done((f32[1,8,1024]{2,1,0:T(8,128)S(1)}, f32[1,8,1024]{2,1,0:T(8,128)S(1)}, u32[]{:S(2)}, u32[]{:S(2)}) %collective-permute-start.17) | collective-permute-done | bytes 32800 | tf_op jit(solution)/shard_map/ppermute | solution.py:56
  314.3 3.1 collective-permute-start.20
  317.5 4.5 %collective-permute-start.21 = (f32[1,8,1024]{2,1,0:T(8,128)S(1)}, f32[1,8,1024]{2,1,0:T(8,128)S(1)}, u32[]{:S(2)}, u32[]{:S(2)}) collective-permute-start(f32[1,8,1024]{2,1,0:T(8,128)S(1)} %add_add_fusion), channel_id=1, source_target_pairs={{0,256},{32,288},{64,320},{96,352},{128,384},{160,416},{192,448},{... | collective-permute-start | bytes 98312 | tf_op jit(solution)/shard_map/ppermute | solution.py:29
  321.9 4.6 %collective-permute-start.22 = (f32[1,8,1024]{2,1,0:T(8,128)S(1)}, f32[1,8,1024]{2,1,0:T(8,128)S(1)}, u32[]{:S(2)}, u32[]{:S(2)}) collective-permute-start(f32[1,8,1024]{2,1,0:T(8,128)S(1)} %add_add_fusion), channel_id=1, source_target_pairs={{0,128},{32,160},{64,192},{96,224},{128,0},{160,32},{192,64},{224,... | collective-permute-start | bytes 98312 | tf_op jit(solution)/shard_map/ppermute | solution.py:29
  327.3 1.3 collective-permute-done.22
  328.7 3.8 %collective-permute-start.23 = (f32[2,2,1,8,1024]{4,3,1,0,2:T(8,128)S(1)}, f32[2,2,1,8,1024]{4,3,1,0,2:T(8,128)S(1)}, u32[]{:S(2)}, u32[]{:S(2)}) collective-permute-start(f32[2,2,1,8,1024]{4,3,1,0,2:T(8,128)S(1)} %bitcast.512), channel_id=1, source_target_pairs={{0,96},{32,64},{64,32},{96,0},{128,224},{160,192},{192,160},{224,1... | collective-permute-start | bytes 393224 | tf_op jit(solution)/shard_map/ppermute | solution.py:29
  332.5 2.4 collective-permute-start.24
  334.8 3.1 collective-permute-start.25
  338.0 1.0 copy.92
  339.3 2.4 collective-permute-done.25
  341.9 0.7 fusion.89
  (94 shorter events, 9.1 us)
Async XLA Ops:
  7.2 127.6 %copy-start = (bf16[8,512]{1,0:T(8,128)(2,1)S(1)}, bf16[8,512]{1,0:T(8,128)(2,1)}, u32[]{:S(2)}) copy-start(bf16[8,512]{1,0:T(8,128)(2,1)} %param.14) | copy-start | bytes 24580
  7.2 121.6 %all-gather.2.cloned.1.call-start = ((), (), s32[]{:S(2)}) async-start(), calls=%async_computation | async-start | bytes 8650752 | tf_op jit(solution)/shard_map/all_gather | solution.py:93
  137.9 3.5 %copy-start.3 = (bf16[4096,512]{0,1:T(8,128)(2,1)S(1)}, bf16[4096,512]{0,1:T(8,128)(2,1)}, u32[]{:S(2)}) copy-start(bf16[4096,512]{0,1:T(8,128)(2,1)} %get-tuple-element.19) | copy-start | bytes 12582916
  137.9 4.8 %copy-start.13 = (f32[8,1024]{1,0:T(8,128)S(1)}, f32[8,1024]{1,0:T(8,128)}, u32[]{:S(2)}) copy-start(f32[8,1024]{1,0:T(8,128)} %param.13) | copy-start | bytes 98308
  141.4 32.0 %copy-start.7 = (bf16[1,128,2048]{2,1,0:T(8,128)(2,1)S(1)}, bf16[1,128,2048]{2,1,0:T(8,128)(2,1)}, u32[]{:S(2)}) copy-start(bf16[1,128,2048]{2,1,0:T(8,128)(2,1)} %param.9) | copy-start | bytes 1572868
  141.4 32.3 %copy-start.8 = (bf16[1,128,2048]{2,1,0:T(8,128)(2,1)S(1)}, bf16[1,128,2048]{2,1,0:T(8,128)(2,1)}, u32[]{:S(2)}) copy-start(bf16[1,128,2048]{2,1,0:T(8,128)(2,1)} %param.12) | copy-start | bytes 1572868
  142.8 12.8 %collective-permute-start = (f32[1,9,1024]{2,1,0:T(8,128)S(1)}, f32[1,9,1024]{2,1,0:T(8,128)S(1)}, u32[]{:S(2)}, u32[]{:S(2)}) collective-permute-start(f32[1,9,1024]{2,1,0:T(8,128)S(1)} %maximum_bitcast_fusion.1), channel_id=1, source_target_pairs={{0,384},{32,416},{64,448},{96,480},{128,256},{160,288},{192,320},{... | collective-permute-start | bytes 110600 | tf_op jit(solution)/shard_map/ppermute | solution.py:29
  149.4 11.0 %collective-permute-start.1 = (f32[1,9,1024]{2,1,0:T(8,128)S(1)}, f32[1,9,1024]{2,1,0:T(8,128)S(1)}, u32[]{:S(2)}, u32[]{:S(2)}) collective-permute-start(f32[1,9,1024]{2,1,0:T(8,128)S(1)} %maximum_bitcast_fusion.1), channel_id=1, source_target_pairs={{0,256},{32,288},{64,320},{96,352},{128,384},{160,416},{192,448},{... | collective-permute-start | bytes 110600 | tf_op jit(solution)/shard_map/ppermute | solution.py:29
  153.0 9.2 %collective-permute-start.2 = (f32[1,9,1024]{2,1,0:T(8,128)S(1)}, f32[1,9,1024]{2,1,0:T(8,128)S(1)}, u32[]{:S(2)}, u32[]{:S(2)}) collective-permute-start(f32[1,9,1024]{2,1,0:T(8,128)S(1)} %maximum_bitcast_fusion.1), channel_id=1, source_target_pairs={{0,128},{32,160},{64,192},{96,224},{128,0},{160,32},{192,64},{224,... | collective-permute-start | bytes 110600 | tf_op jit(solution)/shard_map/ppermute | solution.py:29
  162.3 12.4 %collective-permute-start.3 = (f32[2,2,1,9,1024]{4,3,1,0,2:T(8,128)S(1)}, f32[2,2,1,9,1024]{4,3,1,0,2:T(8,128)S(1)}, u32[]{:S(2)}, u32[]{:S(2)}) collective-permute-start(f32[2,2,1,9,1024]{4,3,1,0,2:T(8,128)S(1)} %bitcast.502), channel_id=1, source_target_pairs={{0,96},{32,64},{64,32},{96,0},{128,224},{160,192},{192,160},{224,1... | collective-permute-start | bytes 442376 | tf_op jit(solution)/shard_map/ppermute | solution.py:29
  164.6 14.1 %collective-permute-start.4 = (f32[2,2,1,9,1024]{4,3,1,0,2:T(8,128)S(1)}, f32[2,2,1,9,1024]{4,3,1,0,2:T(8,128)S(1)}, u32[]{:S(2)}, u32[]{:S(2)}) collective-permute-start(f32[2,2,1,9,1024]{4,3,1,0,2:T(8,128)S(1)} %bitcast.503), channel_id=1, source_target_pairs={{0,64},{32,96},{64,0},{96,32},{128,192},{160,224},{192,128},{224,1... | collective-permute-start | bytes 442376 | tf_op jit(solution)/shard_map/ppermute | solution.py:29
  169.0 10.4 %collective-permute-start.5 = (f32[2,2,1,9,1024]{4,3,1,0,2:T(8,128)S(1)}, f32[2,2,1,9,1024]{4,3,1,0,2:T(8,128)}, u32[]{:S(2)}, u32[]{:S(2)}) collective-permute-start(f32[2,2,1,9,1024]{4,3,1,0,2:T(8,128)S(1)} %bitcast.504), channel_id=1, source_target_pairs={{0,32},{32,0},{64,96},{96,64},{128,160},{160,128},{192,224},{224,1... | collective-permute-start | bytes 442376 | tf_op jit(solution)/shard_map/ppermute | solution.py:29
  173.2 48.0 %copy-start.4 = (pred[128,2048]{0,1:T(8,128)(4,1)}, pred[128,2048]{0,1:T(8,128)(4,1)S(1)}, u32[]{:S(2)}) copy-start(pred[128,2048]{0,1:T(8,128)(4,1)S(1)} %get-tuple-element.78) | copy-start | bytes 786436
  178.7 0.7 copy-start.10
  181.6 19.8 %collective-permute-start.6 = (bf16[1,8,1024]{2,1,0:T(8,128)(2,1)S(1)}, bf16[1,8,1024]{2,1,0:T(8,128)(2,1)S(1)}, u32[]{:S(2)}, u32[]{:S(2)}) collective-permute-start(bf16[1,8,1024]{2,1,0:T(8,128)(2,1)S(1)} %get-tuple-element.16), channel_id=1, source_target_pairs={{0,24},{1,25},{2,26},{3,27},{4,28},{5,29},{6,30},{7,31},{8,16},{9,... | collective-permute-start | bytes 49160 | tf_op jit(solution)/shard_map/ppermute | solution.py:29
  186.4 15.0 %collective-permute-start.7 = (bf16[1,8,1024]{2,1,0:T(8,128)(2,1)S(1)}, bf16[1,8,1024]{2,1,0:T(8,128)(2,1)S(1)}, u32[]{:S(2)}, u32[]{:S(2)}) collective-permute-start(bf16[1,8,1024]{2,1,0:T(8,128)(2,1)S(1)} %get-tuple-element.16), channel_id=1, source_target_pairs={{0,16},{1,17},{2,18},{3,19},{4,20},{5,21},{6,22},{7,23},{8,24},{9,... | collective-permute-start | bytes 49160 | tf_op jit(solution)/shard_map/ppermute | solution.py:29
  191.0 10.5 %collective-permute-start.8 = (bf16[1,8,1024]{2,1,0:T(8,128)(2,1)S(1)}, bf16[1,8,1024]{2,1,0:T(8,128)(2,1)S(1)}, u32[]{:S(2)}, u32[]{:S(2)}) collective-permute-start(bf16[1,8,1024]{2,1,0:T(8,128)(2,1)S(1)} %get-tuple-element.16), channel_id=1, source_target_pairs={{0,8},{1,9},{2,10},{3,11},{4,12},{5,13},{6,14},{7,15},{8,0},{9,1},... | collective-permute-start | bytes 49160 | tf_op jit(solution)/shard_map/ppermute | solution.py:29
  201.5 17.5 %collective-permute-start.9 = (bf16[2,2,1,8,1024]{4,3,1,0,2:T(8,128)(2,1)S(1)}, bf16[2,2,1,8,1024]{4,3,1,0,2:T(8,128)(2,1)S(1)}, u32[]{:S(2)}, u32[]{:S(2)}) collective-permute-start(bf16[2,2,1,8,1024]{4,3,1,0,2:T(8,128)(2,1)S(1)} %bitcast.518), channel_id=1, source_target_pairs={{0,6},{1,7},{2,4},{3,5},{4,2},{5,3},{6,0},{7,1},{8,14},{9,15},{10,... | collective-permute-start | bytes 196616 | tf_op jit(solution)/shard_map/ppermute | solution.py:29
  205.7 13.3 %collective-permute-start.10 = (bf16[2,2,1,8,1024]{4,3,1,0,2:T(8,128)(2,1)S(1)}, bf16[2,2,1,8,1024]{4,3,1,0,2:T(8,128)(2,1)S(1)}, u32[]{:S(2)}, u32[]{:S(2)}) collective-permute-start(bf16[2,2,1,8,1024]{4,3,1,0,2:T(8,128)(2,1)S(1)} %bitcast.519), channel_id=1, source_target_pairs={{0,4},{1,5},{2,6},{3,7},{4,0},{5,1},{6,2},{7,3},{8,12},{9,13},{10,... | collective-permute-start | bytes 196616 | tf_op jit(solution)/shard_map/ppermute | solution.py:29
  208.2 10.8 %collective-permute-start.11 = (bf16[2,2,1,8,1024]{4,3,1,0,2:T(8,128)(2,1)S(1)}, bf16[2,2,1,8,1024]{4,3,1,0,2:T(8,128)(2,1)S(1)}, u32[]{:S(2)}, u32[]{:S(2)}) collective-permute-start(bf16[2,2,1,8,1024]{4,3,1,0,2:T(8,128)(2,1)S(1)} %bitcast.520), channel_id=1, source_target_pairs={{0,2},{1,3},{2,0},{3,1},{4,6},{5,7},{6,4},{7,5},{8,10},{9,11},{10,... | collective-permute-start | bytes 196616 | tf_op jit(solution)/shard_map/ppermute | solution.py:29
  219.1 9.5 %collective-permute-start.12 = (bf16[2,2,2,2,1,8,1024]{6,5,3,2,1,0,4:T(8,128)(2,1)S(1)}, bf16[2,2,2,2,1,8,1024]{6,5,3,2,1,0,4:T(8,128)(2,1)S(1)}, u32[]{:S(2)}, u32[]{:S(2)}) collective-permute-start(bf16[2,2,2,2,1,8,1024]{6,5,3,2,1,0,4:T(8,128)(2,1)S(1)} %bitcast.506), channel_id=1, source_target_pairs={{0,1},{1,0},{2,3},{3,2},{4,5},{5,4},{6,7},{7,6},{8,9},{9,8},{10,11... | collective-permute-start | bytes 786440 | tf_op jit(solution)/shard_map/ppermute | solution.py:29
  232.1 10.6 %copy-start.2 = (f32[4,2048,128,4]{2,1,3,0:T(8,128)S(1)}, f32[4,2048,128,4]{2,1,3,0:T(8,128)}, u32[]{:S(2)}) copy-start(f32[4,2048,128,4]{2,1,3,0:T(8,128)} %get-tuple-element.86) | copy-start | bytes 50331652
  232.2 10.6 %copy-start.5 = (pred[128,2048]{0,1:T(8,128)(4,1)S(1)}, pred[128,2048]{0,1:T(8,128)(4,1)}, u32[]{:S(2)}) copy-start(pred[128,2048]{0,1:T(8,128)(4,1)} %copy-done.4) | copy-start | bytes 786436
  248.6 8.7 %copy-start.6 = (bf16[2048,512]{0,1:T(8,128)(2,1)S(1)}, bf16[2048,512]{0,1:T(8,128)(2,1)}, u32[]{:S(2)}) copy-start(bf16[2048,512]{0,1:T(8,128)(2,1)} %get-tuple-element.20) | copy-start | bytes 6291460
  257.3 8.2 %copy-start.11 = (bf16[256,512]{0,1:T(8,128)(2,1)S(1)}, bf16[256,512]{0,1:T(8,128)(2,1)}, u32[]{:S(2)}) copy-start(bf16[256,512]{0,1:T(8,128)(2,1)} %copy.82) | copy-start | bytes 786436
  265.6 2.8 copy-start.12
  271.9 66.1 %copy-start.9 = (bf16[128,4,4,128]{0,3,2,1:T(8,128)(2,1)S(1)}, bf16[128,4,4,128]{0,3,2,1:T(8,128)(2,1)}, u32[]{:S(2)}) copy-start(bf16[128,4,4,128]{0,3,2,1:T(8,128)(2,1)} %get-tuple-element.87) | copy-start | bytes 1572868
  273.6 3.9 %collective-permute-start.13 = (f32[16,8,1024]{2,1,0:T(8,128)S(1)}, f32[16,8,1024]{2,1,0:T(8,128)S(1)}, u32[]{:S(2)}, u32[]{:S(2)}) collective-permute-start(f32[16,8,1024]{2,1,0:T(8,128)S(1)} %dynamic-slice_bitcast_fusion), channel_id=1, source_target_pairs={{0,1},{1,0},{2,3},{3,2},{4,5},{5,4},{6,7},{7,6},{8,9},{9,8},{10,11... | collective-permute-start | bytes 1572872 | tf_op jit(solution)/shard_map/ppermute | solution.py:56
  276.0 66.7 %copy-start.1 = (bf16[8,512]{1,0:T(8,128)(2,1)S(1)}, bf16[8,512]{1,0:T(8,128)(2,1)}, u32[]{:S(2)}) copy-start(bf16[8,512]{1,0:T(8,128)(2,1)} %param.14) | copy-start | bytes 24580
  277.6 10.2 %collective-permute-start.16 = (f32[4,8,1024]{2,1,0:T(8,128)S(1)}, f32[4,8,1024]{2,1,0:T(8,128)S(1)}, u32[]{:S(2)}, u32[]{:S(2)}) collective-permute-start(f32[4,8,1024]{2,1,0:T(8,128)S(1)} %get-tuple-element.48), channel_id=1, source_target_pairs={{0,6},{1,7},{2,4},{3,5},{4,2},{5,3},{6,0},{7,1},{8,14},{9,15},{10,... | collective-permute-start | bytes 393224 | tf_op jit(solution)/shard_map/ppermute | solution.py:56
  281.8 12.0 %collective-permute-start.15 = (f32[4,8,1024]{2,1,0:T(8,128)S(1)}, f32[4,8,1024]{2,1,0:T(8,128)S(1)}, u32[]{:S(2)}, u32[]{:S(2)}) collective-permute-start(f32[4,8,1024]{2,1,0:T(8,128)S(1)} %get-tuple-element.49), channel_id=1, source_target_pairs={{0,4},{1,5},{2,6},{3,7},{4,0},{5,1},{6,2},{7,3},{8,12},{9,13},{10,... | collective-permute-start | bytes 393224 | tf_op jit(solution)/shard_map/ppermute | solution.py:56
  283.7 10.3 %collective-permute-start.14 = (f32[4,8,1024]{2,1,0:T(8,128)S(1)}, f32[4,8,1024]{2,1,0:T(8,128)S(1)}, u32[]{:S(2)}, u32[]{:S(2)}) collective-permute-start(f32[4,8,1024]{2,1,0:T(8,128)S(1)} %get-tuple-element.47), channel_id=1, source_target_pairs={{0,2},{1,3},{2,0},{3,1},{4,6},{5,7},{6,4},{7,5},{8,10},{9,11},{10,... | collective-permute-start | bytes 393224 | tf_op jit(solution)/shard_map/ppermute | solution.py:56
  294.1 14.7 %collective-permute-start.19 = (f32[1,8,1024]{2,1,0:T(8,128)S(1)}, f32[1,8,1024]{2,1,0:T(8,128)S(1)}, u32[]{:S(2)}, u32[]{:S(2)}) collective-permute-start(f32[1,8,1024]{2,1,0:T(8,128)S(1)} %get-tuple-element.66), channel_id=1, source_target_pairs={{0,24},{1,25},{2,26},{3,27},{4,28},{5,29},{6,30},{7,31},{8,16},{9,... | collective-permute-start | bytes 98312 | tf_op jit(solution)/shard_map/ppermute | solution.py:56
  299.7 9.0 %collective-permute-start.18 = (f32[1,8,1024]{2,1,0:T(8,128)S(1)}, f32[1,8,1024]{2,1,0:T(8,128)S(1)}, u32[]{:S(2)}, u32[]{:S(2)}) collective-permute-start(f32[1,8,1024]{2,1,0:T(8,128)S(1)} %get-tuple-element.67), channel_id=1, source_target_pairs={{0,16},{1,17},{2,18},{3,19},{4,20},{5,21},{6,22},{7,23},{8,24},{9,... | collective-permute-start | bytes 98312 | tf_op jit(solution)/shard_map/ppermute | solution.py:56
  304.3 10.0 %collective-permute-start.17 = (f32[1,8,1024]{2,1,0:T(8,128)S(1)}, f32[1,8,1024]{2,1,0:T(8,128)S(1)}, u32[]{:S(2)}, u32[]{:S(2)}) collective-permute-start(f32[1,8,1024]{2,1,0:T(8,128)S(1)} %get-tuple-element.65), channel_id=1, source_target_pairs={{0,8},{1,9},{2,10},{3,11},{4,12},{5,13},{6,14},{7,15},{8,0},{9,1},... | collective-permute-start | bytes 98312 | tf_op jit(solution)/shard_map/ppermute | solution.py:56
  314.3 12.2 %collective-permute-start.20 = (f32[1,8,1024]{2,1,0:T(8,128)S(1)}, f32[1,8,1024]{2,1,0:T(8,128)S(1)}, u32[]{:S(2)}, u32[]{:S(2)}) collective-permute-start(f32[1,8,1024]{2,1,0:T(8,128)S(1)} %add_add_fusion), channel_id=1, source_target_pairs={{0,384},{32,416},{64,448},{96,480},{128,256},{160,288},{192,320},{... | collective-permute-start | bytes 98312 | tf_op jit(solution)/shard_map/ppermute | solution.py:29
  317.5 9.8 %collective-permute-start.21 = (f32[1,8,1024]{2,1,0:T(8,128)S(1)}, f32[1,8,1024]{2,1,0:T(8,128)S(1)}, u32[]{:S(2)}, u32[]{:S(2)}) collective-permute-start(f32[1,8,1024]{2,1,0:T(8,128)S(1)} %add_add_fusion), channel_id=1, source_target_pairs={{0,256},{32,288},{64,320},{96,352},{128,384},{160,416},{192,448},{... | collective-permute-start | bytes 98312 | tf_op jit(solution)/shard_map/ppermute | solution.py:29
  321.9 6.7 %collective-permute-start.22 = (f32[1,8,1024]{2,1,0:T(8,128)S(1)}, f32[1,8,1024]{2,1,0:T(8,128)S(1)}, u32[]{:S(2)}, u32[]{:S(2)}) collective-permute-start(f32[1,8,1024]{2,1,0:T(8,128)S(1)} %add_add_fusion), channel_id=1, source_target_pairs={{0,128},{32,160},{64,192},{96,224},{128,0},{160,32},{192,64},{224,... | collective-permute-start | bytes 98312 | tf_op jit(solution)/shard_map/ppermute | solution.py:29
  328.7 10.3 %collective-permute-start.23 = (f32[2,2,1,8,1024]{4,3,1,0,2:T(8,128)S(1)}, f32[2,2,1,8,1024]{4,3,1,0,2:T(8,128)S(1)}, u32[]{:S(2)}, u32[]{:S(2)}) collective-permute-start(f32[2,2,1,8,1024]{4,3,1,0,2:T(8,128)S(1)} %bitcast.512), channel_id=1, source_target_pairs={{0,96},{32,64},{64,32},{96,0},{128,224},{160,192},{192,160},{224,1... | collective-permute-start | bytes 393224 | tf_op jit(solution)/shard_map/ppermute | solution.py:29
  332.5 6.9 %collective-permute-start.24 = (f32[2,2,1,8,1024]{4,3,1,0,2:T(8,128)S(1)}, f32[2,2,1,8,1024]{4,3,1,0,2:T(8,128)S(1)}, u32[]{:S(2)}, u32[]{:S(2)}) collective-permute-start(f32[2,2,1,8,1024]{4,3,1,0,2:T(8,128)S(1)} %bitcast.513), channel_id=1, source_target_pairs={{0,64},{32,96},{64,0},{96,32},{128,192},{160,224},{192,128},{224,1... | collective-permute-start | bytes 393224 | tf_op jit(solution)/shard_map/ppermute | solution.py:29
  334.8 6.9 %collective-permute-start.25 = (f32[2,2,1,8,1024]{4,3,1,0,2:T(8,128)S(1)}, f32[2,2,1,8,1024]{4,3,1,0,2:T(8,128)S(1)}, u32[]{:S(2)}, u32[]{:S(2)}) collective-permute-start(f32[2,2,1,8,1024]{4,3,1,0,2:T(8,128)S(1)} %bitcast.514), channel_id=1, source_target_pairs={{0,32},{32,0},{64,96},{96,64},{128,160},{160,128},{192,224},{224,1... | collective-permute-start | bytes 393224 | tf_op jit(solution)/shard_map/ppermute | solution.py:29
Sparse Core Ops, SparseCore 0:
  11.7 117.0 all-gather.1

commit v2 on v0

--- a/solution.py
+++ b/solution.py
@@ -212,11 +212,21 @@
     )
     local_grad = scattered_sum(grad_slots, "tok", (1, 2, 2))
 
-    all_local = gathered(local_grad, "seg", ((2, 3), (0, 1)))
-    memory_grad = all_local[seg_count - 1]
-    for step in range(seg_count - 2, -1, -1):
-        earlier_grad = all_local[step] + all_decay[step] * memory_grad
-        memory_grad = jnp.where(step >= seg_index, earlier_grad, memory_grad)
+    grad_terms = jnp.concatenate([local_grad, decay_rate[None]], axis=0)
+    distance = 1
+    while distance < seg_count:
+        route = [(i, i - distance) for i in range(distance, seg_count)]
+        arrived = lax.ppermute(grad_terms, "seg", route)
+        own_decay = grad_terms[mem_rows]
+        grad_terms = jnp.concatenate(
+            [
+                grad_terms[:mem_rows] + own_decay * arrived[:mem_rows],
+                (own_decay * arrived[mem_rows])[None],
+            ],
+            axis=0,
+        )
+        distance *= 2
+    memory_grad = grad_terms[:mem_rows]
     return (attended, memory_in[None], memory_grad[None])
 
 

time: 349 us -> 353 us (1.011)
  waiting for transfers between devices: 132 us -> 151 us
  starting transfers between devices: 97.4 us -> 82.8 us
    ppermute x0 -> x4, waiting for transfers between devices: none -> 24 us  [shards(): arrived = lax.ppermute(grad_terms, 'seg', route)]
    ppermute x19 -> x13, starting transfers between devices: 70.2 us -> 48.8 us  [gathered(): lax.ppermute(held, axis, [(i, i ^ flip) for i in range(size)])]
    ppermute x0 -> x4, starting transfers between devices: none -> 6.82 us  [shards(): arrived = lax.ppermute(grad_terms, 'seg', route)]
    ppermute x19 -> x13, waiting for transfers between devices: 11.8 us -> 6.17 us  [gathered(): lax.ppermute(held, axis, [(i, i ^ flip) for i in range(size)])]
  transfers between devices with their start and end apart: 27 -> 25, of which waited for: 13 -> 13; matrix products, arithmetic and copies ran while one was open for 10% -> 10% of each run, Pallas kernels for 0% -> 0%
where the time goes in v2:
time: 353 us; the launch traced here: 352 us
  waiting for transfers between devices  151 us (43%)
  starting transfers between devices  82.8 us (23%)
  matrix products  53.6 us (15%)
  other arithmetic  24.4 us (7%)
  local copies, waits for them, and re-layouts  24.3 us (7%)
  between operations  16 us (5%)
    all_gather x1, waiting for transfers between devices, shards(): lax.all_gather(jnp.concatenate([seg_keys[0], seg_values[0]], axis=1), 'to...  107 us
    ppermute x13, starting transfers between devices, gathered(): lax.ppermute(held, axis, [(i, i ^ flip) for i in range(size)])  48.8 us
    ppermute x7, starting transfers between devices, scattered_sum(): lax.ppermute(send, axis, [(i, i ^ flip) for i in range(size)])  27.1 us
    ppermute x4, waiting for transfers between devices, shards(): arrived = lax.ppermute(grad_terms, 'seg', route)  24 us
    dot_general x4, matrix products, shards(): jnp.einsum('tgjd,ugd->gjtu', queries, key_block, preferred_element_type=j...  21 us
    dot_general x4, matrix products, shards(): jnp.einsum('gjtu,ugd->tgjd', seg_weights, value_block, preferred_element_...  16.5 us
    reduce_sum x4, other arithmetic, softmax_step(): new_total = row_total * multiplier + jnp.sum(weights, axis=-1)  13.4 us
    ppermute x7, waiting for transfers between devices, scattered_sum(): lax.ppermute(send, axis, [(i, i ^ flip) for i in range(size)])  13.2 us
  transfers between devices with their start and end apart: 25, of which 13 were waited for; matrix products, arithmetic and copies ran while one was open for 10% of the time, Pallas kernels for 0%

profile of v2, /device:TPU:2, one launch (start us, length us, event | category | flops | bytes accessed | tf_op | source)
XLA Modules:
  0.0 351.7 jit_solution(13719616127454125462)
XLA Ops:
  10.2 1.2 dynamic_slice.32
  12.1 1.4 reshape_squeeze.3
  13.5 1.3 copy.105
  14.8 1.2 dynamic_slice.31
  19.4 2.1 compare_and_fusion.1
  21.6 107.2 %all-gather.2.cloned.1.call-done = bf16[4096,1024]{0,1:T(8,128)(2,1)} async-done(((bf16[128,1024]{0,1:T(8,128)(2,1)}), bf16[4096,1024]{0,1:T(8,128)(2,1)}) %all-gather.2.cloned.1.call-update) | async-done | bytes 8388624 | tf_op jit(solution)/shard_map/all_gather | solution.py:93
  128.8 6.0 %fusion.176 = (bf16[4096,512]{0,1:T(8,128)(2,1)}, bf16[4096,512]{0,1:T(8,128)(2,1)}) fusion(bf16[4096,1024]{0,1:T(8,128)(2,1)} %all-gather.2.cloned.1.call-done), kind=kLoop, calls=%fused_computation.259 | loop fusion | bytes 16777216 | tf_op jit(solution)/shard_map/slice | solution.py:97
  134.8 3.1 fusion.179
  137.9 3.5 %fusion.80 = f32[8,4,128]{2,0,1:T(8,128)S(1)} fusion(bf16[4096,4,128]{0,2,1:T(8,128)(2,1)} %bitcast.600, bf16[4,8,4096]{2,1,0:T(8,128)(2,1)S(1)} %get-tuple-element.79, f32[8,4]{0,1:T(4,128)S(1)} %bitcast.654), kind=kOutput, calls=%fused_computation.70 | convolution fusion | flops 33558528 | bytes 4472960 | tf_op jit(solution)/shard_map/gru,ugd->rgd/dot_general | solution.py:110
  141.5 3.5 fusion.79
  145.2 6.6 %collective-permute-start = (f32[1,9,1024]{2,1,0:T(8,128)S(1)}, f32[1,9,1024]{2,1,0:T(8,128)S(1)}, u32[]{:S(2)}, u32[]{:S(2)}) collective-permute-start(f32[1,9,1024]{2,1,0:T(8,128)S(1)} %fusion.109), channel_id=1, source_target_pairs={{0,384},{32,416},{64,448},{96,480},{128,256},{160,288},{192,320},{... | collective-permute-start | bytes 110600 | tf_op jit(solution)/shard_map/ppermute | solution.py:29
  151.8 3.5 %collective-permute-start.1 = (f32[1,9,1024]{2,1,0:T(8,128)S(1)}, f32[1,9,1024]{2,1,0:T(8,128)S(1)}, u32[]{:S(2)}, u32[]{:S(2)}) collective-permute-start(f32[1,9,1024]{2,1,0:T(8,128)S(1)} %fusion.109), channel_id=1, source_target_pairs={{0,256},{32,288},{64,320},{96,352},{128,384},{160,416},{192,448},{... | collective-permute-start | bytes 110600 | tf_op jit(solution)/shard_map/ppermute | solution.py:29
  155.3 2.7 collective-permute-start.2
  158.0 2.6 fusion.175
  160.5 2.2 collective-permute-done.1
  162.8 1.8 collective-permute-done.2
  164.6 2.3 collective-permute-start.3
  166.9 4.4 %collective-permute-start.4 = (f32[2,2,1,9,1024]{4,3,1,0,2:T(8,128)S(1)}, f32[2,2,1,9,1024]{4,3,1,0,2:T(8,128)S(1)}, u32[]{:S(2)}, u32[]{:S(2)}) collective-permute-start(f32[2,2,1,9,1024]{4,3,1,0,2:T(8,128)S(1)} %bitcast.618), channel_id=1, source_target_pairs={{0,64},{32,96},{64,0},{96,32},{128,192},{160,224},{192,128},{224,1... | collective-permute-start | bytes 442376 | tf_op jit(solution)/shard_map/ppermute | solution.py:29
  171.4 2.5 collective-permute-start.5
  173.9 5.4 %fusion.4 = (f32[4,4,128]{2,1,0:T(4,128)}, f32[4,1024,128,4]{2,1,3,0:T(8,128)}) fusion(pred[128,1024]{0,1:T(8,128)(4,1)S(1)} %get-tuple-element.75, bf16[1024,4,128,1]{0,2,3,1:T(8,128)(2,1)S(1)} %bitcast.604, bf16[128,4,4,128]{3,2,1,0:T(4,128)(2,1)S(1)} %reshape_squeeze.3), kind=kOutput, calls=%fused_computation.12 | convolution fusion | flops 543160320 | bytes 10100736 | tf_op jit(solution)/shard_map/tgjd,ugd->gjtu/dot_general | solution.py:154
  179.3 1.7 collective-permute-done.4
  182.7 4.9 %collective-permute-start.6 = (bf16[1,8,1024]{2,1,0:T(8,128)(2,1)S(1)}, bf16[1,8,1024]{2,1,0:T(8,128)(2,1)S(1)}, u32[]{:S(2)}, u32[]{:S(2)}) collective-permute-start(bf16[1,8,1024]{2,1,0:T(8,128)(2,1)S(1)} %get-tuple-element.17), channel_id=1, source_target_pairs={{0,24},{1,25},{2,26},{3,27},{4,28},{5,29},{6,30},{7,31},{8,16},{9,... | collective-permute-start | bytes 49160 | tf_op jit(solution)/shard_map/ppermute | solution.py:29
  187.6 4.4 %collective-permute-start.7 = (bf16[1,8,1024]{2,1,0:T(8,128)(2,1)S(1)}, bf16[1,8,1024]{2,1,0:T(8,128)(2,1)S(1)}, u32[]{:S(2)}, u32[]{:S(2)}) collective-permute-start(bf16[1,8,1024]{2,1,0:T(8,128)(2,1)S(1)} %get-tuple-element.17), channel_id=1, source_target_pairs={{0,16},{1,17},{2,18},{3,19},{4,20},{5,21},{6,22},{7,23},{8,24},{9,... | collective-permute-start | bytes 49160 | tf_op jit(solution)/shard_map/ppermute | solution.py:29
  192.0 5.3 %collective-permute-start.8 = (bf16[1,8,1024]{2,1,0:T(8,128)(2,1)S(1)}, bf16[1,8,1024]{2,1,0:T(8,128)(2,1)S(1)}, u32[]{:S(2)}, u32[]{:S(2)}) collective-permute-start(bf16[1,8,1024]{2,1,0:T(8,128)(2,1)S(1)} %get-tuple-element.17), channel_id=1, source_target_pairs={{0,8},{1,9},{2,10},{3,11},{4,12},{5,13},{6,14},{7,15},{8,0},{9,1},... | collective-permute-start | bytes 49160 | tf_op jit(solution)/shard_map/ppermute | solution.py:29
  197.3 5.4 %fusion.3 = (f32[4,4,128]{2,1,0:T(4,128)}, f32[4,1024,128,4]{2,1,3,0:T(8,128)}) fusion(pred[128,1024]{0,1:T(8,128)(4,1)S(1)} %get-tuple-element.74, bf16[1024,4,128,1]{0,2,3,1:T(8,128)(2,1)S(1)} %bitcast.603, bf16[128,4,4,128]{3,2,1,0:T(4,128)(2,1)S(1)} %reshape_squeeze.3), kind=kOutput, calls=%fused_computation.11 | convolution fusion | flops 543160320 | bytes 10100736 | tf_op jit(solution)/shard_map/tgjd,ugd->gjtu/dot_general | solution.py:154
  202.8 4.0 %collective-permute-start.9 = (bf16[2,2,1,8,1024]{4,3,1,0,2:T(8,128)(2,1)S(1)}, bf16[2,2,1,8,1024]{4,3,1,0,2:T(8,128)(2,1)S(1)}, u32[]{:S(2)}, u32[]{:S(2)}) collective-permute-start(bf16[2,2,1,8,1024]{4,3,1,0,2:T(8,128)(2,1)S(1)} %bitcast.629), channel_id=1, source_target_pairs={{0,6},{1,7},{2,4},{3,5},{4,2},{5,3},{6,0},{7,1},{8,14},{9,15},{10,... | collective-permute-start | bytes 196616 | tf_op jit(solution)/shard_map/ppermute | solution.py:29
  206.8 2.7 collective-permute-start.10
  209.6 3.3 collective-permute-start.11
  212.9 5.4 %fusion.2 = (f32[4,4,128]{2,1,0:T(4,128)}, f32[4,1024,128,4]{2,1,3,0:T(8,128)}) fusion(pred[128,1024]{0,1:T(8,128)(4,1)S(1)} %get-tuple-element.76, bf16[1024,4,128,1]{0,2,3,1:T(8,128)(2,1)S(1)} %bitcast.602, bf16[128,4,4,128]{3,2,1,0:T(4,128)(2,1)S(1)} %reshape_squeeze.3), kind=kOutput, calls=%fused_computation.10 | convolution fusion | flops 543160320 | bytes 10100736 | tf_op jit(solution)/shard_map/tgjd,ugd->gjtu/dot_general | solution.py:154
  218.4 2.1 collective-permute-start.12
  220.6 4.8 %fusion.1 = (f32[4,4,128]{2,1,0:T(4,128)S(1)}, f32[4,1024,128,4]{2,1,3,0:T(8,128)}) fusion(pred[128,1024]{0,1:T(8,128)(4,1)S(1)} %copy-done.3, bf16[1024,4,128,1]{0,2,3,1:T(8,128)(2,1)S(1)} %bitcast.601, bf16[128,4,4,128]{3,2,1,0:T(4,128)(2,1)S(1)} %reshape_squeeze.3), kind=kOutput, calls=%fused_computation.9 | convolution fusion | flops 543160320 | bytes 10100736 | tf_op jit(solution)/shard_map/tgjd,ugd->gjtu/dot_general | solution.py:154
  227.1 1.5 bitcast_reduce_fusion
  229.7 4.6 %fusion.11 = f32[4,4,128]{2,1,0:T(4,128)S(1)} fusion(f32[4,1024,128,4]{2,1,3,0:T(8,128)} %get-tuple-element.83, f32[4,4,128]{2,1,0:T(4,128)S(1)} %get-tuple-element.14, pred[128,1024]{0,1:T(8,128)(4,1)S(1)} %get-tuple-element.75), kind=kLoop, calls=%fused_computation.19 | loop fusion | flops 10483712 | bytes 8536064 | tf_op jit(solution)/shard_map/reduce_sum | solution.py:73
  234.3 4.8 %fusion.9 = f32[4,4,128]{2,1,0:T(4,128)S(1)} fusion(f32[4,1024,128,4]{2,1,3,0:T(8,128)} %get-tuple-element.85, f32[4,4,128]{2,1,0:T(4,128)S(1)} %get-tuple-element.15, pred[128,1024]{0,1:T(8,128)(4,1)S(1)} %get-tuple-element.74), kind=kLoop, calls=%fused_computation.17 | loop fusion | flops 10483712 | bytes 8536064 | tf_op jit(solution)/shard_map/reduce_sum | solution.py:73
  239.5 2.0 fusion.7
  241.5 2.0 fusion.5
  244.8 1.8 copy.60
  246.7 5.9 %fusion.64 = f32[128,4,4,128]{0,3,2,1:T(8,128)S(1)} fusion(bf16[1024,4,128,1]{0,2,3,1:T(8,128)(2,1)} %bitcast.616, f32[4,1024,128,4]{2,1,3,0:T(8,128)} %get-tuple-element.89, f32[4,4,128]{2,1,0:T(4,128)} %copy-done.25, pred[128,1024]{0,1:T(8,128)(4,1)} %get-tuple-element.77, f32[128,4,4]{0,2,1:T(4,128)} %get-tuple-element.69, ...), kind=kOutput, calls=%fused_computation.59 | convolution fusion | flops 547880960 | bytes 10641408 | tf_op jit(solution)/shard_map/gjtu,ugd->tgjd/dot_general | solution.py:160
  252.6 5.7 %fusion.67 = f32[128,4,4,128]{0,3,2,1:T(8,128)S(1)} fusion(f32[128,4,4,128]{0,3,2,1:T(8,128)S(1)} %fusion.64, bf16[1024,4,128,1]{0,2,3,1:T(8,128)(2,1)S(1)} %bitcast.615, f32[4,1024,128,4]{2,1,3,0:T(8,128)} %get-tuple-element.87, f32[4,4,128]{2,1,0:T(4,128)S(1)} %copy-done.22, pred[128,1024]{0,1:T(8,128)(4,1)S(1)} %get-tuple-element.76, ...), kind=kOutput, calls=%fused_computation.60 | convolution fusion | flops 547880960 | bytes 11681792 | tf_op jit(solution)/shard_map/gjtu,ugd->tgjd/dot_general | solution.py:160
  258.4 2.4 fusion.70
  260.9 2.6 fusion.73
  263.6 1.4 fusion.180
  265.2 1.3 convolution_bitcast_fusion.1
  266.4 1.8 fusion.78
  268.2 1.4 copy.64
  269.9 1.3 copy.66
  271.5 2.4 collective-permute-start.13
  274.0 1.5 collective-permute-done.13
  275.6 4.0 %collective-permute-start.16 = (f32[4,8,1024]{2,1,0:T(8,128)S(1)}, f32[4,8,1024]{2,1,0:T(8,128)S(1)}, u32[]{:S(2)}, u32[]{:S(2)}) collective-permute-start(f32[4,8,1024]{2,1,0:T(8,128)S(1)} %get-tuple-element.49), channel_id=1, source_target_pairs={{0,6},{1,7},{2,4},{3,5},{4,2},{5,3},{6,0},{7,1},{8,14},{9,15},{10,... | collective-permute-start | bytes 393224 | tf_op jit(solution)/shard_map/ppermute | solution.py:56
  279.6 1.9 collective-permute-start.15
  281.6 4.2 %collective-permute-start.14 = (f32[4,8,1024]{2,1,0:T(8,128)S(1)}, f32[4,8,1024]{2,1,0:T(8,128)S(1)}, u32[]{:S(2)}, u32[]{:S(2)}) collective-permute-start(f32[4,8,1024]{2,1,0:T(8,128)S(1)} %get-tuple-element.48), channel_id=1, source_target_pairs={{0,2},{1,3},{2,0},{3,1},{4,6},{5,7},{6,4},{7,5},{8,10},{9,11},{10,... | collective-permute-start | bytes 393224 | tf_op jit(solution)/shard_map/ppermute | solution.py:56
  285.8 6.1 %collective-permute-done.15 = f32[4,8,1024]{2,1,0:T(8,128)S(1)} collective-permute-done((f32[4,8,1024]{2,1,0:T(8,128)S(1)}, f32[4,8,1024]{2,1,0:T(8,128)S(1)}, u32[]{:S(2)}, u32[]{:S(2)}) %collective-permute-start.15) | collective-permute-done | bytes 131104 | tf_op jit(solution)/shard_map/ppermute | solution.py:56
  292.1 5.8 %collective-permute-start.19 = (f32[1,8,1024]{2,1,0:T(8,128)S(1)}, f32[1,8,1024]{2,1,0:T(8,128)S(1)}, u32[]{:S(2)}, u32[]{:S(2)}) collective-permute-start(f32[1,8,1024]{2,1,0:T(8,128)S(1)} %get-tuple-element.63), channel_id=1, source_target_pairs={{0,24},{1,25},{2,26},{3,27},{4,28},{5,29},{6,30},{7,31},{8,16},{9,... | collective-permute-start | bytes 98312 | tf_op jit(solution)/shard_map/ppermute | solution.py:56
  297.9 4.4 %collective-permute-start.18 = (f32[1,8,1024]{2,1,0:T(8,128)S(1)}, f32[1,8,1024]{2,1,0:T(8,128)S(1)}, u32[]{:S(2)}, u32[]{:S(2)}) collective-permute-start(f32[1,8,1024]{2,1,0:T(8,128)S(1)} %get-tuple-element.64), channel_id=1, source_target_pairs={{0,16},{1,17},{2,18},{3,19},{4,20},{5,21},{6,22},{7,23},{8,24},{9,... | collective-permute-start | bytes 98312 | tf_op jit(solution)/shard_map/ppermute | solution.py:56
  302.3 4.4 %collective-permute-start.17 = (f32[1,8,1024]{2,1,0:T(8,128)S(1)}, f32[1,8,1024]{2,1,0:T(8,128)S(1)}, u32[]{:S(2)}, u32[]{:S(2)}) collective-permute-start(f32[1,8,1024]{2,1,0:T(8,128)S(1)} %get-tuple-element.62), channel_id=1, source_target_pairs={{0,8},{1,9},{2,10},{3,11},{4,12},{5,13},{6,14},{7,15},{8,0},{9,1},... | collective-permute-start | bytes 98312 | tf_op jit(solution)/shard_map/ppermute | solution.py:56
  306.7 5.4 %collective-permute-done.17 = f32[1,8,1024]{2,1,0:T(8,128)S(1)} collective-permute-done((f32[1,8,1024]{2,1,0:T(8,128)S(1)}, f32[1,8,1024]{2,1,0:T(8,128)S(1)}, u32[]{:S(2)}, u32[]{:S(2)}) %collective-permute-start.17) | collective-permute-done | bytes 32800 | tf_op jit(solution)/shard_map/ppermute | solution.py:56
  312.2 2.9 collective-permute-start.20
  315.2 4.3 %collective-permute-done.20 = f32[9,1024]{1,0:T(8,128)S(1)} collective-permute-done((f32[9,1024]{1,0:T(8,128)S(1)}, f32[9,1024]{1,0:T(8,128)S(1)}, u32[]{:S(2)}, u32[]{:S(2)}) %collective-permute-start.20) | collective-permute-done | bytes 36896 | tf_op jit(solution)/shard_map/ppermute | solution.py:219
  319.5 1.3 collective-permute-start.21
  320.8 5.6 %collective-permute-done.21 = f32[9,1024]{1,0:T(8,128)S(1)} collective-permute-done((f32[9,1024]{1,0:T(8,128)S(1)}, f32[9,1024]{1,0:T(8,128)S(1)}, u32[]{:S(2)}, u32[]{:S(2)}) %collective-permute-start.21) | collective-permute-done | bytes 36896 | tf_op jit(solution)/shard_map/ppermute | solution.py:219
  326.4 1.3 collective-permute-start.22
  327.7 6.5 %collective-permute-done.22 = f32[9,1024]{1,0:T(8,128)S(1)} collective-permute-done((f32[9,1024]{1,0:T(8,128)S(1)}, f32[9,1024]{1,0:T(8,128)S(1)}, u32[]{:S(2)}, u32[]{:S(2)}) %collective-permute-start.22) | collective-permute-done | bytes 36896 | tf_op jit(solution)/shard_map/ppermute | solution.py:219
  334.2 1.3 collective-permute-start.23
  336.5 7.7 %collective-permute-done.23 = f32[9,1024]{1,0:T(8,128)S(1)} collective-permute-done((f32[9,1024]{1,0:T(8,128)S(1)}, f32[9,1024]{1,0:T(8,128)S(1)}, u32[]{:S(2)}, u32[]{:S(2)}) %collective-permute-start.23) | collective-permute-done | bytes 36896 | tf_op jit(solution)/shard_map/ppermute | solution.py:219
  (155 shorter events, 15.6 us)
Async XLA Ops:
  7.2 127.7 %copy-start = (bf16[8,512]{1,0:T(8,128)(2,1)S(1)}, bf16[8,512]{1,0:T(8,128)(2,1)}, u32[]{:S(2)}) copy-start(bf16[8,512]{1,0:T(8,128)(2,1)} %param.14) | copy-start | bytes 24580
  7.2 121.6 %all-gather.2.cloned.1.call-start = ((), (), s32[]{:S(2)}) async-start(), calls=%async_computation | async-start | bytes 8650752 | tf_op jit(solution)/shard_map/all_gather | solution.py:93
  134.8 10.2 %copy-start.10 = (f32[8,1024]{1,0:T(8,128)S(1)}, f32[8,1024]{1,0:T(8,128)}, u32[]{:S(2)}) copy-start(f32[8,1024]{1,0:T(8,128)} %param.13) | copy-start | bytes 98308
  137.9 20.0 %copy-start.2 = (bf16[4096,1024]{0,1:T(8,128)(2,1)S(1)}, bf16[4096,1024]{0,1:T(8,128)(2,1)}, u32[]{:S(2)}) copy-start(bf16[4096,1024]{0,1:T(8,128)(2,1)} %all-gather.2.cloned.1.call-done) | copy-start | bytes 25165828
  145.2 15.4 %collective-permute-start = (f32[1,9,1024]{2,1,0:T(8,128)S(1)}, f32[1,9,1024]{2,1,0:T(8,128)S(1)}, u32[]{:S(2)}, u32[]{:S(2)}) collective-permute-start(f32[1,9,1024]{2,1,0:T(8,128)S(1)} %fusion.109), channel_id=1, source_target_pairs={{0,384},{32,416},{64,448},{96,480},{128,256},{160,288},{192,320},{... | collective-permute-start | bytes 110600 | tf_op jit(solution)/shard_map/ppermute | solution.py:29
  151.8 11.0 %collective-permute-start.1 = (f32[1,9,1024]{2,1,0:T(8,128)S(1)}, f32[1,9,1024]{2,1,0:T(8,128)S(1)}, u32[]{:S(2)}, u32[]{:S(2)}) collective-permute-start(f32[1,9,1024]{2,1,0:T(8,128)S(1)} %fusion.109), channel_id=1, source_target_pairs={{0,256},{32,288},{64,320},{96,352},{128,384},{160,416},{192,448},{... | collective-permute-start | bytes 110600 | tf_op jit(solution)/shard_map/ppermute | solution.py:29
  155.3 9.2 %collective-permute-start.2 = (f32[1,9,1024]{2,1,0:T(8,128)S(1)}, f32[1,9,1024]{2,1,0:T(8,128)S(1)}, u32[]{:S(2)}, u32[]{:S(2)}) collective-permute-start(f32[1,9,1024]{2,1,0:T(8,128)S(1)} %fusion.109), channel_id=1, source_target_pairs={{0,128},{32,160},{64,192},{96,224},{128,0},{160,32},{192,64},{224,... | collective-permute-start | bytes 110600 | tf_op jit(solution)/shard_map/ppermute | solution.py:29
  164.6 14.7 %collective-permute-start.3 = (f32[2,2,1,9,1024]{4,3,1,0,2:T(8,128)S(1)}, f32[2,2,1,9,1024]{4,3,1,0,2:T(8,128)S(1)}, u32[]{:S(2)}, u32[]{:S(2)}) collective-permute-start(f32[2,2,1,9,1024]{4,3,1,0,2:T(8,128)S(1)} %bitcast.617), channel_id=1, source_target_pairs={{0,96},{32,64},{64,32},{96,0},{128,224},{160,192},{192,160},{224,1... | collective-permute-start | bytes 442376 | tf_op jit(solution)/shard_map/ppermute | solution.py:29
  166.9 14.1 %collective-permute-start.4 = (f32[2,2,1,9,1024]{4,3,1,0,2:T(8,128)S(1)}, f32[2,2,1,9,1024]{4,3,1,0,2:T(8,128)S(1)}, u32[]{:S(2)}, u32[]{:S(2)}) collective-permute-start(f32[2,2,1,9,1024]{4,3,1,0,2:T(8,128)S(1)} %bitcast.618), channel_id=1, source_target_pairs={{0,64},{32,96},{64,0},{96,32},{128,192},{160,224},{192,128},{224,1... | collective-permute-start | bytes 442376 | tf_op jit(solution)/shard_map/ppermute | solution.py:29
  171.4 10.1 %collective-permute-start.5 = (f32[2,2,1,9,1024]{4,3,1,0,2:T(8,128)S(1)}, f32[2,2,1,9,1024]{4,3,1,0,2:T(8,128)S(1)}, u32[]{:S(2)}, u32[]{:S(2)}) collective-permute-start(f32[2,2,1,9,1024]{4,3,1,0,2:T(8,128)S(1)} %bitcast.619), channel_id=1, source_target_pairs={{0,32},{32,0},{64,96},{96,64},{128,160},{160,128},{192,224},{224,1... | collective-permute-start | bytes 442376 | tf_op jit(solution)/shard_map/ppermute | solution.py:29
  173.9 8.1 %copy-start.11 = (f32[8,1024]{1,0:T(8,128)S(1)}, f32[8,1024]{1,0:T(8,128)}, u32[]{:S(2)}) copy-start(f32[8,1024]{1,0:T(8,128)} %param.13) | copy-start | bytes 98308
  182.7 20.0 %collective-permute-start.6 = (bf16[1,8,1024]{2,1,0:T(8,128)(2,1)S(1)}, bf16[1,8,1024]{2,1,0:T(8,128)(2,1)S(1)}, u32[]{:S(2)}, u32[]{:S(2)}) collective-permute-start(bf16[1,8,1024]{2,1,0:T(8,128)(2,1)S(1)} %get-tuple-element.17), channel_id=1, source_target_pairs={{0,24},{1,25},{2,26},{3,27},{4,28},{5,29},{6,30},{7,31},{8,16},{9,... | collective-permute-start | bytes 49160 | tf_op jit(solution)/shard_map/ppermute | solution.py:29
  187.6 15.1 %collective-permute-start.7 = (bf16[1,8,1024]{2,1,0:T(8,128)(2,1)S(1)}, bf16[1,8,1024]{2,1,0:T(8,128)(2,1)S(1)}, u32[]{:S(2)}, u32[]{:S(2)}) collective-permute-start(bf16[1,8,1024]{2,1,0:T(8,128)(2,1)S(1)} %get-tuple-element.17), channel_id=1, source_target_pairs={{0,16},{1,17},{2,18},{3,19},{4,20},{5,21},{6,22},{7,23},{8,24},{9,... | collective-permute-start | bytes 49160 | tf_op jit(solution)/shard_map/ppermute | solution.py:29
  192.0 10.7 %collective-permute-start.8 = (bf16[1,8,1024]{2,1,0:T(8,128)(2,1)S(1)}, bf16[1,8,1024]{2,1,0:T(8,128)(2,1)S(1)}, u32[]{:S(2)}, u32[]{:S(2)}) collective-permute-start(bf16[1,8,1024]{2,1,0:T(8,128)(2,1)S(1)} %get-tuple-element.17), channel_id=1, source_target_pairs={{0,8},{1,9},{2,10},{3,11},{4,12},{5,13},{6,14},{7,15},{8,0},{9,1},... | collective-permute-start | bytes 49160 | tf_op jit(solution)/shard_map/ppermute | solution.py:29
  202.7 17.8 %copy-start.3 = (pred[128,1024]{0,1:T(8,128)(4,1)S(1)}, pred[128,1024]{0,1:T(8,128)(4,1)}, u32[]{:S(2)}) copy-start(pred[128,1024]{0,1:T(8,128)(4,1)} %get-tuple-element.77) | copy-start | bytes 393220
  202.8 15.6 %collective-permute-start.9 = (bf16[2,2,1,8,1024]{4,3,1,0,2:T(8,128)(2,1)S(1)}, bf16[2,2,1,8,1024]{4,3,1,0,2:T(8,128)(2,1)S(1)}, u32[]{:S(2)}, u32[]{:S(2)}) collective-permute-start(bf16[2,2,1,8,1024]{4,3,1,0,2:T(8,128)(2,1)S(1)} %bitcast.629), channel_id=1, source_target_pairs={{0,6},{1,7},{2,4},{3,5},{4,2},{5,3},{6,0},{7,1},{8,14},{9,15},{10,... | collective-permute-start | bytes 196616 | tf_op jit(solution)/shard_map/ppermute | solution.py:29
  206.8 11.5 %collective-permute-start.10 = (bf16[2,2,1,8,1024]{4,3,1,0,2:T(8,128)(2,1)S(1)}, bf16[2,2,1,8,1024]{4,3,1,0,2:T(8,128)(2,1)S(1)}, u32[]{:S(2)}, u32[]{:S(2)}) collective-permute-start(bf16[2,2,1,8,1024]{4,3,1,0,2:T(8,128)(2,1)S(1)} %bitcast.630), channel_id=1, source_target_pairs={{0,4},{1,5},{2,6},{3,7},{4,0},{5,1},{6,2},{7,3},{8,12},{9,13},{10,... | collective-permute-start | bytes 196616 | tf_op jit(solution)/shard_map/ppermute | solution.py:29
  209.6 8.8 %collective-permute-start.11 = (bf16[2,2,1,8,1024]{4,3,1,0,2:T(8,128)(2,1)S(1)}, bf16[2,2,1,8,1024]{4,3,1,0,2:T(8,128)(2,1)S(1)}, u32[]{:S(2)}, u32[]{:S(2)}) collective-permute-start(bf16[2,2,1,8,1024]{4,3,1,0,2:T(8,128)(2,1)S(1)} %bitcast.631), channel_id=1, source_target_pairs={{0,2},{1,3},{2,0},{3,1},{4,6},{5,7},{6,4},{7,5},{8,10},{9,11},{10,... | collective-permute-start | bytes 196616 | tf_op jit(solution)/shard_map/ppermute | solution.py:29
  218.4 6.9 %collective-permute-start.12 = (bf16[2,2,2,2,1,8,1024]{6,5,3,2,1,0,4:T(8,128)(2,1)S(1)}, bf16[2,2,2,2,1,8,1024]{6,5,3,2,1,0,4:T(8,128)(2,1)S(1)}, u32[]{:S(2)}, u32[]{:S(2)}) collective-permute-start(bf16[2,2,2,2,1,8,1024]{6,5,3,2,1,0,4:T(8,128)(2,1)S(1)} %bitcast.621), channel_id=1, source_target_pairs={{0,1},{1,0},{2,3},{3,2},{4,5},{5,4},{6,7},{7,6},{8,9},{9,8},{10,11... | collective-permute-start | bytes 786440 | tf_op jit(solution)/shard_map/ppermute | solution.py:29
  229.3 12.2 %copy-start.25 = (f32[4,4,128]{2,1,0:T(4,128)}, f32[4,4,128]{2,1,0:T(4,128)S(1)}, u32[]{:S(2)}) copy-start(f32[4,4,128]{2,1,0:T(4,128)S(1)} %get-tuple-element.71) | copy-start | bytes 24580
  229.3 14.9 %copy-start.15 = (f32[4,4,128]{2,1,0:T(4,128)}, f32[4,4,128]{2,1,0:T(4,128)S(1)}, u32[]{:S(2)}) copy-start(f32[4,4,128]{2,1,0:T(4,128)S(1)} %get-tuple-element.13) | copy-start | bytes 24580
  229.3 14.9 %copy-start.17 = (f32[4,4,128]{2,1,0:T(4,128)}, f32[4,4,128]{2,1,0:T(4,128)S(1)}, u32[]{:S(2)}) copy-start(f32[4,4,128]{2,1,0:T(4,128)S(1)} %get-tuple-element.14) | copy-start | bytes 24580
  229.3 14.9 %copy-start.19 = (f32[4,4,128]{2,1,0:T(4,128)}, f32[4,4,128]{2,1,0:T(4,128)S(1)}, u32[]{:S(2)}) copy-start(f32[4,4,128]{2,1,0:T(4,128)S(1)} %get-tuple-element.15) | copy-start | bytes 24580
  229.3 14.9 %copy-start.21 = (f32[4,4,128]{2,1,0:T(4,128)}, f32[4,4,128]{2,1,0:T(4,128)S(1)}, u32[]{:S(2)}) copy-start(f32[4,4,128]{2,1,0:T(4,128)S(1)} %get-tuple-element.16) | copy-start | bytes 24580
  229.7 9.4 %slice-start.4 = ((s8[8388608]{0:T(1024)(128)(4,1)}), s8[4194304]{0:T(1024)(128)(4,1)S(1)}, s32[]{:S(2)}) async-start(s8[8388608]{0:T(1024)(128)(4,1)} %bitcast.594), calls=%async_computation.5 | async-start | bytes 8388608
  229.7 11.8 %slice-start.6 = ((s8[8388608]{0:T(1024)(128)(4,1)}), s8[4194304]{0:T(1024)(128)(4,1)S(1)}, s32[]{:S(2)}) async-start(s8[8388608]{0:T(1024)(128)(4,1)} %bitcast.596), calls=%async_computation.7 | async-start | bytes 8388608
  234.3 5.1 %slice-start.5 = ((s8[8388608]{0:T(1024)(128)(4,1)}), s8[4194304]{0:T(1024)(128)(4,1)S(1)}, s32[]{:S(2)}) async-start(s8[8388608]{0:T(1024)(128)(4,1)} %bitcast.594), calls=%async_computation.6 | async-start | bytes 8388608
  234.3 7.2 %slice-start.7 = ((s8[8388608]{0:T(1024)(128)(4,1)}), s8[4194304]{0:T(1024)(128)(4,1)S(1)}, s32[]{:S(2)}) async-start(s8[8388608]{0:T(1024)(128)(4,1)} %bitcast.596), calls=%async_computation.8 | async-start | bytes 8388608
  234.3 7.2 %copy-start.4 = (pred[128,1024]{0,1:T(8,128)(4,1)S(1)}, pred[128,1024]{0,1:T(8,128)(4,1)}, u32[]{:S(2)}) copy-start(pred[128,1024]{0,1:T(8,128)(4,1)} %get-tuple-element.77) | copy-start | bytes 393220
  239.5 4.1 %copy-start.12 = (f32[4,4,128]{2,1,0:T(4,128)S(1)}, f32[4,4,128]{2,1,0:T(4,128)}, u32[]{:S(2)}) copy-start(f32[4,4,128]{2,1,0:T(4,128)} %get-tuple-element.82) | copy-start | bytes 24580
  239.5 4.1 %copy-start.13 = (f32[4,4,128]{2,1,0:T(4,128)S(1)}, f32[4,4,128]{2,1,0:T(4,128)}, u32[]{:S(2)}) copy-start(f32[4,4,128]{2,1,0:T(4,128)} %get-tuple-element.84) | copy-start | bytes 24580
  239.5 4.1 %copy-start.14 = (f32[4,4,128]{2,1,0:T(4,128)S(1)}, f32[4,4,128]{2,1,0:T(4,128)}, u32[]{:S(2)}) copy-start(f32[4,4,128]{2,1,0:T(4,128)} %get-tuple-element.86) | copy-start | bytes 24580
  246.6 5.9 %copy-start.7 = (bf16[1024,512]{0,1:T(8,128)(2,1)S(1)}, bf16[1024,512]{0,1:T(8,128)(2,1)}, u32[]{:S(2)}) copy-start(bf16[1024,512]{0,1:T(8,128)(2,1)} %get-tuple-element.23) | copy-start | bytes 3145732
  246.6 5.9 %copy-start.22 = (f32[4,4,128]{2,1,0:T(4,128)S(1)}, f32[4,4,128]{2,1,0:T(4,128)}, u32[]{:S(2)}) copy-start(f32[4,4,128]{2,1,0:T(4,128)} %copy-done.21) | copy-start | bytes 24580
  246.6 5.9 %copy-start.29 = (f32[128,4,4]{0,2,1:T(4,128)S(1)}, f32[128,4,4]{0,2,1:T(4,128)}, u32[]{:S(2)}) copy-start(f32[128,4,4]{0,2,1:T(4,128)} %get-tuple-element.12) | copy-start | bytes 24580
  246.6 11.7 %slice-start.2 = ((s8[8388608]{0:T(1024)(128)(4,1)}), s8[4194304]{0:T(1024)(128)(4,1)S(1)}, s32[]{:S(2)}) async-start(s8[8388608]{0:T(1024)(128)(4,1)} %bitcast.592), calls=%async_computation.3 | async-start | bytes 8388608
  252.6 5.8 %slice-start.3 = ((s8[8388608]{0:T(1024)(128)(4,1)}), s8[4194304]{0:T(1024)(128)(4,1)S(1)}, s32[]{:S(2)}) async-start(s8[8388608]{0:T(1024)(128)(4,1)} %bitcast.592), calls=%async_computation.4 | async-start | bytes 8388608
  252.6 5.8 %copy-start.6 = (bf16[1024,512]{0,1:T(8,128)(2,1)S(1)}, bf16[1024,512]{0,1:T(8,128)(2,1)}, u32[]{:S(2)}) copy-start(bf16[1024,512]{0,1:T(8,128)(2,1)} %get-tuple-element.21) | copy-start | bytes 3145732
  252.6 5.8 %copy-start.20 = (f32[4,4,128]{2,1,0:T(4,128)S(1)}, f32[4,4,128]{2,1,0:T(4,128)}, u32[]{:S(2)}) copy-start(f32[4,4,128]{2,1,0:T(4,128)} %copy-done.19) | copy-start | bytes 24580
  252.6 5.8 %copy-start.28 = (f32[128,4,4]{0,2,1:T(4,128)S(1)}, f32[128,4,4]{0,2,1:T(4,128)}, u32[]{:S(2)}) copy-start(f32[128,4,4]{0,2,1:T(4,128)} %get-tuple-element.11) | copy-start | bytes 24580
  252.6 8.2 %slice-start = ((s8[8388608]{0:T(1024)(128)(4,1)}), s8[4194304]{0:T(1024)(128)(4,1)S(1)}, s32[]{:S(2)}) async-start(s8[8388608]{0:T(1024)(128)(4,1)} %bitcast.590), calls=%async_computation.1 | async-start | bytes 8388608
  258.4 2.4 slice-start.1
  258.4 2.5 copy-start.5
  258.4 2.5 copy-start.18
  258.4 2.5 copy-start.27
  260.9 2.6 copy-start.9
  260.9 2.6 copy-start.16
  260.9 2.6 copy-start.26
  260.9 4.2 %copy-start.23 = (f32[4,4,128]{2,1,0:T(4,128)S(1)}, f32[4,4,128]{2,1,0:T(4,128)}, u32[]{:S(2)}) copy-start(f32[4,4,128]{2,1,0:T(4,128)} %log_add_fusion) | copy-start | bytes 24580
  263.5 2.9 copy-start.24
  265.1 79.7 %copy-start.1 = (bf16[8,512]{1,0:T(8,128)(2,1)S(1)}, bf16[8,512]{1,0:T(8,128)(2,1)}, u32[]{:S(2)}) copy-start(bf16[8,512]{1,0:T(8,128)(2,1)} %param.14) | copy-start | bytes 24580
  268.2 67.2 %copy-start.8 = (bf16[128,4,4,128]{0,3,2,1:T(8,128)(2,1)S(1)}, bf16[128,4,4,128]{0,3,2,1:T(8,128)(2,1)}, u32[]{:S(2)}) copy-start(bf16[128,4,4,128]{0,3,2,1:T(8,128)(2,1)} %get-tuple-element.90) | copy-start | bytes 1572868
  271.5 3.9 %collective-permute-start.13 = (f32[16,8,1024]{2,1,0:T(8,128)S(1)}, f32[16,8,1024]{2,1,0:T(8,128)S(1)}, u32[]{:S(2)}, u32[]{:S(2)}) collective-permute-start(f32[16,8,1024]{2,1,0:T(8,128)S(1)} %dynamic-slice_bitcast_fusion), channel_id=1, source_target_pairs={{0,1},{1,0},{2,3},{3,2},{4,5},{5,4},{6,7},{7,6},{8,9},{9,8},{10,11... | collective-permute-start | bytes 1572872 | tf_op jit(solution)/shard_map/ppermute | solution.py:56
  275.6 10.2 %collective-permute-start.16 = (f32[4,8,1024]{2,1,0:T(8,128)S(1)}, f32[4,8,1024]{2,1,0:T(8,128)S(1)}, u32[]{:S(2)}, u32[]{:S(2)}) collective-permute-start(f32[4,8,1024]{2,1,0:T(8,128)S(1)} %get-tuple-element.49), channel_id=1, source_target_pairs={{0,6},{1,7},{2,4},{3,5},{4,2},{5,3},{6,0},{7,1},{8,14},{9,15},{10,... | collective-permute-start | bytes 393224 | tf_op jit(solution)/shard_map/ppermute | solution.py:56
  279.6 12.2 %collective-permute-start.15 = (f32[4,8,1024]{2,1,0:T(8,128)S(1)}, f32[4,8,1024]{2,1,0:T(8,128)S(1)}, u32[]{:S(2)}, u32[]{:S(2)}) collective-permute-start(f32[4,8,1024]{2,1,0:T(8,128)S(1)} %get-tuple-element.50), channel_id=1, source_target_pairs={{0,4},{1,5},{2,6},{3,7},{4,0},{5,1},{6,2},{7,3},{8,12},{9,13},{10,... | collective-permute-start | bytes 393224 | tf_op jit(solution)/shard_map/ppermute | solution.py:56
  281.6 10.4 %collective-permute-start.14 = (f32[4,8,1024]{2,1,0:T(8,128)S(1)}, f32[4,8,1024]{2,1,0:T(8,128)S(1)}, u32[]{:S(2)}, u32[]{:S(2)}) collective-permute-start(f32[4,8,1024]{2,1,0:T(8,128)S(1)} %get-tuple-element.48), channel_id=1, source_target_pairs={{0,2},{1,3},{2,0},{3,1},{4,6},{5,7},{6,4},{7,5},{8,10},{9,11},{10,... | collective-permute-start | bytes 393224 | tf_op jit(solution)/shard_map/ppermute | solution.py:56
  292.1 14.7 %collective-permute-start.19 = (f32[1,8,1024]{2,1,0:T(8,128)S(1)}, f32[1,8,1024]{2,1,0:T(8,128)S(1)}, u32[]{:S(2)}, u32[]{:S(2)}) collective-permute-start(f32[1,8,1024]{2,1,0:T(8,128)S(1)} %get-tuple-element.63), channel_id=1, source_target_pairs={{0,24},{1,25},{2,26},{3,27},{4,28},{5,29},{6,30},{7,31},{8,16},{9,... | collective-permute-start | bytes 98312 | tf_op jit(solution)/shard_map/ppermute | solution.py:56
  297.9 8.8 %collective-permute-start.18 = (f32[1,8,1024]{2,1,0:T(8,128)S(1)}, f32[1,8,1024]{2,1,0:T(8,128)S(1)}, u32[]{:S(2)}, u32[]{:S(2)}) collective-permute-start(f32[1,8,1024]{2,1,0:T(8,128)S(1)} %get-tuple-element.64), channel_id=1, source_target_pairs={{0,16},{1,17},{2,18},{3,19},{4,20},{5,21},{6,22},{7,23},{8,24},{9,... | collective-permute-start | bytes 98312 | tf_op jit(solution)/shard_map/ppermute | solution.py:56
  302.3 9.9 %collective-permute-start.17 = (f32[1,8,1024]{2,1,0:T(8,128)S(1)}, f32[1,8,1024]{2,1,0:T(8,128)S(1)}, u32[]{:S(2)}, u32[]{:S(2)}) collective-permute-start(f32[1,8,1024]{2,1,0:T(8,128)S(1)} %get-tuple-element.62), channel_id=1, source_target_pairs={{0,8},{1,9},{2,10},{3,11},{4,12},{5,13},{6,14},{7,15},{8,0},{9,1},... | collective-permute-start | bytes 98312 | tf_op jit(solution)/shard_map/ppermute | solution.py:56
  312.2 7.2 %collective-permute-start.20 = (f32[9,1024]{1,0:T(8,128)S(1)}, f32[9,1024]{1,0:T(8,128)S(1)}, u32[]{:S(2)}, u32[]{:S(2)}) collective-permute-start(f32[9,1024]{1,0:T(8,128)S(1)} %pad_maximum_fusion.4), channel_id=1, source_target_pairs={{32,0},{64,32},{96,64},{128,96},{160,128},{192,160},{224,192},{256... | collective-permute-start | bytes 110600 | tf_op jit(solution)/shard_map/ppermute | solution.py:219
  319.5 6.9 %collective-permute-start.21 = (f32[9,1024]{1,0:T(8,128)S(1)}, f32[9,1024]{1,0:T(8,128)S(1)}, u32[]{:S(2)}, u32[]{:S(2)}) collective-permute-start(f32[9,1024]{1,0:T(8,128)S(1)} %pad_maximum_fusion.7), channel_id=1, source_target_pairs={{64,0},{96,32},{128,64},{160,96},{192,128},{224,160},{256,192},{28... | collective-permute-start | bytes 110600 | tf_op jit(solution)/shard_map/ppermute | solution.py:219
  326.4 7.8 %collective-permute-start.22 = (f32[9,1024]{1,0:T(8,128)S(1)}, f32[9,1024]{1,0:T(8,128)S(1)}, u32[]{:S(2)}, u32[]{:S(2)}) collective-permute-start(f32[9,1024]{1,0:T(8,128)S(1)} %pad_maximum_fusion.8), channel_id=1, source_target_pairs={{128,0},{160,32},{192,64},{224,96},{256,128},{288,160},{320,192},{... | collective-permute-start | bytes 110600 | tf_op jit(solution)/shard_map/ppermute | solution.py:219
  334.2 10.1 %collective-permute-start.23 = (f32[9,1024]{1,0:T(8,128)S(1)}, f32[9,1024]{1,0:T(8,128)S(1)}, u32[]{:S(2)}, u32[]{:S(2)}) collective-permute-start(f32[9,1024]{1,0:T(8,128)S(1)} %pad_maximum_fusion.9), channel_id=1, source_target_pairs={{256,0},{288,32},{320,64},{352,96},{384,128},{416,160},{448,192},{... | collective-permute-start | bytes 110600 | tf_op jit(solution)/shard_map/ppermute | solution.py:219
Sparse Core Ops, SparseCore 0:
  11.7 117.0 all-gather.1

commit v3 on v0

--- a/solution.py
+++ b/solution.py
@@ -210,7 +210,7 @@
     grad_slots = jnp.concatenate(
         [grad_keys.reshape(-1, width_kv), grad_vals.reshape(-1, width_kv)], axis=1
     )
-    local_grad = scattered_sum(grad_slots, "tok", (1, 2, 2))
+    local_grad = scattered_sum(grad_slots, "tok", (1, 1, 1, 1, 1))
 
     all_local = gathered(local_grad, "seg", ((2, 3), (0, 1)))
     memory_grad = all_local[seg_count - 1]

time: 349 us -> 351 us (level)
  waiting for transfers between devices: 132 us -> 146 us
  starting transfers between devices: 97.4 us -> 85.5 us
    ppermute x7 -> x5, waiting for transfers between devices: 13.2 us -> 27.4 us  [scattered_sum(): lax.ppermute(send, axis, [(i, i ^ flip) for i in range(size)])]
    ppermute x7 -> x5, starting transfers between devices: 27.1 us -> 15.2 us  [scattered_sum(): lax.ppermute(send, axis, [(i, i ^ flip) for i in range(size)])]
  transfers between devices with their start and end apart: 27 -> 25, of which waited for: 13 -> 14; matrix products, arithmetic and copies ran while one was open for 10% -> 10% of each run, Pallas kernels for 0% -> 0%
where the time goes in v3:
time: 351 us; the launch traced here: 350 us
  waiting for transfers between devices  146 us (42%)
  starting transfers between devices  85.5 us (24%)
  matrix products  53.2 us (15%)
  other arithmetic  24.6 us (7%)
  local copies, waits for them, and re-layouts  24.4 us (7%)
  between operations  16.4 us (5%)
    all_gather x1, waiting for transfers between devices, shards(): lax.all_gather(jnp.concatenate([seg_keys[0], seg_values[0]], axis=1), 'to...  107 us
    ppermute x19, starting transfers between devices, gathered(): lax.ppermute(held, axis, [(i, i ^ flip) for i in range(size)])  70.2 us
    ppermute x5, waiting for transfers between devices, scattered_sum(): lax.ppermute(send, axis, [(i, i ^ flip) for i in range(size)])  27.4 us
    dot_general x4, matrix products, shards(): jnp.einsum('tgjd,ugd->gjtu', queries, key_block, preferred_element_type=j...  20.6 us
    dot_general x4, matrix products, shards(): jnp.einsum('gjtu,ugd->tgjd', seg_weights, value_block, preferred_element_...  16.5 us
    ppermute x5, starting transfers between devices, scattered_sum(): lax.ppermute(send, axis, [(i, i ^ flip) for i in range(size)])  15.2 us
    reduce_sum x4, other arithmetic, softmax_step(): new_total = row_total * multiplier + jnp.sum(weights, axis=-1)  13.4 us
    ppermute x19, waiting for transfers between devices, gathered(): lax.ppermute(held, axis, [(i, i ^ flip) for i in range(size)])  11.8 us
  transfers between devices with their start and end apart: 25, of which 14 were waited for; matrix products, arithmetic and copies ran while one was open for 10% of the time, Pallas kernels for 0%

profile of v3, /device:TPU:2, one launch (start us, length us, event | category | flops | bytes accessed | tf_op | source)
XLA Modules:
  0.0 350.0 jit_solution(12330219052943023307)
XLA Ops:
  10.2 1.2 dynamic_slice.38
  12.1 1.4 reshape_squeeze.3
  13.5 1.3 copy.194
  14.9 1.2 dynamic_slice.37
  20.0 2.2 compare_and_fusion.1
  22.1 106.7 %all-gather.2.cloned.1.call-done = bf16[4096,1024]{0,1:T(8,128)(2,1)} async-done(((bf16[128,1024]{0,1:T(8,128)(2,1)}), bf16[4096,1024]{0,1:T(8,128)(2,1)}) %all-gather.2.cloned.1.call-update) | async-done | bytes 8388624 | tf_op jit(solution)/shard_map/all_gather | solution.py:93
  128.8 6.1 %fusion.183 = (bf16[4096,512]{0,1:T(8,128)(2,1)}, bf16[4096,512]{0,1:T(8,128)(2,1)}) fusion(bf16[4096,1024]{0,1:T(8,128)(2,1)} %all-gather.2.cloned.1.call-done), kind=kLoop, calls=%fused_computation.280 | loop fusion | bytes 16777216 | tf_op jit(solution)/shard_map/slice | solution.py:97
  134.9 3.1 fusion.186
  138.0 3.5 %fusion.80 = f32[8,4,128]{2,0,1:T(8,128)S(1)} fusion(bf16[4096,4,128]{0,2,1:T(8,128)(2,1)} %bitcast.625, bf16[4,8,4096]{2,1,0:T(8,128)(2,1)S(1)} %get-tuple-element.87, f32[8,4]{0,1:T(4,128)S(1)} %bitcast.699), kind=kOutput, calls=%fused_computation.70 | convolution fusion | flops 33558528 | bytes 4472960 | tf_op jit(solution)/shard_map/gru,ugd->rgd/dot_general | solution.py:110
  141.5 3.5 fusion.79
  145.3 6.6 %collective-permute-start = (f32[1,9,1024]{2,1,0:T(8,128)S(1)}, f32[1,9,1024]{2,1,0:T(8,128)S(1)}, u32[]{:S(2)}, u32[]{:S(2)}) collective-permute-start(f32[1,9,1024]{2,1,0:T(8,128)S(1)} %maximum_bitcast_fusion.1), channel_id=1, source_target_pairs={{0,384},{32,416},{64,448},{96,480},{128,256},{160,288},{192,320},{... | collective-permute-start | bytes 110600 | tf_op jit(solution)/shard_map/ppermute | solution.py:29
  151.8 3.5 %collective-permute-start.1 = (f32[1,9,1024]{2,1,0:T(8,128)S(1)}, f32[1,9,1024]{2,1,0:T(8,128)S(1)}, u32[]{:S(2)}, u32[]{:S(2)}) collective-permute-start(f32[1,9,1024]{2,1,0:T(8,128)S(1)} %maximum_bitcast_fusion.1), channel_id=1, source_target_pairs={{0,256},{32,288},{64,320},{96,352},{128,384},{160,416},{192,448},{... | collective-permute-start | bytes 110600 | tf_op jit(solution)/shard_map/ppermute | solution.py:29
  155.4 2.7 collective-permute-start.2
  158.1 2.4 fusion.182
  160.5 2.4 collective-permute-done.1
  162.8 1.8 collective-permute-done.2
  164.7 2.3 collective-permute-start.3
  167.0 4.4 %collective-permute-start.4 = (f32[2,2,1,9,1024]{4,3,1,0,2:T(8,128)S(1)}, f32[2,2,1,9,1024]{4,3,1,0,2:T(8,128)S(1)}, u32[]{:S(2)}, u32[]{:S(2)}) collective-permute-start(f32[2,2,1,9,1024]{4,3,1,0,2:T(8,128)S(1)} %bitcast.644), channel_id=1, source_target_pairs={{0,64},{32,96},{64,0},{96,32},{128,192},{160,224},{192,128},{224,1... | collective-permute-start | bytes 442376 | tf_op jit(solution)/shard_map/ppermute | solution.py:29
  171.4 2.5 collective-permute-start.5
  173.9 4.9 %fusion.4 = (f32[4,4,128]{2,1,0:T(4,128)S(1)}, f32[4,1024,128,4]{2,1,3,0:T(8,128)}) fusion(pred[128,1024]{0,1:T(8,128)(4,1)S(1)} %get-tuple-element.83, bf16[1024,4,128,1]{0,2,3,1:T(8,128)(2,1)S(1)} %bitcast.629, bf16[128,4,4,128]{3,2,1,0:T(4,128)(2,1)S(1)} %reshape_squeeze.3), kind=kOutput, calls=%fused_computation.12 | convolution fusion | flops 543160320 | bytes 10100736 | tf_op jit(solution)/shard_map/tgjd,ugd->gjtu/dot_general | solution.py:154
  178.8 2.3 collective-permute-done.4
  182.9 4.9 %collective-permute-start.6 = (bf16[1,8,1024]{2,1,0:T(8,128)(2,1)S(1)}, bf16[1,8,1024]{2,1,0:T(8,128)(2,1)S(1)}, u32[]{:S(2)}, u32[]{:S(2)}) collective-permute-start(bf16[1,8,1024]{2,1,0:T(8,128)(2,1)S(1)} %get-tuple-element.23), channel_id=1, source_target_pairs={{0,24},{1,25},{2,26},{3,27},{4,28},{5,29},{6,30},{7,31},{8,16},{9,... | collective-permute-start | bytes 49160 | tf_op jit(solution)/shard_map/ppermute | solution.py:29
  187.8 4.4 %collective-permute-start.7 = (bf16[1,8,1024]{2,1,0:T(8,128)(2,1)S(1)}, bf16[1,8,1024]{2,1,0:T(8,128)(2,1)S(1)}, u32[]{:S(2)}, u32[]{:S(2)}) collective-permute-start(bf16[1,8,1024]{2,1,0:T(8,128)(2,1)S(1)} %get-tuple-element.23), channel_id=1, source_target_pairs={{0,16},{1,17},{2,18},{3,19},{4,20},{5,21},{6,22},{7,23},{8,24},{9,... | collective-permute-start | bytes 49160 | tf_op jit(solution)/shard_map/ppermute | solution.py:29
  192.3 5.3 %collective-permute-start.8 = (bf16[1,8,1024]{2,1,0:T(8,128)(2,1)S(1)}, bf16[1,8,1024]{2,1,0:T(8,128)(2,1)S(1)}, u32[]{:S(2)}, u32[]{:S(2)}) collective-permute-start(bf16[1,8,1024]{2,1,0:T(8,128)(2,1)S(1)} %get-tuple-element.23), channel_id=1, source_target_pairs={{0,8},{1,9},{2,10},{3,11},{4,12},{5,13},{6,14},{7,15},{8,0},{9,1},... | collective-permute-start | bytes 49160 | tf_op jit(solution)/shard_map/ppermute | solution.py:29
  197.7 5.5 %fusion.3 = (f32[4,4,128]{2,1,0:T(4,128)}, f32[4,1024,128,4]{2,1,3,0:T(8,128)}) fusion(pred[128,1024]{0,1:T(8,128)(4,1)S(1)} %get-tuple-element.82, bf16[1024,4,128,1]{0,2,3,1:T(8,128)(2,1)S(1)} %bitcast.628, bf16[128,4,4,128]{3,2,1,0:T(4,128)(2,1)S(1)} %reshape_squeeze.3), kind=kOutput, calls=%fused_computation.11 | convolution fusion | flops 543160320 | bytes 10100736 | tf_op jit(solution)/shard_map/tgjd,ugd->gjtu/dot_general | solution.py:154
  203.2 4.0 %collective-permute-start.9 = (bf16[2,2,1,8,1024]{4,3,1,0,2:T(8,128)(2,1)S(1)}, bf16[2,2,1,8,1024]{4,3,1,0,2:T(8,128)(2,1)S(1)}, u32[]{:S(2)}, u32[]{:S(2)}) collective-permute-start(bf16[2,2,1,8,1024]{4,3,1,0,2:T(8,128)(2,1)S(1)} %bitcast.663), channel_id=1, source_target_pairs={{0,6},{1,7},{2,4},{3,5},{4,2},{5,3},{6,0},{7,1},{8,14},{9,15},{10,... | collective-permute-start | bytes 196616 | tf_op jit(solution)/shard_map/ppermute | solution.py:29
  207.2 2.7 collective-permute-start.10
  210.0 3.3 collective-permute-start.11
  213.3 5.5 %fusion.2 = (f32[4,4,128]{2,1,0:T(4,128)}, f32[4,1024,128,4]{2,1,3,0:T(8,128)}) fusion(pred[128,1024]{0,1:T(8,128)(4,1)S(1)} %get-tuple-element.84, bf16[1024,4,128,1]{0,2,3,1:T(8,128)(2,1)S(1)} %bitcast.627, bf16[128,4,4,128]{3,2,1,0:T(4,128)(2,1)S(1)} %reshape_squeeze.3), kind=kOutput, calls=%fused_computation.10 | convolution fusion | flops 543160320 | bytes 10100736 | tf_op jit(solution)/shard_map/tgjd,ugd->gjtu/dot_general | solution.py:154
  218.9 2.1 collective-permute-start.12
  221.0 4.8 %fusion.1 = (f32[4,4,128]{2,1,0:T(4,128)S(1)}, f32[4,1024,128,4]{2,1,3,0:T(8,128)}) fusion(pred[128,1024]{0,1:T(8,128)(4,1)S(1)} %copy-done.3, bf16[1024,4,128,1]{0,2,3,1:T(8,128)(2,1)S(1)} %bitcast.626, bf16[128,4,4,128]{3,2,1,0:T(4,128)(2,1)S(1)} %reshape_squeeze.3), kind=kOutput, calls=%fused_computation.9 | convolution fusion | flops 543160320 | bytes 10100736 | tf_op jit(solution)/shard_map/tgjd,ugd->gjtu/dot_general | solution.py:154
  227.6 1.5 bitcast_reduce_fusion
  230.2 4.6 %fusion.11 = f32[4,4,128]{2,1,0:T(4,128)S(1)} fusion(f32[4,1024,128,4]{2,1,3,0:T(8,128)} %get-tuple-element.91, f32[4,4,128]{2,1,0:T(4,128)S(1)} %get-tuple-element.20, pred[128,1024]{0,1:T(8,128)(4,1)S(1)} %get-tuple-element.83), kind=kLoop, calls=%fused_computation.19 | loop fusion | flops 10483712 | bytes 8536064 | tf_op jit(solution)/shard_map/reduce_sum | solution.py:73
  234.8 4.8 %fusion.9 = f32[4,4,128]{2,1,0:T(4,128)S(1)} fusion(f32[4,1024,128,4]{2,1,3,0:T(8,128)} %get-tuple-element.93, f32[4,4,128]{2,1,0:T(4,128)S(1)} %get-tuple-element.21, pred[128,1024]{0,1:T(8,128)(4,1)S(1)} %get-tuple-element.82), kind=kLoop, calls=%fused_computation.17 | loop fusion | flops 10483712 | bytes 8536064 | tf_op jit(solution)/shard_map/reduce_sum | solution.py:73
  239.9 2.0 fusion.7
  242.0 2.0 fusion.5
  244.7 1.8 copy.140
  246.5 5.9 %fusion.64 = f32[128,4,4,128]{0,3,2,1:T(8,128)S(1)} fusion(bf16[1024,4,128,1]{0,2,3,1:T(8,128)(2,1)} %bitcast.642, f32[4,1024,128,4]{2,1,3,0:T(8,128)} %get-tuple-element.97, f32[4,4,128]{2,1,0:T(4,128)} %copy-done.52, pred[128,1024]{0,1:T(8,128)(4,1)} %get-tuple-element.85, f32[128,4,4]{0,2,1:T(4,128)} %get-tuple-element.77, ...), kind=kOutput, calls=%fused_computation.59 | convolution fusion | flops 547880960 | bytes 10641408 | tf_op jit(solution)/shard_map/gjtu,ugd->tgjd/dot_general | solution.py:160
  252.5 5.7 %fusion.67 = f32[128,4,4,128]{0,3,2,1:T(8,128)S(1)} fusion(f32[128,4,4,128]{0,3,2,1:T(8,128)S(1)} %fusion.64, bf16[1024,4,128,1]{0,2,3,1:T(8,128)(2,1)S(1)} %bitcast.641, f32[4,1024,128,4]{2,1,3,0:T(8,128)} %get-tuple-element.95, f32[4,4,128]{2,1,0:T(4,128)S(1)} %copy-done.21, pred[128,1024]{0,1:T(8,128)(4,1)S(1)} %get-tuple-element.84, ...), kind=kOutput, calls=%fused_computation.60 | convolution fusion | flops 547880960 | bytes 11681792 | tf_op jit(solution)/shard_map/gjtu,ugd->tgjd/dot_general | solution.py:160
  258.3 2.4 fusion.70
  260.8 2.6 fusion.73
  263.4 1.4 fusion.187
  265.0 1.3 convolution_bitcast_fusion.1
  266.3 1.8 fusion.78
  268.2 1.5 copy.146
  269.9 1.3 copy.148
  271.5 2.4 collective-permute-start.13
  273.9 1.5 collective-permute-done.13
  275.6 2.5 collective-permute-start.14
  278.1 8.0 %collective-permute-done.14 = f32[8,8,1024]{2,1,0:T(8,128)S(1)} collective-permute-done((f32[8,8,1024]{2,1,0:T(8,128)S(1)}, f32[8,8,1024]{2,1,0:T(8,128)S(1)}, u32[]{:S(2)}, u32[]{:S(2)}) %collective-permute-start.14) | collective-permute-done | bytes 262176 | tf_op jit(solution)/shard_map/ppermute | solution.py:56
  286.1 2.9 collective-permute-start.15
  289.0 7.6 %collective-permute-done.15 = f32[4,8,1024]{2,1,0:T(8,128)S(1)} collective-permute-done((f32[4,8,1024]{2,1,0:T(8,128)S(1)}, f32[4,8,1024]{2,1,0:T(8,128)S(1)}, u32[]{:S(2)}, u32[]{:S(2)}) %collective-permute-start.15) | collective-permute-done | bytes 131104 | tf_op jit(solution)/shard_map/ppermute | solution.py:56
  296.7 4.5 %collective-permute-start.16 = (f32[2,8,1024]{2,1,0:T(8,128)S(1)}, f32[2,8,1024]{2,1,0:T(8,128)S(1)}, u32[]{:S(2)}, u32[]{:S(2)}) collective-permute-start(f32[2,8,1024]{2,1,0:T(8,128)S(1)} %dynamic-slice_bitcast_fusion.3), channel_id=1, source_target_pairs={{0,8},{1,9},{2,10},{3,11},{4,12},{5,13},{6,14},{7,15},{8,0},{9,1},... | collective-permute-start | bytes 196616 | tf_op jit(solution)/shard_map/ppermute | solution.py:56
  301.2 6.0 %collective-permute-done.16 = f32[2,8,1024]{2,1,0:T(8,128)S(1)} collective-permute-done((f32[2,8,1024]{2,1,0:T(8,128)S(1)}, f32[2,8,1024]{2,1,0:T(8,128)S(1)}, u32[]{:S(2)}, u32[]{:S(2)}) %collective-permute-start.16) | collective-permute-done | bytes 65568 | tf_op jit(solution)/shard_map/ppermute | solution.py:56
  307.2 3.0 collective-permute-start.17
  310.1 4.4 %collective-permute-done.17 = f32[1,8,1024]{2,1,0:T(8,128)S(1)} collective-permute-done((f32[1,8,1024]{2,1,0:T(8,128)S(1)}, f32[1,8,1024]{2,1,0:T(8,128)S(1)}, u32[]{:S(2)}, u32[]{:S(2)}) %collective-permute-start.17) | collective-permute-done | bytes 32800 | tf_op jit(solution)/shard_map/ppermute | solution.py:56
  314.5 3.3 collective-permute-start.18
  317.8 4.3 %collective-permute-start.19 = (f32[1,8,1024]{2,1,0:T(8,128)S(1)}, f32[1,8,1024]{2,1,0:T(8,128)S(1)}, u32[]{:S(2)}, u32[]{:S(2)}) collective-permute-start(f32[1,8,1024]{2,1,0:T(8,128)S(1)} %dynamic-slice_add_fusion), channel_id=1, source_target_pairs={{0,256},{32,288},{64,320},{96,352},{128,384},{160,416},{192,448},{... | collective-permute-start | bytes 98312 | tf_op jit(solution)/shard_map/ppermute | solution.py:29
  322.2 4.6 %collective-permute-start.20 = (f32[1,8,1024]{2,1,0:T(8,128)S(1)}, f32[1,8,1024]{2,1,0:T(8,128)S(1)}, u32[]{:S(2)}, u32[]{:S(2)}) collective-permute-start(f32[1,8,1024]{2,1,0:T(8,128)S(1)} %dynamic-slice_add_fusion), channel_id=1, source_target_pairs={{0,128},{32,160},{64,192},{96,224},{128,0},{160,32},{192,64},{224,... | collective-permute-start | bytes 98312 | tf_op jit(solution)/shard_map/ppermute | solution.py:29
  327.6 1.3 collective-permute-done.20
  328.9 3.9 %collective-permute-start.21 = (f32[2,2,1,8,1024]{4,3,1,0,2:T(8,128)S(1)}, f32[2,2,1,8,1024]{4,3,1,0,2:T(8,128)S(1)}, u32[]{:S(2)}, u32[]{:S(2)}) collective-permute-start(f32[2,2,1,8,1024]{4,3,1,0,2:T(8,128)S(1)} %bitcast.657), channel_id=1, source_target_pairs={{0,96},{32,64},{64,32},{96,0},{128,224},{160,192},{192,160},{224,1... | collective-permute-start | bytes 393224 | tf_op jit(solution)/shard_map/ppermute | solution.py:29
  332.8 2.4 collective-permute-start.22
  335.2 2.9 collective-permute-start.23
  339.7 2.4 collective-permute-done.23
  (211 shorter events, 17.0 us)
Async XLA Ops:
  7.2 127.7 %copy-start = (bf16[8,512]{1,0:T(8,128)(2,1)S(1)}, bf16[8,512]{1,0:T(8,128)(2,1)}, u32[]{:S(2)}) copy-start(bf16[8,512]{1,0:T(8,128)(2,1)} %param.14) | copy-start | bytes 24580
  7.2 121.6 %all-gather.2.cloned.1.call-start = ((), (), s32[]{:S(2)}) async-start(), calls=%async_computation | async-start | bytes 8650752 | tf_op jit(solution)/shard_map/all_gather | solution.py:93
  138.0 20.0 %copy-start.2 = (bf16[4096,1024]{0,1:T(8,128)(2,1)S(1)}, bf16[4096,1024]{0,1:T(8,128)(2,1)}, u32[]{:S(2)}) copy-start(bf16[4096,1024]{0,1:T(8,128)(2,1)} %all-gather.2.cloned.1.call-done) | copy-start | bytes 25165828
  145.3 15.2 %collective-permute-start = (f32[1,9,1024]{2,1,0:T(8,128)S(1)}, f32[1,9,1024]{2,1,0:T(8,128)S(1)}, u32[]{:S(2)}, u32[]{:S(2)}) collective-permute-start(f32[1,9,1024]{2,1,0:T(8,128)S(1)} %maximum_bitcast_fusion.1), channel_id=1, source_target_pairs={{0,384},{32,416},{64,448},{96,480},{128,256},{160,288},{192,320},{... | collective-permute-start | bytes 110600 | tf_op jit(solution)/shard_map/ppermute | solution.py:29
  151.8 11.0 %collective-permute-start.1 = (f32[1,9,1024]{2,1,0:T(8,128)S(1)}, f32[1,9,1024]{2,1,0:T(8,128)S(1)}, u32[]{:S(2)}, u32[]{:S(2)}) collective-permute-start(f32[1,9,1024]{2,1,0:T(8,128)S(1)} %maximum_bitcast_fusion.1), channel_id=1, source_target_pairs={{0,256},{32,288},{64,320},{96,352},{128,384},{160,416},{192,448},{... | collective-permute-start | bytes 110600 | tf_op jit(solution)/shard_map/ppermute | solution.py:29
  155.4 9.2 %collective-permute-start.2 = (f32[1,9,1024]{2,1,0:T(8,128)S(1)}, f32[1,9,1024]{2,1,0:T(8,128)S(1)}, u32[]{:S(2)}, u32[]{:S(2)}) collective-permute-start(f32[1,9,1024]{2,1,0:T(8,128)S(1)} %maximum_bitcast_fusion.1), channel_id=1, source_target_pairs={{0,128},{32,160},{64,192},{96,224},{128,0},{160,32},{192,64},{224,... | collective-permute-start | bytes 110600 | tf_op jit(solution)/shard_map/ppermute | solution.py:29
  164.7 14.1 %collective-permute-start.3 = (f32[2,2,1,9,1024]{4,3,1,0,2:T(8,128)S(1)}, f32[2,2,1,9,1024]{4,3,1,0,2:T(8,128)S(1)}, u32[]{:S(2)}, u32[]{:S(2)}) collective-permute-start(f32[2,2,1,9,1024]{4,3,1,0,2:T(8,128)S(1)} %bitcast.643), channel_id=1, source_target_pairs={{0,96},{32,64},{64,32},{96,0},{128,224},{160,192},{192,160},{224,1... | collective-permute-start | bytes 442376 | tf_op jit(solution)/shard_map/ppermute | solution.py:29
  167.0 14.1 %collective-permute-start.4 = (f32[2,2,1,9,1024]{4,3,1,0,2:T(8,128)S(1)}, f32[2,2,1,9,1024]{4,3,1,0,2:T(8,128)S(1)}, u32[]{:S(2)}, u32[]{:S(2)}) collective-permute-start(f32[2,2,1,9,1024]{4,3,1,0,2:T(8,128)S(1)} %bitcast.644), channel_id=1, source_target_pairs={{0,64},{32,96},{64,0},{96,32},{128,192},{160,224},{192,128},{224,1... | collective-permute-start | bytes 442376 | tf_op jit(solution)/shard_map/ppermute | solution.py:29
  171.4 10.1 %collective-permute-start.5 = (f32[2,2,1,9,1024]{4,3,1,0,2:T(8,128)S(1)}, f32[2,2,1,9,1024]{4,3,1,0,2:T(8,128)S(1)}, u32[]{:S(2)}, u32[]{:S(2)}) collective-permute-start(f32[2,2,1,9,1024]{4,3,1,0,2:T(8,128)S(1)} %bitcast.645), channel_id=1, source_target_pairs={{0,32},{32,0},{64,96},{96,64},{128,160},{160,128},{192,224},{224,1... | collective-permute-start | bytes 442376 | tf_op jit(solution)/shard_map/ppermute | solution.py:29
  182.0 15.5 %copy-start.26 = (f32[1,1,1024]{2,1,0:T(1,128)}, f32[1,1,1024]{2,1,0:T(1,128)S(1)}, u32[]{:S(2)}) copy-start(f32[1,1,1024]{2,1,0:T(1,128)S(1)} %get-tuple-element.37) | copy-start | bytes 12292
  182.0 15.5 %copy-start.28 = (f32[1,1,1024]{2,1,0:T(1,128)}, f32[1,1,1024]{2,1,0:T(1,128)S(1)}, u32[]{:S(2)}) copy-start(f32[1,1,1024]{2,1,0:T(1,128)S(1)} %get-tuple-element.38) | copy-start | bytes 12292
  182.0 15.5 %copy-start.30 = (f32[1,1,1024]{2,1,0:T(1,128)}, f32[1,1,1024]{2,1,0:T(1,128)S(1)}, u32[]{:S(2)}) copy-start(f32[1,1,1024]{2,1,0:T(1,128)S(1)} %get-tuple-element.39) | copy-start | bytes 12292
  182.0 15.5 %copy-start.32 = (f32[1,1,1024]{2,1,0:T(1,128)}, f32[1,1,1024]{2,1,0:T(1,128)S(1)}, u32[]{:S(2)}) copy-start(f32[1,1,1024]{2,1,0:T(1,128)S(1)} %get-tuple-element.40) | copy-start | bytes 12292
  182.0 15.5 %copy-start.34 = (f32[1,1,1024]{2,1,0:T(1,128)}, f32[1,1,1024]{2,1,0:T(1,128)S(1)}, u32[]{:S(2)}) copy-start(f32[1,1,1024]{2,1,0:T(1,128)S(1)} %get-tuple-element.41) | copy-start | bytes 12292
  182.0 15.5 %copy-start.36 = (f32[1,1,1024]{2,1,0:T(1,128)}, f32[1,1,1024]{2,1,0:T(1,128)S(1)}, u32[]{:S(2)}) copy-start(f32[1,1,1024]{2,1,0:T(1,128)S(1)} %get-tuple-element.42) | copy-start | bytes 12292
  182.1 15.5 %copy-start.38 = (f32[1,1,1024]{2,1,0:T(1,128)}, f32[1,1,1024]{2,1,0:T(1,128)S(1)}, u32[]{:S(2)}) copy-start(f32[1,1,1024]{2,1,0:T(1,128)S(1)} %get-tuple-element.43) | copy-start | bytes 12292
  182.1 15.5 %copy-start.40 = (f32[1,1,1024]{2,1,0:T(1,128)}, f32[1,1,1024]{2,1,0:T(1,128)S(1)}, u32[]{:S(2)}) copy-start(f32[1,1,1024]{2,1,0:T(1,128)S(1)} %get-tuple-element.44) | copy-start | bytes 12292
  182.1 15.5 %copy-start.42 = (f32[1,1,1024]{2,1,0:T(1,128)}, f32[1,1,1024]{2,1,0:T(1,128)S(1)}, u32[]{:S(2)}) copy-start(f32[1,1,1024]{2,1,0:T(1,128)S(1)} %get-tuple-element.45) | copy-start | bytes 12292
  182.1 15.5 %copy-start.44 = (f32[1,1,1024]{2,1,0:T(1,128)}, f32[1,1,1024]{2,1,0:T(1,128)S(1)}, u32[]{:S(2)}) copy-start(f32[1,1,1024]{2,1,0:T(1,128)S(1)} %get-tuple-element.46) | copy-start | bytes 12292
  182.1 15.5 %copy-start.46 = (f32[1,1,1024]{2,1,0:T(1,128)}, f32[1,1,1024]{2,1,0:T(1,128)S(1)}, u32[]{:S(2)}) copy-start(f32[1,1,1024]{2,1,0:T(1,128)S(1)} %get-tuple-element.47) | copy-start | bytes 12292
  182.1 15.5 %copy-start.48 = (f32[1,1,1024]{2,1,0:T(1,128)}, f32[1,1,1024]{2,1,0:T(1,128)S(1)}, u32[]{:S(2)}) copy-start(f32[1,1,1024]{2,1,0:T(1,128)S(1)} %get-tuple-element.48) | copy-start | bytes 12292
  182.1 15.5 %copy-start.50 = (f32[1,1,1024]{2,1,0:T(1,128)}, f32[1,1,1024]{2,1,0:T(1,128)S(1)}, u32[]{:S(2)}) copy-start(f32[1,1,1024]{2,1,0:T(1,128)S(1)} %get-tuple-element.49) | copy-start | bytes 12292
  182.1 36.7 %copy-start.22 = (f32[1,1,1024]{2,1,0:T(1,128)}, f32[1,1,1024]{2,1,0:T(1,128)S(1)}, u32[]{:S(2)}) copy-start(f32[1,1,1024]{2,1,0:T(1,128)S(1)} %get-tuple-element.35) | copy-start | bytes 12292
  182.1 36.7 %copy-start.24 = (f32[1,1,1024]{2,1,0:T(1,128)}, f32[1,1,1024]{2,1,0:T(1,128)S(1)}, u32[]{:S(2)}) copy-start(f32[1,1,1024]{2,1,0:T(1,128)S(1)} %get-tuple-element.36) | copy-start | bytes 12292
  182.9 20.2 %collective-permute-start.6 = (bf16[1,8,1024]{2,1,0:T(8,128)(2,1)S(1)}, bf16[1,8,1024]{2,1,0:T(8,128)(2,1)S(1)}, u32[]{:S(2)}, u32[]{:S(2)}) collective-permute-start(bf16[1,8,1024]{2,1,0:T(8,128)(2,1)S(1)} %get-tuple-element.23), channel_id=1, source_target_pairs={{0,24},{1,25},{2,26},{3,27},{4,28},{5,29},{6,30},{7,31},{8,16},{9,... | collective-permute-start | bytes 49160 | tf_op jit(solution)/shard_map/ppermute | solution.py:29
  187.8 15.3 %collective-permute-start.7 = (bf16[1,8,1024]{2,1,0:T(8,128)(2,1)S(1)}, bf16[1,8,1024]{2,1,0:T(8,128)(2,1)S(1)}, u32[]{:S(2)}, u32[]{:S(2)}) collective-permute-start(bf16[1,8,1024]{2,1,0:T(8,128)(2,1)S(1)} %get-tuple-element.23), channel_id=1, source_target_pairs={{0,16},{1,17},{2,18},{3,19},{4,20},{5,21},{6,22},{7,23},{8,24},{9,... | collective-permute-start | bytes 49160 | tf_op jit(solution)/shard_map/ppermute | solution.py:29
  192.3 10.9 %collective-permute-start.8 = (bf16[1,8,1024]{2,1,0:T(8,128)(2,1)S(1)}, bf16[1,8,1024]{2,1,0:T(8,128)(2,1)S(1)}, u32[]{:S(2)}, u32[]{:S(2)}) collective-permute-start(bf16[1,8,1024]{2,1,0:T(8,128)(2,1)S(1)} %get-tuple-element.23), channel_id=1, source_target_pairs={{0,8},{1,9},{2,10},{3,11},{4,12},{5,13},{6,14},{7,15},{8,0},{9,1},... | collective-permute-start | bytes 49160 | tf_op jit(solution)/shard_map/ppermute | solution.py:29
  203.1 17.9 %copy-start.3 = (pred[128,1024]{0,1:T(8,128)(4,1)S(1)}, pred[128,1024]{0,1:T(8,128)(4,1)}, u32[]{:S(2)}) copy-start(pred[128,1024]{0,1:T(8,128)(4,1)} %get-tuple-element.85) | copy-start | bytes 393220
  203.2 15.6 %collective-permute-start.9 = (bf16[2,2,1,8,1024]{4,3,1,0,2:T(8,128)(2,1)S(1)}, bf16[2,2,1,8,1024]{4,3,1,0,2:T(8,128)(2,1)S(1)}, u32[]{:S(2)}, u32[]{:S(2)}) collective-permute-start(bf16[2,2,1,8,1024]{4,3,1,0,2:T(8,128)(2,1)S(1)} %bitcast.663), channel_id=1, source_target_pairs={{0,6},{1,7},{2,4},{3,5},{4,2},{5,3},{6,0},{7,1},{8,14},{9,15},{10,... | collective-permute-start | bytes 196616 | tf_op jit(solution)/shard_map/ppermute | solution.py:29
  207.2 11.6 %collective-permute-start.10 = (bf16[2,2,1,8,1024]{4,3,1,0,2:T(8,128)(2,1)S(1)}, bf16[2,2,1,8,1024]{4,3,1,0,2:T(8,128)(2,1)S(1)}, u32[]{:S(2)}, u32[]{:S(2)}) collective-permute-start(bf16[2,2,1,8,1024]{4,3,1,0,2:T(8,128)(2,1)S(1)} %bitcast.664), channel_id=1, source_target_pairs={{0,4},{1,5},{2,6},{3,7},{4,0},{5,1},{6,2},{7,3},{8,12},{9,13},{10,... | collective-permute-start | bytes 196616 | tf_op jit(solution)/shard_map/ppermute | solution.py:29
  210.0 8.9 %collective-permute-start.11 = (bf16[2,2,1,8,1024]{4,3,1,0,2:T(8,128)(2,1)S(1)}, bf16[2,2,1,8,1024]{4,3,1,0,2:T(8,128)(2,1)S(1)}, u32[]{:S(2)}, u32[]{:S(2)}) collective-permute-start(bf16[2,2,1,8,1024]{4,3,1,0,2:T(8,128)(2,1)S(1)} %bitcast.665), channel_id=1, source_target_pairs={{0,2},{1,3},{2,0},{3,1},{4,6},{5,7},{6,4},{7,5},{8,10},{9,11},{10,... | collective-permute-start | bytes 196616 | tf_op jit(solution)/shard_map/ppermute | solution.py:29
  218.9 6.9 %collective-permute-start.12 = (bf16[2,2,2,2,1,8,1024]{6,5,3,2,1,0,4:T(8,128)(2,1)S(1)}, bf16[2,2,2,2,1,8,1024]{6,5,3,2,1,0,4:T(8,128)(2,1)S(1)}, u32[]{:S(2)}, u32[]{:S(2)}) collective-permute-start(bf16[2,2,2,2,1,8,1024]{6,5,3,2,1,0,4:T(8,128)(2,1)S(1)} %bitcast.647), channel_id=1, source_target_pairs={{0,1},{1,0},{2,3},{3,2},{4,5},{5,4},{6,7},{7,6},{8,9},{9,8},{10,11... | collective-permute-start | bytes 786440 | tf_op jit(solution)/shard_map/ppermute | solution.py:29
  229.8 14.9 %copy-start.14 = (f32[4,4,128]{2,1,0:T(4,128)}, f32[4,4,128]{2,1,0:T(4,128)S(1)}, u32[]{:S(2)}) copy-start(f32[4,4,128]{2,1,0:T(4,128)S(1)} %get-tuple-element.19) | copy-start | bytes 24580
  229.8 14.8 %copy-start.16 = (f32[4,4,128]{2,1,0:T(4,128)}, f32[4,4,128]{2,1,0:T(4,128)S(1)}, u32[]{:S(2)}) copy-start(f32[4,4,128]{2,1,0:T(4,128)S(1)} %get-tuple-element.20) | copy-start | bytes 24580
  229.8 14.8 %copy-start.18 = (f32[4,4,128]{2,1,0:T(4,128)}, f32[4,4,128]{2,1,0:T(4,128)S(1)}, u32[]{:S(2)}) copy-start(f32[4,4,128]{2,1,0:T(4,128)S(1)} %get-tuple-element.21) | copy-start | bytes 24580
  229.8 14.8 %copy-start.20 = (f32[4,4,128]{2,1,0:T(4,128)}, f32[4,4,128]{2,1,0:T(4,128)S(1)}, u32[]{:S(2)}) copy-start(f32[4,4,128]{2,1,0:T(4,128)S(1)} %get-tuple-element.22) | copy-start | bytes 24580
  266.3 76.8 %copy-start.1 = (bf16[8,512]{1,0:T(8,128)(2,1)S(1)}, bf16[8,512]{1,0:T(8,128)(2,1)}, u32[]{:S(2)}) copy-start(bf16[8,512]{1,0:T(8,128)(2,1)} %param.14) | copy-start | bytes 24580
  268.1 70.1 %copy-start.8 = (bf16[128,4,4,128]{0,3,2,1:T(8,128)(2,1)S(1)}, bf16[128,4,4,128]{0,3,2,1:T(8,128)(2,1)}, u32[]{:S(2)}) copy-start(bf16[128,4,4,128]{0,3,2,1:T(8,128)(2,1)} %get-tuple-element.98) | copy-start | bytes 1572868
  268.1 74.1 %copy-start.23 = (f32[1,1,1024]{2,1,0:T(1,128)S(1)}, f32[1,1,1024]{2,1,0:T(1,128)}, u32[]{:S(2)}) copy-start(f32[1,1,1024]{2,1,0:T(1,128)} %copy-done.22) | copy-start | bytes 12292
  268.1 74.2 %copy-start.25 = (f32[1,1,1024]{2,1,0:T(1,128)S(1)}, f32[1,1,1024]{2,1,0:T(1,128)}, u32[]{:S(2)}) copy-start(f32[1,1,1024]{2,1,0:T(1,128)} %copy-done.24) | copy-start | bytes 12292
  268.1 74.2 %copy-start.27 = (f32[1,1,1024]{2,1,0:T(1,128)S(1)}, f32[1,1,1024]{2,1,0:T(1,128)}, u32[]{:S(2)}) copy-start(f32[1,1,1024]{2,1,0:T(1,128)} %copy-done.26) | copy-start | bytes 12292
  268.1 74.2 %copy-start.29 = (f32[1,1,1024]{2,1,0:T(1,128)S(1)}, f32[1,1,1024]{2,1,0:T(1,128)}, u32[]{:S(2)}) copy-start(f32[1,1,1024]{2,1,0:T(1,128)} %copy-done.28) | copy-start | bytes 12292
  268.1 74.2 %copy-start.31 = (f32[1,1,1024]{2,1,0:T(1,128)S(1)}, f32[1,1,1024]{2,1,0:T(1,128)}, u32[]{:S(2)}) copy-start(f32[1,1,1024]{2,1,0:T(1,128)} %copy-done.30) | copy-start | bytes 12292
  268.1 74.2 %copy-start.33 = (f32[1,1,1024]{2,1,0:T(1,128)S(1)}, f32[1,1,1024]{2,1,0:T(1,128)}, u32[]{:S(2)}) copy-start(f32[1,1,1024]{2,1,0:T(1,128)} %copy-done.32) | copy-start | bytes 12292
  268.1 74.2 %copy-start.35 = (f32[1,1,1024]{2,1,0:T(1,128)S(1)}, f32[1,1,1024]{2,1,0:T(1,128)}, u32[]{:S(2)}) copy-start(f32[1,1,1024]{2,1,0:T(1,128)} %copy-done.34) | copy-start | bytes 12292
  268.1 74.2 %copy-start.37 = (f32[1,1,1024]{2,1,0:T(1,128)S(1)}, f32[1,1,1024]{2,1,0:T(1,128)}, u32[]{:S(2)}) copy-start(f32[1,1,1024]{2,1,0:T(1,128)} %copy-done.36) | copy-start | bytes 12292
  268.1 74.2 %copy-start.39 = (f32[1,1,1024]{2,1,0:T(1,128)S(1)}, f32[1,1,1024]{2,1,0:T(1,128)}, u32[]{:S(2)}) copy-start(f32[1,1,1024]{2,1,0:T(1,128)} %copy-done.38) | copy-start | bytes 12292
  268.1 74.2 %copy-start.41 = (f32[1,1,1024]{2,1,0:T(1,128)S(1)}, f32[1,1,1024]{2,1,0:T(1,128)}, u32[]{:S(2)}) copy-start(f32[1,1,1024]{2,1,0:T(1,128)} %copy-done.40) | copy-start | bytes 12292
  268.1 74.2 %copy-start.43 = (f32[1,1,1024]{2,1,0:T(1,128)S(1)}, f32[1,1,1024]{2,1,0:T(1,128)}, u32[]{:S(2)}) copy-start(f32[1,1,1024]{2,1,0:T(1,128)} %copy-done.42) | copy-start | bytes 12292
  268.2 74.2 %copy-start.45 = (f32[1,1,1024]{2,1,0:T(1,128)S(1)}, f32[1,1,1024]{2,1,0:T(1,128)}, u32[]{:S(2)}) copy-start(f32[1,1,1024]{2,1,0:T(1,128)} %copy-done.44) | copy-start | bytes 12292
  268.2 74.2 %copy-start.47 = (f32[1,1,1024]{2,1,0:T(1,128)S(1)}, f32[1,1,1024]{2,1,0:T(1,128)}, u32[]{:S(2)}) copy-start(f32[1,1,1024]{2,1,0:T(1,128)} %copy-done.46) | copy-start | bytes 12292
  268.2 74.2 %copy-start.49 = (f32[1,1,1024]{2,1,0:T(1,128)S(1)}, f32[1,1,1024]{2,1,0:T(1,128)}, u32[]{:S(2)}) copy-start(f32[1,1,1024]{2,1,0:T(1,128)} %copy-done.48) | copy-start | bytes 12292
  268.2 74.2 %copy-start.51 = (f32[1,1,1024]{2,1,0:T(1,128)S(1)}, f32[1,1,1024]{2,1,0:T(1,128)}, u32[]{:S(2)}) copy-start(f32[1,1,1024]{2,1,0:T(1,128)} %copy-done.50) | copy-start | bytes 12292
  271.5 3.9 %collective-permute-start.13 = (f32[16,8,1024]{2,1,0:T(8,128)S(1)}, f32[16,8,1024]{2,1,0:T(8,128)S(1)}, u32[]{:S(2)}, u32[]{:S(2)}) collective-permute-start(f32[16,8,1024]{2,1,0:T(8,128)S(1)} %dynamic-slice_bitcast_fusion), channel_id=1, source_target_pairs={{0,1},{1,0},{2,3},{3,2},{4,5},{5,4},{6,7},{7,6},{8,9},{9,8},{10,11... | collective-permute-start | bytes 1572872 | tf_op jit(solution)/shard_map/ppermute | solution.py:56
  275.6 10.5 %collective-permute-start.14 = (f32[8,8,1024]{2,1,0:T(8,128)S(1)}, f32[8,8,1024]{2,1,0:T(8,128)S(1)}, u32[]{:S(2)}, u32[]{:S(2)}) collective-permute-start(f32[8,8,1024]{2,1,0:T(8,128)S(1)} %dynamic-slice_bitcast_fusion.1), channel_id=1, source_target_pairs={{0,2},{1,3},{2,0},{3,1},{4,6},{5,7},{6,4},{7,5},{8,10},{9,11},{10,... | collective-permute-start | bytes 786440 | tf_op jit(solution)/shard_map/ppermute | solution.py:56
  286.1 10.5 %collective-permute-start.15 = (f32[4,8,1024]{2,1,0:T(8,128)S(1)}, f32[4,8,1024]{2,1,0:T(8,128)S(1)}, u32[]{:S(2)}, u32[]{:S(2)}) collective-permute-start(f32[4,8,1024]{2,1,0:T(8,128)S(1)} %dynamic-slice_bitcast_fusion.2), channel_id=1, source_target_pairs={{0,4},{1,5},{2,6},{3,7},{4,0},{5,1},{6,2},{7,3},{8,12},{9,13},{10,... | collective-permute-start | bytes 393224 | tf_op jit(solution)/shard_map/ppermute | solution.py:56
  296.7 10.5 %collective-permute-start.16 = (f32[2,8,1024]{2,1,0:T(8,128)S(1)}, f32[2,8,1024]{2,1,0:T(8,128)S(1)}, u32[]{:S(2)}, u32[]{:S(2)}) collective-permute-start(f32[2,8,1024]{2,1,0:T(8,128)S(1)} %dynamic-slice_bitcast_fusion.3), channel_id=1, source_target_pairs={{0,8},{1,9},{2,10},{3,11},{4,12},{5,13},{6,14},{7,15},{8,0},{9,1},... | collective-permute-start | bytes 196616 | tf_op jit(solution)/shard_map/ppermute | solution.py:56
  307.2 7.3 %collective-permute-start.17 = (f32[1,8,1024]{2,1,0:T(8,128)S(1)}, f32[1,8,1024]{2,1,0:T(8,128)S(1)}, u32[]{:S(2)}, u32[]{:S(2)}) collective-permute-start(f32[1,8,1024]{2,1,0:T(8,128)S(1)} %constant_dynamic-slice_fusion), channel_id=1, source_target_pairs={{0,16},{1,17},{2,18},{3,19},{4,20},{5,21},{6,22},{7,23},{8,24},{9,... | collective-permute-start | bytes 98312 | tf_op jit(solution)/shard_map/ppermute | solution.py:56
  314.5 12.2 %collective-permute-start.18 = (f32[1,8,1024]{2,1,0:T(8,128)S(1)}, f32[1,8,1024]{2,1,0:T(8,128)S(1)}, u32[]{:S(2)}, u32[]{:S(2)}) collective-permute-start(f32[1,8,1024]{2,1,0:T(8,128)S(1)} %dynamic-slice_add_fusion), channel_id=1, source_target_pairs={{0,384},{32,416},{64,448},{96,480},{128,256},{160,288},{192,320},{... | collective-permute-start | bytes 98312 | tf_op jit(solution)/shard_map/ppermute | solution.py:29
  317.8 9.7 %collective-permute-start.19 = (f32[1,8,1024]{2,1,0:T(8,128)S(1)}, f32[1,8,1024]{2,1,0:T(8,128)S(1)}, u32[]{:S(2)}, u32[]{:S(2)}) collective-permute-start(f32[1,8,1024]{2,1,0:T(8,128)S(1)} %dynamic-slice_add_fusion), channel_id=1, source_target_pairs={{0,256},{32,288},{64,320},{96,352},{128,384},{160,416},{192,448},{... | collective-permute-start | bytes 98312 | tf_op jit(solution)/shard_map/ppermute | solution.py:29
  322.2 6.7 %collective-permute-start.20 = (f32[1,8,1024]{2,1,0:T(8,128)S(1)}, f32[1,8,1024]{2,1,0:T(8,128)S(1)}, u32[]{:S(2)}, u32[]{:S(2)}) collective-permute-start(f32[1,8,1024]{2,1,0:T(8,128)S(1)} %dynamic-slice_add_fusion), channel_id=1, source_target_pairs={{0,128},{32,160},{64,192},{96,224},{128,0},{160,32},{192,64},{224,... | collective-permute-start | bytes 98312 | tf_op jit(solution)/shard_map/ppermute | solution.py:29
  328.9 10.3 %collective-permute-start.21 = (f32[2,2,1,8,1024]{4,3,1,0,2:T(8,128)S(1)}, f32[2,2,1,8,1024]{4,3,1,0,2:T(8,128)S(1)}, u32[]{:S(2)}, u32[]{:S(2)}) collective-permute-start(f32[2,2,1,8,1024]{4,3,1,0,2:T(8,128)S(1)} %bitcast.657), channel_id=1, source_target_pairs={{0,96},{32,64},{64,32},{96,0},{128,224},{160,192},{192,160},{224,1... | collective-permute-start | bytes 393224 | tf_op jit(solution)/shard_map/ppermute | solution.py:29
  332.8 6.9 %collective-permute-start.22 = (f32[2,2,1,8,1024]{4,3,1,0,2:T(8,128)S(1)}, f32[2,2,1,8,1024]{4,3,1,0,2:T(8,128)S(1)}, u32[]{:S(2)}, u32[]{:S(2)}) collective-permute-start(f32[2,2,1,8,1024]{4,3,1,0,2:T(8,128)S(1)} %bitcast.658), channel_id=1, source_target_pairs={{0,64},{32,96},{64,0},{96,32},{128,192},{160,224},{192,128},{224,1... | collective-permute-start | bytes 393224 | tf_op jit(solution)/shard_map/ppermute | solution.py:29
  335.2 6.9 %collective-permute-start.23 = (f32[2,2,1,8,1024]{4,3,1,0,2:T(8,128)S(1)}, f32[2,2,1,8,1024]{4,3,1,0,2:T(8,128)S(1)}, u32[]{:S(2)}, u32[]{:S(2)}) collective-permute-start(f32[2,2,1,8,1024]{4,3,1,0,2:T(8,128)S(1)} %bitcast.659), channel_id=1, source_target_pairs={{0,32},{32,0},{64,96},{96,64},{128,160},{160,128},{192,224},{224,1... | collective-permute-start | bytes 393224 | tf_op jit(solution)/shard_map/ppermute | solution.py:29
  (28 other events, 164.8 us)
Sparse Core Ops, SparseCore 0:
  11.7 117.0 all-gather.1

commit v4 on v0

--- a/solution.py
+++ b/solution.py
@@ -162,7 +162,7 @@
         )
         running = (seg_top, seg_total, seg_acc)
 
-    memory_all = gathered(memory_in.astype(jnp.bfloat16), "tok", ((3, 4), (1, 2), (0,))).reshape(
+    memory_all = gathered(memory_in.astype(jnp.bfloat16), "tok", ((4,), (3,), (2,), (1,), (0,))).reshape(
         -1, 2 * width_kv
     )
     mem_keys = memory_all[:, :width_kv].reshape(-1, KVH, HD)

time: 349 us -> 351 us (level)
  starting transfers between devices: 97.4 us -> 87.3 us
  waiting for transfers between devices: 132 us -> 141 us
    ppermute x19 -> x17, starting transfers between devices: 70.2 us -> 60.1 us  [gathered(): lax.ppermute(held, axis, [(i, i ^ flip) for i in range(size)])]
    all_gather x1, waiting for transfers between devices: 107 us -> 113 us  [shards(): lax.all_gather(jnp.concatenate([seg_keys[0], seg_values[0]], axis=1), 'to...]
    ppermute x19 -> x17, waiting for transfers between devices: 11.8 us -> 15.7 us  [gathered(): lax.ppermute(held, axis, [(i, i ^ flip) for i in range(size)])]
  transfers between devices with their start and end apart: 27 -> 25, of which waited for: 13 -> 13; matrix products, arithmetic and copies ran while one was open for 10% -> 10% of each run, Pallas kernels for 0% -> 0%
where the time goes in v4:
time: 351 us; the launch traced here: 350 us
  waiting for transfers between devices  141 us (40%)
  starting transfers between devices  87.3 us (25%)
  matrix products  52.9 us (15%)
  other arithmetic  26.4 us (8%)
  local copies, waits for them, and re-layouts  25.9 us (7%)
  between operations  16.3 us (5%)
    all_gather x1, waiting for transfers between devices, shards(): lax.all_gather(jnp.concatenate([seg_keys[0], seg_values[0]], axis=1), 'to...  113 us
    ppermute x17, starting transfers between devices, gathered(): lax.ppermute(held, axis, [(i, i ^ flip) for i in range(size)])  60.1 us
    ppermute x7, starting transfers between devices, scattered_sum(): lax.ppermute(send, axis, [(i, i ^ flip) for i in range(size)])  27.1 us
    dot_general x4, matrix products, shards(): jnp.einsum('tgjd,ugd->gjtu', queries, key_block, preferred_element_type=j...  20.6 us
    dot_general x4, matrix products, shards(): jnp.einsum('gjtu,ugd->tgjd', seg_weights, value_block, preferred_element_...  16.5 us
    ppermute x17, waiting for transfers between devices, gathered(): lax.ppermute(held, axis, [(i, i ^ flip) for i in range(size)])  15.7 us
    reduce_sum x4, other arithmetic, softmax_step(): new_total = row_total * multiplier + jnp.sum(weights, axis=-1)  13.4 us
    ppermute x7, waiting for transfers between devices, scattered_sum(): lax.ppermute(send, axis, [(i, i ^ flip) for i in range(size)])  12.5 us
  transfers between devices with their start and end apart: 25, of which 13 were waited for; matrix products, arithmetic and copies ran while one was open for 10% of the time, Pallas kernels for 0%

profile of v4, /device:TPU:2, one launch (start us, length us, event | category | flops | bytes accessed | tf_op | source)
XLA Modules:
  0.0 350.1 jit_solution(10024102139230311221)
XLA Ops:
  10.0 1.2 dynamic_slice.32
  12.0 1.2 dynamic_slice.31
  15.9 112.9 %all-gather.2.cloned.1.call-done = bf16[4096,1024]{0,1:T(8,128)(2,1)} async-done(((bf16[128,1024]{0,1:T(8,128)(2,1)}), bf16[4096,1024]{0,1:T(8,128)(2,1)}) %all-gather.2.cloned.1.call-update) | async-done | bytes 8388624 | tf_op jit(solution)/shard_map/all_gather | solution.py:93
  128.8 6.1 %fusion.185 = (bf16[4096,512]{0,1:T(8,128)(2,1)}, bf16[4096,512]{0,1:T(8,128)(2,1)}) fusion(bf16[4096,1024]{0,1:T(8,128)(2,1)} %all-gather.2.cloned.1.call-done), kind=kLoop, calls=%fused_computation.284 | loop fusion | bytes 16777216 | tf_op jit(solution)/shard_map/slice | solution.py:97
  134.9 3.2 fusion.188
  138.1 3.4 fusion.80
  141.5 3.4 fusion.79
  145.1 6.6 %collective-permute-start = (f32[1,9,1024]{2,1,0:T(8,128)S(1)}, f32[1,9,1024]{2,1,0:T(8,128)S(1)}, u32[]{:S(2)}, u32[]{:S(2)}) collective-permute-start(f32[1,9,1024]{2,1,0:T(8,128)S(1)} %maximum_bitcast_fusion), channel_id=1, source_target_pairs={{0,384},{32,416},{64,448},{96,480},{128,256},{160,288},{192,320},{... | collective-permute-start | bytes 110600 | tf_op jit(solution)/shard_map/ppermute | solution.py:29
  151.7 3.5 %collective-permute-start.1 = (f32[1,9,1024]{2,1,0:T(8,128)S(1)}, f32[1,9,1024]{2,1,0:T(8,128)S(1)}, u32[]{:S(2)}, u32[]{:S(2)}) collective-permute-start(f32[1,9,1024]{2,1,0:T(8,128)S(1)} %maximum_bitcast_fusion), channel_id=1, source_target_pairs={{0,256},{32,288},{64,320},{96,352},{128,384},{160,416},{192,448},{... | collective-permute-start | bytes 110600 | tf_op jit(solution)/shard_map/ppermute | solution.py:29
  155.2 2.7 collective-permute-start.2
  157.9 4.7 %collective-permute-done.1 = f32[1,9,1024]{2,1,0:T(8,128)S(1)} collective-permute-done((f32[1,9,1024]{2,1,0:T(8,128)S(1)}, f32[1,9,1024]{2,1,0:T(8,128)S(1)}, u32[]{:S(2)}, u32[]{:S(2)}) %collective-permute-start.1) | collective-permute-done | bytes 36896 | tf_op jit(solution)/shard_map/ppermute | solution.py:29
  162.7 1.8 collective-permute-done.2
  164.5 2.3 collective-permute-start.3
  166.8 4.4 %collective-permute-start.4 = (f32[2,2,1,9,1024]{4,3,1,0,2:T(8,128)S(1)}, f32[2,2,1,9,1024]{4,3,1,0,2:T(8,128)S(1)}, u32[]{:S(2)}, u32[]{:S(2)}) collective-permute-start(f32[2,2,1,9,1024]{4,3,1,0,2:T(8,128)S(1)} %bitcast.638), channel_id=1, source_target_pairs={{0,64},{32,96},{64,0},{96,32},{128,192},{160,224},{192,128},{224,1... | collective-permute-start | bytes 442376 | tf_op jit(solution)/shard_map/ppermute | solution.py:29
  171.3 2.5 collective-permute-start.5
  173.8 2.2 compare_and_fusion.1
  176.6 1.2 compare_convert_fusion
  177.8 3.2 collective-permute-done.4
  181.7 1.3 select_bitcast_fusion.5
  183.4 1.5 convert_bitcast_fusion
  184.9 2.7 collective-permute-start.6
  187.6 5.3 %fusion.184 = (bf16[1024,512]{0,1:T(8,128)(2,1)}, bf16[1024,512]{0,1:T(8,128)(2,1)S(1)}, bf16[1024,512]{0,1:T(8,128)(2,1)}, bf16[1024,512]{0,1:T(8,128)(2,1)S(1)...) fusion(bf16[4096,1024]{0,1:T(8,128)(2,1)} %all-gather.2.cloned., ...), kind=kLoop, calls=%fused_computation.283 | loop fusion | bytes 16777216 | tf_op jit(solution)/shard_map/slice | solution.py:150
  193.1 4.5 %collective-permute-start.7 = (bf16[2,1,8,1024]{3,2,0,1:T(8,128)(2,1)S(1)}, bf16[2,1,8,1024]{3,2,0,1:T(8,128)(2,1)S(1)}, u32[]{:S(2)}, u32[]{:S(2)}) collective-permute-start(bf16[2,1,8,1024]{3,2,0,1:T(8,128)(2,1)S(1)} %pad_maximum_fusion.10), channel_id=1, source_target_pairs={{0,8},{1,9},{2,10},{3,11},{4,12},{5,13},{6,14},{7,15},{8,0},{9,1},... | collective-permute-start | bytes 98312 | tf_op jit(solution)/shard_map/ppermute | solution.py:29
  197.6 4.9 %fusion.4 = (f32[4,4,128]{2,1,0:T(4,128)S(1)}, f32[4,1024,128,4]{2,1,3,0:T(8,128)}) fusion(pred[128,1024]{0,1:T(8,128)(4,1)S(1)} %get-tuple-element.86, bf16[1024,4,128,1]{0,2,3,1:T(8,128)(2,1)S(1)} %bitcast.622, bf16[128,4,4,128]{3,2,1,0:T(4,128)(2,1)S(1)} %reshape_squeeze.3), kind=kOutput, calls=%fused_computation.12 | convolution fusion | flops 543160320 | bytes 10100736 | tf_op jit(solution)/shard_map/tgjd,ugd->gjtu/dot_general | solution.py:154
  202.9 2.7 collective-permute-start.8
  205.6 5.5 %fusion.3 = (f32[4,4,128]{2,1,0:T(4,128)}, f32[4,1024,128,4]{2,1,3,0:T(8,128)}) fusion(pred[128,1024]{0,1:T(8,128)(4,1)S(1)} %get-tuple-element.85, bf16[1024,4,128,1]{0,2,3,1:T(8,128)(2,1)S(1)} %bitcast.621, bf16[128,4,4,128]{3,2,1,0:T(4,128)(2,1)S(1)} %reshape_squeeze.3), kind=kOutput, calls=%fused_computation.11 | convolution fusion | flops 543160320 | bytes 10100736 | tf_op jit(solution)/shard_map/tgjd,ugd->gjtu/dot_general | solution.py:154
  211.1 4.7 %collective-permute-start.9 = (bf16[2,2,2,1,8,1024]{5,4,0,1,2,3:T(8,128)(2,1)S(1)}, bf16[2,2,2,1,8,1024]{5,4,0,1,2,3:T(8,128)(2,1)S(1)}, u32[]{:S(2)}, u32[]{:S(2)}) collective-permute-start(bf16[2,2,2,1,8,1024]{5,4,0,1,2,3:T(8,128)(2,1)S(1)} %pad_maximum_fusion.6), channel_id=1, source_target_pairs={{0,2},{1,3},{2,0},{3,1},{4,6},{5,7},{6,4},{7,5},{8,10},{9,11},{10,... | collective-permute-start | bytes 393224 | tf_op jit(solution)/shard_map/ppermute | solution.py:29
  215.8 5.5 %fusion.2 = (f32[4,4,128]{2,1,0:T(4,128)}, f32[4,1024,128,4]{2,1,3,0:T(8,128)}) fusion(pred[128,1024]{0,1:T(8,128)(4,1)S(1)} %get-tuple-element.87, bf16[1024,4,128,1]{0,2,3,1:T(8,128)(2,1)S(1)} %bitcast.620, bf16[128,4,4,128]{3,2,1,0:T(4,128)(2,1)S(1)} %reshape_squeeze.3), kind=kOutput, calls=%fused_computation.10 | convolution fusion | flops 543160320 | bytes 10100736 | tf_op jit(solution)/shard_map/tgjd,ugd->gjtu/dot_general | solution.py:154
  221.4 2.1 collective-permute-start.10
  223.5 4.8 %fusion.1 = (f32[4,4,128]{2,1,0:T(4,128)S(1)}, f32[4,1024,128,4]{2,1,3,0:T(8,128)}) fusion(pred[128,1024]{0,1:T(8,128)(4,1)S(1)} %copy-done.2, bf16[1024,4,128,1]{0,2,3,1:T(8,128)(2,1)S(1)} %bitcast.619, bf16[128,4,4,128]{3,2,1,0:T(4,128)(2,1)S(1)} %reshape_squeeze.3), kind=kOutput, calls=%fused_computation.9 | convolution fusion | flops 543160320 | bytes 10100736 | tf_op jit(solution)/shard_map/tgjd,ugd->gjtu/dot_general | solution.py:154
  230.0 1.5 bitcast_reduce_fusion
  232.5 4.6 %fusion.11 = f32[4,4,128]{2,1,0:T(4,128)S(1)} fusion(f32[4,1024,128,4]{2,1,3,0:T(8,128)} %get-tuple-element.94, f32[4,4,128]{2,1,0:T(4,128)S(1)} %get-tuple-element.17, pred[128,1024]{0,1:T(8,128)(4,1)S(1)} %get-tuple-element.86), kind=kLoop, calls=%fused_computation.19 | loop fusion | flops 10483712 | bytes 8536064 | tf_op jit(solution)/shard_map/reduce_sum | solution.py:73
  237.2 4.8 %fusion.9 = f32[4,4,128]{2,1,0:T(4,128)S(1)} fusion(f32[4,1024,128,4]{2,1,3,0:T(8,128)} %get-tuple-element.96, f32[4,4,128]{2,1,0:T(4,128)S(1)} %get-tuple-element.18, pred[128,1024]{0,1:T(8,128)(4,1)S(1)} %get-tuple-element.85), kind=kLoop, calls=%fused_computation.17 | loop fusion | flops 10483712 | bytes 8536064 | tf_op jit(solution)/shard_map/reduce_sum | solution.py:73
  242.3 2.0 fusion.7
  244.3 2.0 fusion.5
  247.1 1.8 copy.110
  248.9 5.9 %fusion.64 = f32[128,4,4,128]{0,3,2,1:T(8,128)S(1)} fusion(bf16[1024,4,128,1]{0,2,3,1:T(8,128)(2,1)} %bitcast.636, f32[4,1024,128,4]{2,1,3,0:T(8,128)} %get-tuple-element.100, f32[4,4,128]{2,1,0:T(4,128)} %copy-done.54, pred[128,1024]{0,1:T(8,128)(4,1)} %get-tuple-element.88, f32[128,4,4]{0,2,1:T(4,128)} %get-tuple-element.80, ...), kind=kOutput, calls=%fused_computation.59 | convolution fusion | flops 547880960 | bytes 10641408 | tf_op jit(solution)/shard_map/gjtu,ugd->tgjd/dot_general | solution.py:160
  254.9 5.7 %fusion.67 = f32[128,4,4,128]{0,3,2,1:T(8,128)S(1)} fusion(f32[128,4,4,128]{0,3,2,1:T(8,128)S(1)} %fusion.64, bf16[1024,4,128,1]{0,2,3,1:T(8,128)(2,1)S(1)} %bitcast.635, f32[4,1024,128,4]{2,1,3,0:T(8,128)} %get-tuple-element.98, f32[4,4,128]{2,1,0:T(4,128)S(1)} %copy-done.23, pred[128,1024]{0,1:T(8,128)(4,1)S(1)} %get-tuple-element.87, ...), kind=kOutput, calls=%fused_computation.60 | convolution fusion | flops 547880960 | bytes 11681792 | tf_op jit(solution)/shard_map/gjtu,ugd->tgjd/dot_general | solution.py:160
  260.7 2.4 fusion.70
  263.2 2.6 fusion.73
  265.8 1.4 fusion.189
  267.4 1.3 convolution_bitcast_fusion.1
  268.6 1.8 fusion.78
  270.6 1.5 copy.116
  272.3 1.3 copy.118
  273.9 2.4 collective-permute-start.11
  276.3 1.5 collective-permute-done.11
  277.9 2.8 collective-permute-start.14
  280.8 2.5 collective-permute-start.13
  283.2 4.8 %collective-permute-start.12 = (f32[4,8,1024]{2,1,0:T(8,128)S(1)}, f32[4,8,1024]{2,1,0:T(8,128)S(1)}, u32[]{:S(2)}, u32[]{:S(2)}) collective-permute-start(f32[4,8,1024]{2,1,0:T(8,128)S(1)} %get-tuple-element.55), channel_id=1, source_target_pairs={{0,2},{1,3},{2,0},{3,1},{4,6},{5,7},{6,4},{7,5},{8,10},{9,11},{10,... | collective-permute-start | bytes 393224 | tf_op jit(solution)/shard_map/ppermute | solution.py:56
  288.1 5.5 %collective-permute-done.13 = f32[4,8,1024]{2,1,0:T(8,128)S(1)} collective-permute-done((f32[4,8,1024]{2,1,0:T(8,128)S(1)}, f32[4,8,1024]{2,1,0:T(8,128)S(1)}, u32[]{:S(2)}, u32[]{:S(2)}) %collective-permute-start.13) | collective-permute-done | bytes 131104 | tf_op jit(solution)/shard_map/ppermute | solution.py:56
  294.4 6.9 %collective-permute-start.17 = (f32[1,8,1024]{2,1,0:T(8,128)S(1)}, f32[1,8,1024]{2,1,0:T(8,128)S(1)}, u32[]{:S(2)}, u32[]{:S(2)}) collective-permute-start(f32[1,8,1024]{2,1,0:T(8,128)S(1)} %get-tuple-element.72), channel_id=1, source_target_pairs={{0,24},{1,25},{2,26},{3,27},{4,28},{5,29},{6,30},{7,31},{8,16},{9,... | collective-permute-start | bytes 98312 | tf_op jit(solution)/shard_map/ppermute | solution.py:56
  301.3 2.8 collective-permute-start.16
  304.1 4.9 %collective-permute-start.15 = (f32[1,8,1024]{2,1,0:T(8,128)S(1)}, f32[1,8,1024]{2,1,0:T(8,128)S(1)}, u32[]{:S(2)}, u32[]{:S(2)}) collective-permute-start(f32[1,8,1024]{2,1,0:T(8,128)S(1)} %get-tuple-element.71), channel_id=1, source_target_pairs={{0,8},{1,9},{2,10},{3,11},{4,12},{5,13},{6,14},{7,15},{8,0},{9,1},... | collective-permute-start | bytes 98312 | tf_op jit(solution)/shard_map/ppermute | solution.py:56
  309.1 4.8 %collective-permute-done.15 = f32[1,8,1024]{2,1,0:T(8,128)S(1)} collective-permute-done((f32[1,8,1024]{2,1,0:T(8,128)S(1)}, f32[1,8,1024]{2,1,0:T(8,128)S(1)}, u32[]{:S(2)}, u32[]{:S(2)}) %collective-permute-start.15) | collective-permute-done | bytes 32800 | tf_op jit(solution)/shard_map/ppermute | solution.py:56
  313.8 3.2 collective-permute-start.18
  317.0 4.4 %collective-permute-start.19 = (f32[1,8,1024]{2,1,0:T(8,128)S(1)}, f32[1,8,1024]{2,1,0:T(8,128)S(1)}, u32[]{:S(2)}, u32[]{:S(2)}) collective-permute-start(f32[1,8,1024]{2,1,0:T(8,128)S(1)} %add_add_fusion), channel_id=1, source_target_pairs={{0,256},{32,288},{64,320},{96,352},{128,384},{160,416},{192,448},{... | collective-permute-start | bytes 98312 | tf_op jit(solution)/shard_map/ppermute | solution.py:29
  321.5 4.6 %collective-permute-start.20 = (f32[1,8,1024]{2,1,0:T(8,128)S(1)}, f32[1,8,1024]{2,1,0:T(8,128)S(1)}, u32[]{:S(2)}, u32[]{:S(2)}) collective-permute-start(f32[1,8,1024]{2,1,0:T(8,128)S(1)} %add_add_fusion), channel_id=1, source_target_pairs={{0,128},{32,160},{64,192},{96,224},{128,0},{160,32},{192,64},{224,... | collective-permute-start | bytes 98312 | tf_op jit(solution)/shard_map/ppermute | solution.py:29
  326.7 1.4 collective-permute-done.20
  328.2 4.5 %collective-permute-start.21 = (f32[2,2,1,8,1024]{4,3,1,0,2:T(8,128)S(1)}, f32[2,2,1,8,1024]{4,3,1,0,2:T(8,128)S(1)}, u32[]{:S(2)}, u32[]{:S(2)}) collective-permute-start(f32[2,2,1,8,1024]{4,3,1,0,2:T(8,128)S(1)} %bitcast.645), channel_id=1, source_target_pairs={{0,96},{32,64},{64,32},{96,0},{128,224},{160,192},{192,160},{224,1... | collective-permute-start | bytes 393224 | tf_op jit(solution)/shard_map/ppermute | solution.py:29
  332.8 2.5 collective-permute-start.22
  335.3 2.2 collective-permute-start.23
  338.5 1.1 collective-permute-done.22
  339.6 2.5 collective-permute-done.23
  (215 shorter events, 16.2 us)
Async XLA Ops:
  7.2 127.7 %copy-start = (bf16[8,512]{1,0:T(8,128)(2,1)S(1)}, bf16[8,512]{1,0:T(8,128)(2,1)}, u32[]{:S(2)}) copy-start(bf16[8,512]{1,0:T(8,128)(2,1)} %param.14) | copy-start | bytes 24580
  7.2 121.6 %all-gather.2.cloned.1.call-start = ((), (), s32[]{:S(2)}) async-start(), calls=%async_computation | async-start | bytes 8650752 | tf_op jit(solution)/shard_map/all_gather | solution.py:93
  134.9 10.1 %copy-start.13 = (f32[8,1024]{1,0:T(8,128)S(1)}, f32[8,1024]{1,0:T(8,128)}, u32[]{:S(2)}) copy-start(f32[8,1024]{1,0:T(8,128)} %param.13) | copy-start | bytes 98308
  134.9 41.1 %copy-start.7 = (bf16[1,128,2048]{2,1,0:T(8,128)(2,1)S(1)}, bf16[1,128,2048]{2,1,0:T(8,128)(2,1)}, u32[]{:S(2)}) copy-start(bf16[1,128,2048]{2,1,0:T(8,128)(2,1)} %param.9) | copy-start | bytes 1572868
  134.9 41.4 %copy-start.8 = (bf16[1,128,2048]{2,1,0:T(8,128)(2,1)S(1)}, bf16[1,128,2048]{2,1,0:T(8,128)(2,1)}, u32[]{:S(2)}) copy-start(bf16[1,128,2048]{2,1,0:T(8,128)(2,1)} %param.12) | copy-start | bytes 1572868
  145.1 12.8 %collective-permute-start = (f32[1,9,1024]{2,1,0:T(8,128)S(1)}, f32[1,9,1024]{2,1,0:T(8,128)S(1)}, u32[]{:S(2)}, u32[]{:S(2)}) collective-permute-start(f32[1,9,1024]{2,1,0:T(8,128)S(1)} %maximum_bitcast_fusion), channel_id=1, source_target_pairs={{0,384},{32,416},{64,448},{96,480},{128,256},{160,288},{192,320},{... | collective-permute-start | bytes 110600 | tf_op jit(solution)/shard_map/ppermute | solution.py:29
  151.7 11.0 %collective-permute-start.1 = (f32[1,9,1024]{2,1,0:T(8,128)S(1)}, f32[1,9,1024]{2,1,0:T(8,128)S(1)}, u32[]{:S(2)}, u32[]{:S(2)}) collective-permute-start(f32[1,9,1024]{2,1,0:T(8,128)S(1)} %maximum_bitcast_fusion), channel_id=1, source_target_pairs={{0,256},{32,288},{64,320},{96,352},{128,384},{160,416},{192,448},{... | collective-permute-start | bytes 110600 | tf_op jit(solution)/shard_map/ppermute | solution.py:29
  155.2 9.2 %collective-permute-start.2 = (f32[1,9,1024]{2,1,0:T(8,128)S(1)}, f32[1,9,1024]{2,1,0:T(8,128)S(1)}, u32[]{:S(2)}, u32[]{:S(2)}) collective-permute-start(f32[1,9,1024]{2,1,0:T(8,128)S(1)} %maximum_bitcast_fusion), channel_id=1, source_target_pairs={{0,128},{32,160},{64,192},{96,224},{128,0},{160,32},{192,64},{224,... | collective-permute-start | bytes 110600 | tf_op jit(solution)/shard_map/ppermute | solution.py:29
  164.5 13.3 %collective-permute-start.3 = (f32[2,2,1,9,1024]{4,3,1,0,2:T(8,128)S(1)}, f32[2,2,1,9,1024]{4,3,1,0,2:T(8,128)S(1)}, u32[]{:S(2)}, u32[]{:S(2)}) collective-permute-start(f32[2,2,1,9,1024]{4,3,1,0,2:T(8,128)S(1)} %bitcast.637), channel_id=1, source_target_pairs={{0,96},{32,64},{64,32},{96,0},{128,224},{160,192},{192,160},{224,1... | collective-permute-start | bytes 442376 | tf_op jit(solution)/shard_map/ppermute | solution.py:29
  166.8 14.1 %collective-permute-start.4 = (f32[2,2,1,9,1024]{4,3,1,0,2:T(8,128)S(1)}, f32[2,2,1,9,1024]{4,3,1,0,2:T(8,128)S(1)}, u32[]{:S(2)}, u32[]{:S(2)}) collective-permute-start(f32[2,2,1,9,1024]{4,3,1,0,2:T(8,128)S(1)} %bitcast.638), channel_id=1, source_target_pairs={{0,64},{32,96},{64,0},{96,32},{128,192},{160,224},{192,128},{224,1... | collective-permute-start | bytes 442376 | tf_op jit(solution)/shard_map/ppermute | solution.py:29
  171.3 10.4 %collective-permute-start.5 = (f32[2,2,1,9,1024]{4,3,1,0,2:T(8,128)S(1)}, f32[2,2,1,9,1024]{4,3,1,0,2:T(8,128)}, u32[]{:S(2)}, u32[]{:S(2)}) collective-permute-start(f32[2,2,1,9,1024]{4,3,1,0,2:T(8,128)S(1)} %bitcast.639), channel_id=1, source_target_pairs={{0,32},{32,0},{64,96},{96,64},{128,160},{160,128},{192,224},{224,1... | collective-permute-start | bytes 442376 | tf_op jit(solution)/shard_map/ppermute | solution.py:29
  183.2 9.8 %copy-start.24 = (f32[1,1,1024]{2,1,0:T(1,128)}, f32[1,1,1024]{2,1,0:T(1,128)S(1)}, u32[]{:S(2)}) copy-start(f32[1,1,1024]{2,1,0:T(1,128)S(1)} %get-tuple-element.32) | copy-start | bytes 12292
  183.2 9.7 %copy-start.26 = (f32[1,1,1024]{2,1,0:T(1,128)}, f32[1,1,1024]{2,1,0:T(1,128)S(1)}, u32[]{:S(2)}) copy-start(f32[1,1,1024]{2,1,0:T(1,128)S(1)} %get-tuple-element.33) | copy-start | bytes 12292
  183.2 9.7 %copy-start.28 = (f32[1,1,1024]{2,1,0:T(1,128)}, f32[1,1,1024]{2,1,0:T(1,128)S(1)}, u32[]{:S(2)}) copy-start(f32[1,1,1024]{2,1,0:T(1,128)S(1)} %get-tuple-element.34) | copy-start | bytes 12292
  183.2 9.7 %copy-start.30 = (f32[1,1,1024]{2,1,0:T(1,128)}, f32[1,1,1024]{2,1,0:T(1,128)S(1)}, u32[]{:S(2)}) copy-start(f32[1,1,1024]{2,1,0:T(1,128)S(1)} %get-tuple-element.35) | copy-start | bytes 12292
  183.2 9.7 %copy-start.32 = (f32[1,1,1024]{2,1,0:T(1,128)}, f32[1,1,1024]{2,1,0:T(1,128)S(1)}, u32[]{:S(2)}) copy-start(f32[1,1,1024]{2,1,0:T(1,128)S(1)} %get-tuple-element.36) | copy-start | bytes 12292
  183.3 9.7 %copy-start.34 = (f32[1,1,1024]{2,1,0:T(1,128)}, f32[1,1,1024]{2,1,0:T(1,128)S(1)}, u32[]{:S(2)}) copy-start(f32[1,1,1024]{2,1,0:T(1,128)S(1)} %get-tuple-element.37) | copy-start | bytes 12292
  183.3 9.7 %copy-start.36 = (f32[1,1,1024]{2,1,0:T(1,128)}, f32[1,1,1024]{2,1,0:T(1,128)S(1)}, u32[]{:S(2)}) copy-start(f32[1,1,1024]{2,1,0:T(1,128)S(1)} %get-tuple-element.38) | copy-start | bytes 12292
  183.3 9.7 %copy-start.38 = (f32[1,1,1024]{2,1,0:T(1,128)}, f32[1,1,1024]{2,1,0:T(1,128)S(1)}, u32[]{:S(2)}) copy-start(f32[1,1,1024]{2,1,0:T(1,128)S(1)} %get-tuple-element.39) | copy-start | bytes 12292
  183.3 9.7 %copy-start.40 = (f32[1,1,1024]{2,1,0:T(1,128)}, f32[1,1,1024]{2,1,0:T(1,128)S(1)}, u32[]{:S(2)}) copy-start(f32[1,1,1024]{2,1,0:T(1,128)S(1)} %get-tuple-element.40) | copy-start | bytes 12292
  183.3 9.7 %copy-start.42 = (f32[1,1,1024]{2,1,0:T(1,128)}, f32[1,1,1024]{2,1,0:T(1,128)S(1)}, u32[]{:S(2)}) copy-start(f32[1,1,1024]{2,1,0:T(1,128)S(1)} %get-tuple-element.41) | copy-start | bytes 12292
  184.9 8.2 %collective-permute-start.6 = (bf16[1,8,1024]{2,1,0:T(8,128)(2,1)S(1)}, bf16[1,8,1024]{2,1,0:T(8,128)(2,1)S(1)}, u32[]{:S(2)}, u32[]{:S(2)}) collective-permute-start(bf16[1,8,1024]{2,1,0:T(8,128)(2,1)S(1)} %get-tuple-element.20), channel_id=1, source_target_pairs={{0,16},{1,17},{2,18},{3,19},{4,20},{5,21},{6,22},{7,23},{8,24},{9,... | collective-permute-start | bytes 49160 | tf_op jit(solution)/shard_map/ppermute | solution.py:29
  193.1 9.7 %collective-permute-start.7 = (bf16[2,1,8,1024]{3,2,0,1:T(8,128)(2,1)S(1)}, bf16[2,1,8,1024]{3,2,0,1:T(8,128)(2,1)S(1)}, u32[]{:S(2)}, u32[]{:S(2)}) collective-permute-start(bf16[2,1,8,1024]{3,2,0,1:T(8,128)(2,1)S(1)} %pad_maximum_fusion.10), channel_id=1, source_target_pairs={{0,8},{1,9},{2,10},{3,11},{4,12},{5,13},{6,14},{7,15},{8,0},{9,1},... | collective-permute-start | bytes 98312 | tf_op jit(solution)/shard_map/ppermute | solution.py:29
  202.9 8.1 %collective-permute-start.8 = (bf16[2,2,1,8,1024]{4,3,0,1,2:T(8,128)(2,1)S(1)}, bf16[2,2,1,8,1024]{4,3,0,1,2:T(8,128)(2,1)S(1)}, u32[]{:S(2)}, u32[]{:S(2)}) collective-permute-start(bf16[2,2,1,8,1024]{4,3,0,1,2:T(8,128)(2,1)S(1)} %pad_maximum_fusion.8), channel_id=1, source_target_pairs={{0,4},{1,5},{2,6},{3,7},{4,0},{5,1},{6,2},{7,3},{8,12},{9,13},{10,... | collective-permute-start | bytes 196616 | tf_op jit(solution)/shard_map/ppermute | solution.py:29
  211.0 12.4 %copy-start.2 = (pred[128,1024]{0,1:T(8,128)(4,1)S(1)}, pred[128,1024]{0,1:T(8,128)(4,1)}, u32[]{:S(2)}) copy-start(pred[128,1024]{0,1:T(8,128)(4,1)} %get-tuple-element.88) | copy-start | bytes 393220
  211.1 10.2 %collective-permute-start.9 = (bf16[2,2,2,1,8,1024]{5,4,0,1,2,3:T(8,128)(2,1)S(1)}, bf16[2,2,2,1,8,1024]{5,4,0,1,2,3:T(8,128)(2,1)S(1)}, u32[]{:S(2)}, u32[]{:S(2)}) collective-permute-start(bf16[2,2,2,1,8,1024]{5,4,0,1,2,3:T(8,128)(2,1)S(1)} %pad_maximum_fusion.6), channel_id=1, source_target_pairs={{0,2},{1,3},{2,0},{3,1},{4,6},{5,7},{6,4},{7,5},{8,10},{9,11},{10,... | collective-permute-start | bytes 393224 | tf_op jit(solution)/shard_map/ppermute | solution.py:29
  221.4 6.9 %collective-permute-start.10 = (bf16[2,2,2,2,1,8,1024]{6,5,0,1,2,3,4:T(8,128)(2,1)S(1)}, bf16[2,2,2,2,1,8,1024]{6,5,0,1,2,3,4:T(8,128)(2,1)S(1)}, u32[]{:S(2)}, u32[]{:S(2)}) collective-permute-start(bf16[2,2,2,2,1,8,1024]{6,5,0,1,2,3,4:T(8,128)(2,1)S(1)} %pad_maximum_fusion.5), channel_id=1, source_target_pairs={{0,1},{1,0},{2,3},{3,2},{4,5},{5,4},{6,7},{7,6},{8,9},{9,8},{10,11... | collective-permute-start | bytes 786440 | tf_op jit(solution)/shard_map/ppermute | solution.py:29
  232.2 12.1 %copy-start.54 = (f32[4,4,128]{2,1,0:T(4,128)}, f32[4,4,128]{2,1,0:T(4,128)S(1)}, u32[]{:S(2)}) copy-start(f32[4,4,128]{2,1,0:T(4,128)S(1)} %get-tuple-element.82) | copy-start | bytes 24580
  232.2 14.9 %copy-start.16 = (f32[4,4,128]{2,1,0:T(4,128)}, f32[4,4,128]{2,1,0:T(4,128)S(1)}, u32[]{:S(2)}) copy-start(f32[4,4,128]{2,1,0:T(4,128)S(1)} %get-tuple-element.16) | copy-start | bytes 24580
  232.2 14.8 %copy-start.18 = (f32[4,4,128]{2,1,0:T(4,128)}, f32[4,4,128]{2,1,0:T(4,128)S(1)}, u32[]{:S(2)}) copy-start(f32[4,4,128]{2,1,0:T(4,128)S(1)} %get-tuple-element.17) | copy-start | bytes 24580
  232.2 14.8 %copy-start.20 = (f32[4,4,128]{2,1,0:T(4,128)}, f32[4,4,128]{2,1,0:T(4,128)S(1)}, u32[]{:S(2)}) copy-start(f32[4,4,128]{2,1,0:T(4,128)S(1)} %get-tuple-element.18) | copy-start | bytes 24580
  232.2 14.8 %copy-start.22 = (f32[4,4,128]{2,1,0:T(4,128)}, f32[4,4,128]{2,1,0:T(4,128)S(1)}, u32[]{:S(2)}) copy-start(f32[4,4,128]{2,1,0:T(4,128)S(1)} %get-tuple-element.19) | copy-start | bytes 24580
  232.5 11.8 %slice-start.6 = ((s8[8388608]{0:T(1024)(128)(4,1)}), s8[4194304]{0:T(1024)(128)(4,1)S(1)}, s32[]{:S(2)}) async-start(s8[8388608]{0:T(1024)(128)(4,1)} %bitcast.614), calls=%async_computation.7 | async-start | bytes 8388608
  248.9 11.7 %slice-start.2 = ((s8[8388608]{0:T(1024)(128)(4,1)}), s8[4194304]{0:T(1024)(128)(4,1)S(1)}, s32[]{:S(2)}) async-start(s8[8388608]{0:T(1024)(128)(4,1)} %bitcast.610), calls=%async_computation.3 | async-start | bytes 8388608
  268.6 74.6 %copy-start.1 = (bf16[8,512]{1,0:T(8,128)(2,1)S(1)}, bf16[8,512]{1,0:T(8,128)(2,1)}, u32[]{:S(2)}) copy-start(bf16[8,512]{1,0:T(8,128)(2,1)} %param.14) | copy-start | bytes 24580
  270.4 67.1 %copy-start.9 = (bf16[128,4,4,128]{0,3,2,1:T(8,128)(2,1)S(1)}, bf16[128,4,4,128]{0,3,2,1:T(8,128)(2,1)}, u32[]{:S(2)}) copy-start(bf16[128,4,4,128]{0,3,2,1:T(8,128)(2,1)} %get-tuple-element.101) | copy-start | bytes 1572868
  270.4 71.9 %copy-start.25 = (f32[1,1,1024]{2,1,0:T(1,128)S(1)}, f32[1,1,1024]{2,1,0:T(1,128)}, u32[]{:S(2)}) copy-start(f32[1,1,1024]{2,1,0:T(1,128)} %copy-done.24) | copy-start | bytes 12292
  270.4 71.9 %copy-start.27 = (f32[1,1,1024]{2,1,0:T(1,128)S(1)}, f32[1,1,1024]{2,1,0:T(1,128)}, u32[]{:S(2)}) copy-start(f32[1,1,1024]{2,1,0:T(1,128)} %copy-done.26) | copy-start | bytes 12292
  270.4 71.9 %copy-start.29 = (f32[1,1,1024]{2,1,0:T(1,128)S(1)}, f32[1,1,1024]{2,1,0:T(1,128)}, u32[]{:S(2)}) copy-start(f32[1,1,1024]{2,1,0:T(1,128)} %copy-done.28) | copy-start | bytes 12292
  270.4 71.9 %copy-start.31 = (f32[1,1,1024]{2,1,0:T(1,128)S(1)}, f32[1,1,1024]{2,1,0:T(1,128)}, u32[]{:S(2)}) copy-start(f32[1,1,1024]{2,1,0:T(1,128)} %copy-done.30) | copy-start | bytes 12292
  270.4 71.9 %copy-start.33 = (f32[1,1,1024]{2,1,0:T(1,128)S(1)}, f32[1,1,1024]{2,1,0:T(1,128)}, u32[]{:S(2)}) copy-start(f32[1,1,1024]{2,1,0:T(1,128)} %copy-done.32) | copy-start | bytes 12292
  270.5 71.9 %copy-start.35 = (f32[1,1,1024]{2,1,0:T(1,128)S(1)}, f32[1,1,1024]{2,1,0:T(1,128)}, u32[]{:S(2)}) copy-start(f32[1,1,1024]{2,1,0:T(1,128)} %copy-done.34) | copy-start | bytes 12292
  270.5 71.9 %copy-start.37 = (f32[1,1,1024]{2,1,0:T(1,128)S(1)}, f32[1,1,1024]{2,1,0:T(1,128)}, u32[]{:S(2)}) copy-start(f32[1,1,1024]{2,1,0:T(1,128)} %copy-done.36) | copy-start | bytes 12292
  270.5 71.9 %copy-start.39 = (f32[1,1,1024]{2,1,0:T(1,128)S(1)}, f32[1,1,1024]{2,1,0:T(1,128)}, u32[]{:S(2)}) copy-start(f32[1,1,1024]{2,1,0:T(1,128)} %copy-done.38) | copy-start | bytes 12292
  270.5 71.9 %copy-start.41 = (f32[1,1,1024]{2,1,0:T(1,128)S(1)}, f32[1,1,1024]{2,1,0:T(1,128)}, u32[]{:S(2)}) copy-start(f32[1,1,1024]{2,1,0:T(1,128)} %copy-done.40) | copy-start | bytes 12292
  270.5 71.9 %copy-start.43 = (f32[1,1,1024]{2,1,0:T(1,128)S(1)}, f32[1,1,1024]{2,1,0:T(1,128)}, u32[]{:S(2)}) copy-start(f32[1,1,1024]{2,1,0:T(1,128)} %copy-done.42) | copy-start | bytes 12292
  270.5 71.9 %copy-start.45 = (f32[1,1,1024]{2,1,0:T(1,128)S(1)}, f32[1,1,1024]{2,1,0:T(1,128)}, u32[]{:S(2)}) copy-start(f32[1,1,1024]{2,1,0:T(1,128)} %copy-done.44) | copy-start | bytes 12292
  270.5 71.9 %copy-start.47 = (f32[1,1,1024]{2,1,0:T(1,128)S(1)}, f32[1,1,1024]{2,1,0:T(1,128)}, u32[]{:S(2)}) copy-start(f32[1,1,1024]{2,1,0:T(1,128)} %copy-done.46) | copy-start | bytes 12292
  270.5 71.9 %copy-start.49 = (f32[1,1,1024]{2,1,0:T(1,128)S(1)}, f32[1,1,1024]{2,1,0:T(1,128)}, u32[]{:S(2)}) copy-start(f32[1,1,1024]{2,1,0:T(1,128)} %copy-done.48) | copy-start | bytes 12292
  270.5 71.9 %copy-start.51 = (f32[1,1,1024]{2,1,0:T(1,128)S(1)}, f32[1,1,1024]{2,1,0:T(1,128)}, u32[]{:S(2)}) copy-start(f32[1,1,1024]{2,1,0:T(1,128)} %copy-done.50) | copy-start | bytes 12292
  270.5 71.9 %copy-start.53 = (f32[1,1,1024]{2,1,0:T(1,128)S(1)}, f32[1,1,1024]{2,1,0:T(1,128)}, u32[]{:S(2)}) copy-start(f32[1,1,1024]{2,1,0:T(1,128)} %copy-done.52) | copy-start | bytes 12292
  273.9 3.9 %collective-permute-start.11 = (f32[16,8,1024]{2,1,0:T(8,128)S(1)}, f32[16,8,1024]{2,1,0:T(8,128)S(1)}, u32[]{:S(2)}, u32[]{:S(2)}) collective-permute-start(f32[16,8,1024]{2,1,0:T(8,128)S(1)} %dynamic-slice_bitcast_fusion), channel_id=1, source_target_pairs={{0,1},{1,0},{2,3},{3,2},{4,5},{5,4},{6,7},{7,6},{8,9},{9,8},{10,11... | collective-permute-start | bytes 1572872 | tf_op jit(solution)/shard_map/ppermute | solution.py:56
  277.9 10.2 %collective-permute-start.14 = (f32[4,8,1024]{2,1,0:T(8,128)S(1)}, f32[4,8,1024]{2,1,0:T(8,128)S(1)}, u32[]{:S(2)}, u32[]{:S(2)}) collective-permute-start(f32[4,8,1024]{2,1,0:T(8,128)S(1)} %get-tuple-element.56), channel_id=1, source_target_pairs={{0,6},{1,7},{2,4},{3,5},{4,2},{5,3},{6,0},{7,1},{8,14},{9,15},{10,... | collective-permute-start | bytes 393224 | tf_op jit(solution)/shard_map/ppermute | solution.py:56
  280.8 12.8 %collective-permute-start.13 = (f32[4,8,1024]{2,1,0:T(8,128)S(1)}, f32[4,8,1024]{2,1,0:T(8,128)S(1)}, u32[]{:S(2)}, u32[]{:S(2)}) collective-permute-start(f32[4,8,1024]{2,1,0:T(8,128)S(1)} %get-tuple-element.57), channel_id=1, source_target_pairs={{0,4},{1,5},{2,6},{3,7},{4,0},{5,1},{6,2},{7,3},{8,12},{9,13},{10,... | collective-permute-start | bytes 393224 | tf_op jit(solution)/shard_map/ppermute | solution.py:56
  283.2 11.1 %collective-permute-start.12 = (f32[4,8,1024]{2,1,0:T(8,128)S(1)}, f32[4,8,1024]{2,1,0:T(8,128)S(1)}, u32[]{:S(2)}, u32[]{:S(2)}) collective-permute-start(f32[4,8,1024]{2,1,0:T(8,128)S(1)} %get-tuple-element.55), channel_id=1, source_target_pairs={{0,2},{1,3},{2,0},{3,1},{4,6},{5,7},{6,4},{7,5},{8,10},{9,11},{10,... | collective-permute-start | bytes 393224 | tf_op jit(solution)/shard_map/ppermute | solution.py:56
  294.4 14.7 %collective-permute-start.17 = (f32[1,8,1024]{2,1,0:T(8,128)S(1)}, f32[1,8,1024]{2,1,0:T(8,128)S(1)}, u32[]{:S(2)}, u32[]{:S(2)}) collective-permute-start(f32[1,8,1024]{2,1,0:T(8,128)S(1)} %get-tuple-element.72), channel_id=1, source_target_pairs={{0,24},{1,25},{2,26},{3,27},{4,28},{5,29},{6,30},{7,31},{8,16},{9,... | collective-permute-start | bytes 98312 | tf_op jit(solution)/shard_map/ppermute | solution.py:56
  301.3 7.7 %collective-permute-start.16 = (f32[1,8,1024]{2,1,0:T(8,128)S(1)}, f32[1,8,1024]{2,1,0:T(8,128)S(1)}, u32[]{:S(2)}, u32[]{:S(2)}) collective-permute-start(f32[1,8,1024]{2,1,0:T(8,128)S(1)} %get-tuple-element.73), channel_id=1, source_target_pairs={{0,16},{1,17},{2,18},{3,19},{4,20},{5,21},{6,22},{7,23},{8,24},{9,... | collective-permute-start | bytes 98312 | tf_op jit(solution)/shard_map/ppermute | solution.py:56
  304.1 9.7 %collective-permute-start.15 = (f32[1,8,1024]{2,1,0:T(8,128)S(1)}, f32[1,8,1024]{2,1,0:T(8,128)S(1)}, u32[]{:S(2)}, u32[]{:S(2)}) collective-permute-start(f32[1,8,1024]{2,1,0:T(8,128)S(1)} %get-tuple-element.71), channel_id=1, source_target_pairs={{0,8},{1,9},{2,10},{3,11},{4,12},{5,13},{6,14},{7,15},{8,0},{9,1},... | collective-permute-start | bytes 98312 | tf_op jit(solution)/shard_map/ppermute | solution.py:56
  313.8 12.2 %collective-permute-start.18 = (f32[1,8,1024]{2,1,0:T(8,128)S(1)}, f32[1,8,1024]{2,1,0:T(8,128)S(1)}, u32[]{:S(2)}, u32[]{:S(2)}) collective-permute-start(f32[1,8,1024]{2,1,0:T(8,128)S(1)} %add_add_fusion), channel_id=1, source_target_pairs={{0,384},{32,416},{64,448},{96,480},{128,256},{160,288},{192,320},{... | collective-permute-start | bytes 98312 | tf_op jit(solution)/shard_map/ppermute | solution.py:29
  317.0 9.7 %collective-permute-start.19 = (f32[1,8,1024]{2,1,0:T(8,128)S(1)}, f32[1,8,1024]{2,1,0:T(8,128)S(1)}, u32[]{:S(2)}, u32[]{:S(2)}) collective-permute-start(f32[1,8,1024]{2,1,0:T(8,128)S(1)} %add_add_fusion), channel_id=1, source_target_pairs={{0,256},{32,288},{64,320},{96,352},{128,384},{160,416},{192,448},{... | collective-permute-start | bytes 98312 | tf_op jit(solution)/shard_map/ppermute | solution.py:29
  321.5 6.7 %collective-permute-start.20 = (f32[1,8,1024]{2,1,0:T(8,128)S(1)}, f32[1,8,1024]{2,1,0:T(8,128)S(1)}, u32[]{:S(2)}, u32[]{:S(2)}) collective-permute-start(f32[1,8,1024]{2,1,0:T(8,128)S(1)} %add_add_fusion), channel_id=1, source_target_pairs={{0,128},{32,160},{64,192},{96,224},{128,0},{160,32},{192,64},{224,... | collective-permute-start | bytes 98312 | tf_op jit(solution)/shard_map/ppermute | solution.py:29
  328.2 10.3 %collective-permute-start.21 = (f32[2,2,1,8,1024]{4,3,1,0,2:T(8,128)S(1)}, f32[2,2,1,8,1024]{4,3,1,0,2:T(8,128)S(1)}, u32[]{:S(2)}, u32[]{:S(2)}) collective-permute-start(f32[2,2,1,8,1024]{4,3,1,0,2:T(8,128)S(1)} %bitcast.645), channel_id=1, source_target_pairs={{0,96},{32,64},{64,32},{96,0},{128,224},{160,192},{192,160},{224,1... | collective-permute-start | bytes 393224 | tf_op jit(solution)/shard_map/ppermute | solution.py:29
  332.8 6.9 %collective-permute-start.22 = (f32[2,2,1,8,1024]{4,3,1,0,2:T(8,128)S(1)}, f32[2,2,1,8,1024]{4,3,1,0,2:T(8,128)S(1)}, u32[]{:S(2)}, u32[]{:S(2)}) collective-permute-start(f32[2,2,1,8,1024]{4,3,1,0,2:T(8,128)S(1)} %bitcast.646), channel_id=1, source_target_pairs={{0,64},{32,96},{64,0},{96,32},{128,192},{160,224},{192,128},{224,1... | collective-permute-start | bytes 393224 | tf_op jit(solution)/shard_map/ppermute | solution.py:29
  335.3 6.9 %collective-permute-start.23 = (f32[2,2,1,8,1024]{4,3,1,0,2:T(8,128)S(1)}, f32[2,2,1,8,1024]{4,3,1,0,2:T(8,128)S(1)}, u32[]{:S(2)}, u32[]{:S(2)}) collective-permute-start(f32[2,2,1,8,1024]{4,3,1,0,2:T(8,128)S(1)} %bitcast.647), channel_id=1, source_target_pairs={{0,32},{32,0},{64,96},{96,64},{128,160},{160,128},{192,224},{224,1... | collective-permute-start | bytes 393224 | tf_op jit(solution)/shard_map/ppermute | solution.py:29
  (30 other events, 163.3 us)
Sparse Core Ops, SparseCore 0:
  11.7 117.0 all-gather.1
